TPU v7x, 32 devices: a whole 2x2x4 slice. The times are simulated.
32 devices in a mesh: segment: 2 (over core), expert: 16 (over z, y, x).
Axes of the slice: x: 2, y: 2, z: 4, core: 2. Of those that a mesh axis runs over, the one named last changes fastest.
Arguments:
- hidden_in: bfloat16 [2, 256, 7168], P('segment', 'expert'), may hold values from -6 to 6
- norm_gain: bfloat16 [2, 7168], P('segment'), may hold values from 0.25 to 1.75
- up_proj: bfloat16 [2, 8192, 7168], P('segment', 'expert'), may hold values from -0.0625 to 0.0625
- down_proj: bfloat16 [2, 8192, 7168], P('segment', 'expert'), may hold values from -0.1875 to 0.1875
- expert_ids: int32 [2, 256, 2], P('segment', 'expert'), may hold values from 0 to 7, all different within a row; in each aligned block of 16 rows (0 to 15, 16 to 31, ..., all dimensions but the last counted through in order) at most 7 rows name the same one
- gate_weights: float32 [2, 256, 2], P('segment', 'expert'), may hold values from 0.2 to 1
Outputs:
- handed_on: bfloat16 [2, 256, 7168], P('segment', 'expert')
Inputs may be any that keep to these rules, and one draw needn't show every extreme that they name: `expert_ids`: each row names 2 different experts. Among the rows of one device in one section no expert is named by more than 7 rows, and in some device an expert is named by exactly 7.
All inputs are finite; a program needn't handle non-finite values.
Results may differ from a plain program's by a relative error of at most 0.0075.
Values may be sent and summed in bfloat16 or wider, within the bound.
No kernel may reach another device: no remote copies, remote signals or barrier semaphores. Data moves between devices by JAX's collectives and lax.ppermute only.
A program may use at most 64 MiB of HBM per device.

v0:
```python
import jax
import jax.numpy as jnp
from jax import lax
from jax.sharding import PartitionSpec as P

EXPERTS = 8
TOP = 2
CAP = 7


def passed_along(shard, axis, by):
    count = lax.axis_size(axis)
    return lax.ppermute(shard, axis, [(i, (i + by) % count) for i in range(count)])


def expert_block(rows, up_block, down_block):
    senders, places, width = rows.shape
    flat = rows.reshape(senders * places, width)
    inner = jnp.einsum("rd,fd->rf", flat, up_block, preferred_element_type=jnp.float32)
    active = jax.nn.silu(inner).astype(jnp.bfloat16)
    result = jnp.dot(active, down_block, preferred_element_type=jnp.float32).astype(jnp.bfloat16)
    return result.reshape(senders, places, width)


def shards(hidden_in, norm_gain, up_proj, down_proj, expert_ids, gate_weights):
    members = lax.axis_size("expert")
    per_group = members // EXPERTS
    tokens = hidden_in[0]
    gain = norm_gain[0]
    up_block = up_proj[0]
    down_block = down_proj[0]
    routes = expert_ids[0].reshape(-1)
    weights = gate_weights[0].reshape(-1)
    assigned = routes.shape[0]
    rows_here, width = tokens.shape
    square = jnp.mean(tokens.astype(jnp.float32) ** 2, axis=-1, keepdims=True)
    normed = (
        tokens.astype(jnp.float32) * lax.rsqrt(square + 1e-06) * gain.astype(jnp.float32)
    ).astype(jnp.bfloat16)
    onehot = (routes[:, None] == jnp.arange(EXPERTS)[None, :]).astype(jnp.int32)
    positions = jnp.arange(assigned)
    earlier = (positions[None, :] < positions[:, None]).astype(jnp.int32)
    before = jnp.dot(earlier, onehot, preferred_element_type=jnp.int32)
    rank = jnp.sum(before * onehot, axis=1)
    destination = routes * CAP + rank
    picker = (jnp.arange(EXPERTS * CAP)[:, None] == destination[None, :]).astype(jnp.bfloat16)
    repeated = jnp.repeat(normed, TOP, axis=0)
    grouped = jnp.dot(picker, repeated, preferred_element_type=jnp.float32).astype(jnp.bfloat16)
    grouped = grouped.reshape(EXPERTS, CAP, width)
    outgoing = jnp.repeat(grouped, per_group, axis=0)
    incoming = lax.all_to_all(outgoing, "expert", split_axis=0, concat_axis=0, tiled=True)
    partial_value = expert_block(incoming, up_block, down_block)
    returned = lax.all_to_all(partial_value, "expert", split_axis=0, concat_axis=0, tiled=True)
    summed = jnp.sum(returned.astype(jnp.float32).reshape(EXPERTS, per_group, CAP, width), axis=1)
    summed = summed.reshape(EXPERTS * CAP, width)
    collected = jnp.dot(picker.T.astype(jnp.float32), summed, precision=lax.Precision.HIGHEST)
    mixture = jnp.sum((collected * weights[:, None]).reshape(rows_here, TOP, width), axis=1)
    section_out = (tokens.astype(jnp.float32) + mixture).astype(jnp.bfloat16)
    handed = passed_along(section_out, "segment", 1)
    return handed[None]


def solution(mesh):
    in_specs = (
        P("segment", "expert", None),
        P("segment", None),
        P("segment", "expert", None),
        P("segment", "expert", None),
        P("segment", "expert", None),
        P("segment", "expert", None),
    )
    out_specs = P("segment", "expert", None)
    return jax.shard_map(shards, mesh=mesh, in_specs=in_specs, out_specs=out_specs, check_vma=False)
```

profile of v0, /device:TPU:13, one launch (start us, length us, event | category | flops | bytes accessed | tf_op | source)
XLA Modules:
  0.0 121.2 jit_solution(3593394450481062362)
XLA Ops:
  0.0 0.8 copy.9
  0.8 0.1 reshape_squeeze.3
  0.8 0.1 fusion.3
  1.0 0.8 mul.61
  1.8 1.1 fusion.4
  2.9 1.1 fusion.6
  4.0 0.2 broadcast_in_dim.6
  4.2 0.2 reshape.47
  4.4 0.4 convolution_convert_fusion.1
  4.8 0.3 reshape.48
  5.1 0.2 broadcast_in_dim.7
  5.3 47.9 %all_to_all.10 = bf16[16,7,7168]{2,1,0:T(8,128)(2,1)S(1)} all-to-all(bf16[16,7,7168]{2,1,0:T(8,128)(2,1)S(1)} %bitcast.24), channel_id=1, replica_groups=mesh['segment'=2,'expert'=16] {'expert'}, dimensions={0} | all-to-all | bytes 3211264 | tf_op jit(solution)/shard_map/all_to_all | solution.py:51
  53.2 0.6 reshape.50
  53.8 8.8 %convolution_convert_fusion = bf16[112,7168]{1,0:T(8,128)(2,1)S(1)} fusion(bf16[1,512,7168]{2,1,0:T(8,128)(2,1)} %param.9, bf16[112,7168]{1,0:T(8,128)(2,1)S(1)} %reshape.50, bf16[1,512,7168]{2,1,0:T(8,128)(2,1)} %param.8), kind=kOutput, calls=%fused_computation | convolution fusion | flops 1645256704 | bytes 17891328 | tf_op jit(solution)/shard_map/dot_general | solution.py:21
  62.7 1.6 %reshape.51 = bf16[16,7,7168]{2,1,0:T(8,128)(2,1)} reshape(bf16[112,7168]{1,0:T(8,128)(2,1)S(1)} %convolution_convert_fusion) | data formatting | bytes 3211264 | tf_op jit(solution)/shard_map/reshape | solution.py:22
  64.3 0.0 copy-start.1
  64.3 5.2 %all-to-all-start.1 = ((bf16[16,7,7168]{2,1,0:T(8,128)(2,1)}), bf16[16,7,7168]{2,1,0:T(8,128)(2,1)S(1)}, u32[]{:S(2)}, u32[]{:S(2)}) async-start(bf16[16,7,7168]{2,1,0:T(8,128)(2,1)} %reshape.51), calls=%async_computation.1 | async-start | bytes 3670016 | tf_op jit(solution)/shard_map/all_to_all | solution.py:53
  69.4 0.0 copy-done.1
  69.5 0.1 copy.10
  69.5 0.1 mul.58
  69.6 42.5 %all-to-all-done.1 = bf16[16,7,7168]{2,1,0:T(8,128)(2,1)S(1)} async-done(((bf16[16,7,7168]{2,1,0:T(8,128)(2,1)}), bf16[16,7,7168]{2,1,0:T(8,128)(2,1)S(1)}, u32[]{:S(2)}, u32[]{:S(2)}) %all-to-all-start.1) | async-done | bytes 1605664 | tf_op jit(solution)/shard_map/all_to_all | solution.py:53
  112.1 1.6 %convert_reduce_fusion = f32[8,7,7168]{2,1,0:T(8,128)} fusion(bf16[16,7,7168]{2,1,0:T(8,128)(2,1)S(1)} %all-to-all-done.1), kind=kLoop, calls=%fused_computation.6 | loop fusion | flops 1204224 | bytes 3211264 | tf_op jit(solution)/shard_map/reduce_sum | solution.py:54
  113.7 1.7 %reshape.54 = f32[56,7168]{1,0:T(8,128)S(1)} reshape(f32[8,7,7168]{2,1,0:T(8,128)} %convert_reduce_fusion) | data formatting | bytes 3211264 | tf_op jit(solution)/shard_map/reshape | solution.py:55
  115.5 0.7 convolution_multiply_fusion
  116.2 0.0 copy-start
  116.2 0.5 reshape.55
  116.7 1.1 reduce_sum.39
  117.8 0.0 copy-done
  117.9 1.5 %collective-permute-start = (bf16[16,7168]{1,0:T(8,128)(2,1)S(1)}, bf16[16,7168]{1,0:T(8,128)(2,1)S(1)}, u32[]{:S(2)}, u32[]{:S(2)}) collective-permute-start(bf16[16,7168]{1,0:T(8,128)(2,1)S(1)} %fusion.7), channel_id=1, source_target_pairs={{0,16},{16,0},{1,17},{17,1},{2,18},{18,2},{3,19},{19,3},{4,20},{20... | collective-permute-start | bytes 688136 | tf_op jit(solution)/shard_map/ppermute | solution.py:13
  119.4 1.1 collective-permute-done
  120.5 0.7 copy.12
  (3 shorter events, 0.1 us)
Async XLA Ops:
  64.3 5.2 %copy-start.1 = (f32[1,16,2]{1,2,0:T(2,128)S(1)}, f32[1,16,2]{1,2,0:T(2,128)}, u32[]{:S(2)}) copy-start(f32[1,16,2]{1,2,0:T(2,128)} %param.11) | copy-start | bytes 388
  64.3 47.8 %all-to-all-start.1 = ((bf16[16,7,7168]{2,1,0:T(8,128)(2,1)}), bf16[16,7,7168]{2,1,0:T(8,128)(2,1)S(1)}, u32[]{:S(2)}, u32[]{:S(2)}) async-start(bf16[16,7,7168]{2,1,0:T(8,128)(2,1)} %reshape.51), calls=%async_computation.1 | async-start | bytes 3670016 | tf_op jit(solution)/shard_map/all_to_all | solution.py:53
  116.2 1.7 %copy-start = (bf16[1,16,7168]{2,1,0:T(8,128)(2,1)S(1)}, bf16[1,16,7168]{2,1,0:T(8,128)(2,1)}, u32[]{:S(2)}) copy-start(bf16[1,16,7168]{2,1,0:T(8,128)(2,1)} %param.6) | copy-start | bytes 688132
  117.9 2.6 %collective-permute-start = (bf16[16,7168]{1,0:T(8,128)(2,1)S(1)}, bf16[16,7168]{1,0:T(8,128)(2,1)S(1)}, u32[]{:S(2)}, u32[]{:S(2)}) collective-permute-start(bf16[16,7168]{1,0:T(8,128)(2,1)S(1)} %fusion.7), channel_id=1, source_target_pairs={{0,16},{16,0},{1,17},{17,1},{2,18},{18,2},{3,19},{19,3},{4,20},{20... | collective-permute-start | bytes 688136 | tf_op jit(solution)/shard_map/ppermute | solution.py:13
where the time goes:
time: 122 us; the launch traced here: 121 us
  blocking collectives  47.9 us (39%)
  waiting for transfers between devices  43.6 us (36%)
  matrix products  10 us (8%)
  local copies, waits for them, and re-layouts  7.11 us (6%)
  starting transfers between devices  6.71 us (6%)
  other arithmetic  5.74 us (5%)
    all_to_all x1, blocking collectives, shards(): lax.all_to_all(outgoing, 'expert', split_axis=0, concat_axis=0, tiled=True)  47.9 us
    all_to_all x1, waiting for transfers between devices, shards(): lax.all_to_all(partial_value, 'expert', split_axis=0, concat_axis=0, tile...  42.5 us
    dot_general x1, matrix products, expert_block(): jnp.dot(active, down_block, preferred_element_type=jnp.float32)  8.84 us
    all_to_all x1, starting transfers between devices, shards(): lax.all_to_all(partial_value, 'expert', split_axis=0, concat_axis=0, tile...  5.18 us
  transfers between devices with their start and end apart: 2, of which 2 were waited for; matrix products, arithmetic and copies ran while one was open for 0% of the time, Pallas kernels for 0%

commit v1 on v0

v1 whole, which is shorter than its diff:
```python
import jax
import jax.numpy as jnp
from jax import lax
from jax.sharding import PartitionSpec as P

EXPERTS = 8


def passed_along(shard, axis, by):
    count = lax.axis_size(axis)
    return lax.ppermute(shard, axis, [(i, (i + by) % count) for i in range(count)])


def shards(hidden_in, norm_gain, up_proj, down_proj, expert_ids, gate_weights):
    members = lax.axis_size("expert")
    me = lax.axis_index("expert")
    tokens = hidden_in[0]
    gain = norm_gain[0]
    up_block = up_proj[0]
    down_block = down_proj[0]
    local_units = up_block.shape[0]
    units_per_expert = local_units * members // EXPERTS
    my_expert = (me * local_units) // units_per_expert
    square = jnp.mean(tokens.astype(jnp.float32) ** 2, axis=-1, keepdims=True)
    normed = (
        tokens.astype(jnp.float32) * lax.rsqrt(square + 1e-06) * gain.astype(jnp.float32)
    ).astype(jnp.bfloat16)
    all_rows = lax.all_gather(normed, "expert", axis=0, tiled=True)
    all_ids = lax.all_gather(expert_ids[0], "expert", axis=0, tiled=True)
    all_gates = lax.all_gather(gate_weights[0], "expert", axis=0, tiled=True)
    scale = jnp.sum(jnp.where(all_ids == my_expert, all_gates, 0.0), axis=-1, keepdims=True)
    inner = jnp.einsum("rd,fd->rf", all_rows, up_block, preferred_element_type=jnp.float32)
    active = jax.nn.silu(inner).astype(jnp.bfloat16)
    partial = jnp.dot(active, down_block, preferred_element_type=jnp.float32).astype(jnp.bfloat16)
    contribution = partial.astype(jnp.float32) * scale
    mixture = lax.psum_scatter(contribution, "expert", scatter_dimension=0, tiled=True)
    section_out = (tokens.astype(jnp.float32) + mixture).astype(jnp.bfloat16)
    handed = passed_along(section_out, "segment", 1)
    return handed[None]


def solution(mesh):
    in_specs = (
        P("segment", "expert", None),
        P("segment", None),
        P("segment", "expert", None),
        P("segment", "expert", None),
        P("segment", "expert", None),
        P("segment", "expert", None),
    )
    out_specs = P("segment", "expert", None)
    return jax.shard_map(shards, mesh=mesh, in_specs=in_specs, out_specs=out_specs, check_vma=False)
```

time: 122 us -> 273 us (2.24)
  waiting for transfers between devices: 43.6 us -> 179 us
  between operations: 0.13 us -> 13.4 us
  blocking collectives: 47.9 us -> 55.6 us
  starting transfers between devices: 6.71 us -> 1.02 us
  local copies, waits for them, and re-layouts: 7.11 us -> 2.2 us
  matrix products: 10 us -> 13.3 us
    reduce_scatter x0 -> x1, waiting for transfers between devices: none -> 163 us  [shards(): lax.psum_scatter(contribution, 'expert', scatter_dimension=0, tiled=True)]
    all_gather x0 -> x2, blocking collectives: none -> 55.6 us  [the longest x1 30.1 us: shards(): all_ids = lax.all_gather(expert_ids[0], 'expert', axis=0, tiled=True)]
    all_to_all x1 -> x0, blocking collectives: 47.9 us -> none  [shards(): lax.all_to_all(outgoing, 'expert', split_axis=0, concat_axis=0, tiled=True)]
    all_to_all x1 -> x0, waiting for transfers between devices: 42.5 us -> none  [shards(): lax.all_to_all(partial_value, 'expert', split_axis=0, concat_axis=0, tile...]
    all_gather x0 -> x1, waiting for transfers between devices: none -> 15.6 us  [shards(): all_rows = lax.all_gather(normed, 'expert', axis=0, tiled=True)]
    all_to_all x1 -> x0, starting transfers between devices: 5.18 us -> none  [shards(): lax.all_to_all(partial_value, 'expert', split_axis=0, concat_axis=0, tile...]
    reshape x6 -> x0, local copies, waits for them, and re-layouts: 4.99 us -> none  [the longest x1 1.73 us: shards(): summed = summed.reshape(EXPERTS * CAP, width)]
    dot_general x4 -> x1, matrix products: 10 us -> 13.3 us  [shards(): jnp.dot(active, down_block, preferred_element_type=jnp.float32)]
  transfers between devices with their start and end apart: 2 -> 3, of which waited for: 2 -> 3; matrix products, arithmetic and copies ran while one was open for 0% -> 1% of each run, Pallas kernels for 0% -> 0%
where the time goes in v1:
time: 273 us; the launch traced here: 271 us
  waiting for transfers between devices  179 us (66%)
  blocking collectives  55.6 us (20%)
  between operations  13.4 us (5%)
  matrix products  13.3 us (5%)
  other arithmetic  5.74 us (2%)
    reduce_scatter x1, waiting for transfers between devices, shards(): lax.psum_scatter(contribution, 'expert', scatter_dimension=0, tiled=True)  163 us
    all_gather x1, blocking collectives, shards(): all_ids = lax.all_gather(expert_ids[0], 'expert', axis=0, tiled=True)  30.1 us
    all_gather x1, blocking collectives, shards(): all_gates = lax.all_gather(gate_weights[0], 'expert', axis=0, tiled=True)  25.5 us
    all_gather x1, waiting for transfers between devices, shards(): all_rows = lax.all_gather(normed, 'expert', axis=0, tiled=True)  15.6 us
    dot_general x1, matrix products, shards(): jnp.dot(active, down_block, preferred_element_type=jnp.float32)  13.3 us
  transfers between devices with their start and end apart: 3, of which 3 were waited for; matrix products, arithmetic and copies ran while one was open for 1% of the time, Pallas kernels for 0%

profile of v1, /device:TPU:13, one launch (start us, length us, event | category | flops | bytes accessed | tf_op | source)
XLA Modules:
  0.0 270.7 jit_solution(9835408425453076009)
XLA Ops:
  6.5 0.0 all-gather.4.cloned.1.call-start
  6.5 1.1 fusion.9
  7.7 0.8 mul.46
  8.4 1.8 fusion.11
  10.2 0.0 all-gather.4.cloned.1.call-update
  10.2 0.0 reduce-scatter.2.cloned.1.call-start
  10.3 0.8 copy.7
  11.0 0.8 copy.8
  11.8 25.5 %all-gather.1 = f32[1,256,2]{2,0,1:T(1,128)S(1)} all-gather(f32[1,16,2]{2,0,1:T(1,128)S(1)} %copy.8), channel_id=3, replica_groups=mesh['segment'=2,'expert'=16] {'expert'}, dimensions={1}, use_global_device_ids=true | all-gather | bytes 2176 | tf_op jit(solution)/shard_map/all_gather | solution.py:30
  37.3 30.1 %all-gather = s32[1,256,2]{2,0,1:T(1,128)S(1)} all-gather(s32[1,16,2]{2,0,1:T(1,128)S(1)} %copy.7), channel_id=2, replica_groups=mesh['segment'=2,'expert'=16] {'expert'}, dimensions={1}, use_global_device_ids=true | all-gather | bytes 2176 | tf_op jit(solution)/shard_map/all_gather | solution.py:29
  67.4 1.0 fusion.14
  68.4 15.6 %all-gather.4.cloned.1.call-done = bf16[256,7168]{1,0:T(8,128)(2,1)} async-done(((bf16[16,7168]{1,0:T(8,128)(2,1)}), bf16[256,7168]{1,0:T(8,128)(2,1)}) %all-gather.4.cloned.1.call-update) | async-done | bytes 3670032 | tf_op jit(solution)/shard_map/all_gather | solution.py:28
  84.0 13.3 %fusion.1 = f32[256,7168]{1,0:T(8,128)} fusion(bf16[1,512,7168]{2,1,0:T(8,128)(2,1)} %param.9, f32[256]{0:T(256)S(1)} %fusion.14, bf16[256,7168]{1,0:T(8,128)(2,1)} %all-gather.4.cloned.1.call-done, bf16[1,512,7168]{2,1,0:T(8,128)(2,1)} %param.8), kind=kOutput, calls=%fused_computation.2 | convolution fusion | flops 3764256768 | bytes 25691136 | tf_op jit(solution)/shard_map/dot_general | solution.py:34
  97.4 0.0 copy-start
  97.4 0.0 reduce-scatter.2.cloned.1.call-update
  97.4 162.6 %reduce-scatter.2.cloned.1.call-done = f32[16,7168]{1,0:T(8,128)} async-done(((f32[256,7168]{1,0:T(8,128)}), f32[16,7168]{1,0:T(8,128)}) %reduce-scatter.2.cloned.1.call-update) | async-done | bytes 458768 | tf_op jit(solution)/shard_map/reduce_scatter | solution.py:36
  260.0 0.0 copy-done
  260.0 1.1 fusion.12
  261.1 1.0 collective-permute-start
  262.1 1.1 collective-permute-done
  263.2 0.7 copy.10
  (1 shorter events, 0.0 us)
Async XLA Ops:
  6.5 77.5 %all-gather.4.cloned.1.call-start = ((), (), s32[]{:S(2)}) async-start(), calls=%async_computation.1 | async-start | bytes 3899392 | tf_op jit(solution)/shard_map/all_gather | solution.py:28
  10.2 249.8 %reduce-scatter.2.cloned.1.call-start = ((), (), s32[]{:S(2)}) async-start(), calls=%async_computation.2 | async-start | bytes 7798784 | tf_op jit(solution)/shard_map/reduce_scatter | solution.py:36
  97.4 162.7 %copy-start = (bf16[1,16,7168]{2,1,0:T(8,128)(2,1)S(1)}, bf16[1,16,7168]{2,1,0:T(8,128)(2,1)}, u32[]{:S(2)}) copy-start(bf16[1,16,7168]{2,1,0:T(8,128)(2,1)} %param.6) | copy-start | bytes 688132
  261.1 2.1 collective-permute-start
Sparse Core Ops, SparseCore 0:
  10.3 73.6 all-gather.3
  97.5 162.4 reduce-scatter.1

commit v2 on v1

v2 whole, which is shorter than its diff:
```python
import jax
import jax.numpy as jnp
from jax import lax
from jax.sharding import PartitionSpec as P

EXPERTS = 8
CAP = 7


def passed_along(shard, axis, by):
    count = lax.axis_size(axis)
    return lax.ppermute(shard, axis, [(i, (i + by) % count) for i in range(count)])


def shards(hidden_in, norm_gain, up_proj, down_proj, expert_ids, gate_weights):
    members = lax.axis_size("expert")
    per_group = members // EXPERTS
    tokens = hidden_in[0]
    gain = norm_gain[0]
    up_block = up_proj[0]
    down_block = down_proj[0]
    routes = expert_ids[0]
    weights = gate_weights[0]
    rows_here, width = tokens.shape
    top = routes.shape[1]
    square = jnp.mean(tokens.astype(jnp.float32) ** 2, axis=-1, keepdims=True)
    normed = (
        tokens.astype(jnp.float32) * lax.rsqrt(square + 1e-06) * gain.astype(jnp.float32)
    ).astype(jnp.bfloat16)
    flat = routes.reshape(-1)
    onehot = (flat[:, None] == jnp.arange(EXPERTS)[None, :]).astype(jnp.int32)
    positions = jnp.arange(flat.shape[0])
    earlier = (positions[None, :] < positions[:, None]).astype(jnp.int32)
    rank = jnp.sum(jnp.dot(earlier, onehot, preferred_element_type=jnp.int32) * onehot, axis=1)
    rank = rank.reshape(rows_here, top)
    slot = jnp.arange(members * CAP)
    slot_device = slot // CAP
    slot_rank = slot % CAP
    slot_expert = slot_device // per_group
    hits = (routes[None, :, :] == slot_expert[:, None, None]) & (rank[None, :, :] == slot_rank[:, None, None])
    picker = jnp.any(hits, axis=2).astype(jnp.bfloat16)
    outgoing = jnp.dot(picker, normed, preferred_element_type=jnp.float32).astype(jnp.bfloat16)
    outgoing = outgoing.reshape(members, CAP, width)
    incoming = lax.all_to_all(outgoing, "expert", split_axis=0, concat_axis=0, tiled=True)
    inner = jnp.einsum("spd,fd->spf", incoming, up_block, preferred_element_type=jnp.float32)
    active = jax.nn.silu(inner).astype(jnp.bfloat16)
    partial = jnp.einsum("spf,fd->spd", active, down_block, preferred_element_type=jnp.float32).astype(jnp.bfloat16)
    returned = lax.all_to_all(partial, "expert", split_axis=0, concat_axis=0, tiled=True)
    combine = jnp.sum(jnp.where(hits, weights[None, :, :], 0.0), axis=2).T.reshape(rows_here, members, CAP)
    mixture = jnp.einsum("rsp,spd->rd", combine, returned.astype(jnp.float32), precision=lax.Precision.HIGHEST)
    section_out = (tokens.astype(jnp.float32) + mixture).astype(jnp.bfloat16)
    handed = passed_along(section_out, "segment", 1)
    return handed[None]


def solution(mesh):
    in_specs = (
        P("segment", "expert", None),
        P("segment", None),
        P("segment", "expert", None),
        P("segment", "expert", None),
        P("segment", "expert", None),
        P("segment", "expert", None),
    )
    out_specs = P("segment", "expert", None)
    return jax.shard_map(shards, mesh=mesh, in_specs=in_specs, out_specs=out_specs, check_vma=False)
```

time: 273 us -> 117 us (0.43)
  waiting for transfers between devices: 179 us -> 43.4 us
  between operations: 13.4 us -> 0.12 us
  blocking collectives: 55.6 us -> 48.2 us
  starting transfers between devices: 1.02 us -> 6.71 us
  other arithmetic: 5.74 us -> 2.77 us
    reduce_scatter x1 -> x0, waiting for transfers between devices: 163 us -> none  [shards(): lax.psum_scatter(contribution, 'expert', scatter_dimension=0, tiled=True)]
    all_gather x2 -> x0, blocking collectives: 55.6 us -> none  [the longest x1 30.1 us: shards(): all_ids = lax.all_gather(expert_ids[0], 'expert', axis=0, tiled=True)]
    all_to_all x0 -> x1, blocking collectives: none -> 48.2 us  [shards(): lax.all_to_all(outgoing, 'expert', split_axis=0, concat_axis=0, tiled=True)]
    all_to_all x0 -> x1, waiting for transfers between devices: none -> 42.3 us  [shards(): lax.all_to_all(partial, 'expert', split_axis=0, concat_axis=0, tiled=True)]
    all_gather x1 -> x0, waiting for transfers between devices: 15.6 us -> none  [shards(): all_rows = lax.all_gather(normed, 'expert', axis=0, tiled=True)]
    all_to_all x0 -> x1, starting transfers between devices: none -> 5.18 us  [shards(): lax.all_to_all(partial, 'expert', split_axis=0, concat_axis=0, tiled=True)]
    convert_element_type x2 -> x0, other arithmetic: 2.81 us -> none  [the longest x1 1.75 us: shards(): normed = (tokens.astype(jnp.float32) * lax.rsqrt(square + 1e-06) * gain.a...]
    dot_general x1 -> x5, matrix products: 13.3 us -> 11.2 us  [the longest x1 6.05 us: shards(): jnp.einsum('spd,fd->spf', incoming, up_block, preferred_element_type=jnp....]
  transfers between devices with their start and end apart: 3 -> 2, of which waited for: 3 -> 2; matrix products, arithmetic and copies ran while one was open for 1% -> 0% of each run, Pallas kernels for 0% -> 0%
where the time goes in v2:
time: 117 us
  blocking collectives  48.2 us (41%)
  waiting for transfers between devices  43.4 us (37%)
  matrix products  11.2 us (10%)
  starting transfers between devices  6.71 us (6%)
  local copies, waits for them, and re-layouts  4.79 us (4%)
  other arithmetic  2.77 us (2%)
    all_to_all x1, blocking collectives, shards(): lax.all_to_all(outgoing, 'expert', split_axis=0, concat_axis=0, tiled=True)  48.2 us
    all_to_all x1, waiting for transfers between devices, shards(): lax.all_to_all(partial, 'expert', split_axis=0, concat_axis=0, tiled=True)  42.3 us
    dot_general x1, matrix products, shards(): jnp.einsum('spd,fd->spf', incoming, up_block, preferred_element_type=jnp....  6.05 us
    all_to_all x1, starting transfers between devices, shards(): lax.all_to_all(partial, 'expert', split_axis=0, concat_axis=0, tiled=True)  5.18 us
  transfers between devices with their start and end apart: 2, of which 2 were waited for; matrix products, arithmetic and copies ran while one was open for 0% of the time, Pallas kernels for 0%

profile of v2, /device:TPU:13, one launch (start us, length us, event | category | flops | bytes accessed | tf_op | source)
XLA Modules:
  0.0 117.1 jit_solution(13990461318134234292)
XLA Ops:
  0.0 0.8 copy.23
  0.8 0.1 eq.51
  0.9 0.1 fusion.7
  1.0 0.1 eq.55
  1.1 0.1 copy.24
  1.2 0.8 mul.36
  2.0 1.1 fusion.8
  3.1 0.8 fusion.19
  3.9 1.6 %convolution_convert_fusion.1 = bf16[112,7168]{1,0:T(8,128)(2,1)S(1)} fusion(pred[112,16]{0,1:T(8,128)(4,1)S(1)} %fusion.19, bf16[1,16,7168]{2,1,0:T(8,128)(2,1)} %param.6, f32[7168]{0:T(1024)S(1)} %bitcast.35, f32[16]{0:T(128)S(1)} %add_rsqrt_fusion), kind=kOutput, calls=%fused_computation.1 | convolution fusion | flops 26951680 | bytes 1865536 | tf_op jit(solution)/shard_map/dot_general | solution.py:42
  5.4 0.6 reshape.53
  6.1 0.0 slice-start
  6.1 48.2 %all_to_all.10 = bf16[16,7,7168]{2,1,0:T(8,128)(2,1)S(1)} all-to-all(bf16[16,7,7168]{2,1,0:T(8,128)(2,1)S(1)} %reshape.53), channel_id=1, replica_groups=mesh['segment'=2,'expert'=16] {'expert'}, dimensions={0} | all-to-all | bytes 3211264 | tf_op jit(solution)/shard_map/all_to_all | solution.py:44
  54.3 0.0 slice-start.1
  54.3 6.0 %multiply_convert_fusion = bf16[16,7,512]{2,0,1:T(8,128)(2,1)S(1)} fusion(bf16[1,512,7168]{2,1,0:T(8,128)(2,1)} %param.8, bf16[16,7,7168]{2,1,0:T(8,128)(2,1)S(1)} %all_to_all.10), kind=kOutput, calls=%fused_computation.18 | convolution fusion | flops 822370304 | bytes 9060352 | tf_op jit(solution)/shard_map/spd,fd->spf/dot_general | solution.py:45
  60.3 0.0 slice-done
  60.3 0.0 slice-done.1
  60.4 1.2 convolution_convert_fusion
  61.5 2.1 %copy.27 = bf16[16,7,7168]{2,1,0:T(8,128)(2,1)} copy(bf16[16,7,7168]{2,0,1:T(8,128)(2,1)S(1)} %convolution_convert_fusion) | data formatting | bytes 3211264 | tf_op jit(solution)/shard_map/convert_element_type | solution.py:47
  63.7 0.0 copy-start.1
  63.7 0.0 copy-start.2
  63.7 5.2 %all-to-all-start.1 = ((bf16[16,7,7168]{2,1,0:T(8,128)(2,1)}), bf16[16,7,7168]{2,1,0:T(8,128)(2,1)S(1)}, u32[]{:S(2)}, u32[]{:S(2)}) async-start(bf16[16,7,7168]{2,1,0:T(8,128)(2,1)} %copy.27), calls=%async_computation.1 | async-start | bytes 3670016 | tf_op jit(solution)/shard_map/all_to_all | solution.py:48
  68.9 0.0 copy-done.1
  68.9 0.0 copy-done.2
  68.9 0.1 select_reduce_fusion
  69.0 0.1 reshape.59
  69.1 0.2 copy.28
  69.2 42.3 %all-to-all-done.1 = bf16[16,7,7168]{2,1,0:T(8,128)(2,1)S(1)} async-done(((bf16[16,7,7168]{2,1,0:T(8,128)(2,1)}), bf16[16,7,7168]{2,1,0:T(8,128)(2,1)S(1)}, u32[]{:S(2)}, u32[]{:S(2)}) %all-to-all-start.1) | async-done | bytes 1605664 | tf_op jit(solution)/shard_map/all_to_all | solution.py:48
  111.5 0.0 copy-done
  111.5 2.3 %fusion.1 = bf16[16,7168]{1,0:T(8,128)(2,1)S(1)} fusion(f32[16,16,7]{1,0,2:T(8,128)S(1)} %copy.28, bf16[16,7,7168]{2,1,0:T(8,128)(2,1)S(1)} %all-to-all-done.1, bf16[1,16,7168]{2,1,0:T(8,128)(2,1)S(1)} %copy-done), kind=kOutput, calls=%fused_computation.4 | convolution fusion | flops 154484736 | bytes 2071552 | tf_op jit(solution)/shard_map/rsp,spd->rd/dot_general | solution.py:50
  113.8 1.5 %collective-permute-start = (bf16[16,7168]{1,0:T(8,128)(2,1)S(1)}, bf16[16,7168]{1,0:T(8,128)(2,1)S(1)}, u32[]{:S(2)}, u32[]{:S(2)}) collective-permute-start(bf16[16,7168]{1,0:T(8,128)(2,1)S(1)} %fusion.1), channel_id=1, source_target_pairs={{0,16},{16,0},{1,17},{17,1},{2,18},{18,2},{3,19},{19,3},{4,20},{20... | collective-permute-start | bytes 688136 | tf_op jit(solution)/shard_map/ppermute | solution.py:12
  115.3 1.1 collective-permute-done
  116.4 0.7 copy.39
  (4 shorter events, 0.0 us)
Async XLA Ops:
  6.1 54.2 %slice-start = ((s8[7340032]{0:T(1024)(128)(4,1)}), s8[4194304]{0:T(1024)(128)(4,1)S(1)}, s32[]{:S(2)}) async-start(s8[7340032]{0:T(1024)(128)(4,1)} %bitcast.32), calls=%async_computation.2 | async-start | bytes 8388608
  54.3 6.1 %slice-start.1 = ((s8[7340032]{0:T(1024)(128)(4,1)}), s8[3145728]{0:T(1024)(128)(4,1)S(1)}, s32[]{:S(2)}) async-start(s8[7340032]{0:T(1024)(128)(4,1)} %bitcast.32), calls=%async_computation.3 | async-start | bytes 6291456
  63.7 5.2 %copy-start.1 = (s32[1,16,2]{1,2,0:T(2,128)S(1)}, s32[1,16,2]{1,2,0:T(2,128)}, u32[]{:S(2)}) copy-start(s32[1,16,2]{1,2,0:T(2,128)} %param.10) | copy-start | bytes 388
  63.7 5.2 %copy-start.2 = (f32[1,16,2]{1,2,0:T(2,128)S(1)}, f32[1,16,2]{1,2,0:T(2,128)}, u32[]{:S(2)}) copy-start(f32[1,16,2]{1,2,0:T(2,128)} %param.11) | copy-start | bytes 388
  63.7 47.8 %copy-start = (bf16[1,16,7168]{2,1,0:T(8,128)(2,1)S(1)}, bf16[1,16,7168]{2,1,0:T(8,128)(2,1)}, u32[]{:S(2)}) copy-start(bf16[1,16,7168]{2,1,0:T(8,128)(2,1)} %param.6) | copy-start | bytes 688132
  63.7 47.8 %all-to-all-start.1 = ((bf16[16,7,7168]{2,1,0:T(8,128)(2,1)}), bf16[16,7,7168]{2,1,0:T(8,128)(2,1)S(1)}, u32[]{:S(2)}, u32[]{:S(2)}) async-start(bf16[16,7,7168]{2,1,0:T(8,128)(2,1)} %copy.27), calls=%async_computation.1 | async-start | bytes 3670016 | tf_op jit(solution)/shard_map/all_to_all | solution.py:48
  113.8 2.6 %collective-permute-start = (bf16[16,7168]{1,0:T(8,128)(2,1)S(1)}, bf16[16,7168]{1,0:T(8,128)(2,1)S(1)}, u32[]{:S(2)}, u32[]{:S(2)}) collective-permute-start(bf16[16,7168]{1,0:T(8,128)(2,1)S(1)} %fusion.1), channel_id=1, source_target_pairs={{0,16},{16,0},{1,17},{17,1},{2,18},{18,2},{3,19},{19,3},{4,20},{20... | collective-permute-start | bytes 688136 | tf_op jit(solution)/shard_map/ppermute | solution.py:12

commit v3 on v2

--- a/solution.py
+++ b/solution.py
@@ -34,20 +34,20 @@
     rank = jnp.sum(jnp.dot(earlier, onehot, preferred_element_type=jnp.int32) * onehot, axis=1)
     rank = rank.reshape(rows_here, top)
     slot = jnp.arange(members * CAP)
-    slot_device = slot // CAP
-    slot_rank = slot % CAP
+    slot_device = slot % members
+    slot_rank = slot // members
     slot_expert = slot_device // per_group
     hits = (routes[None, :, :] == slot_expert[:, None, None]) & (rank[None, :, :] == slot_rank[:, None, None])
     picker = jnp.any(hits, axis=2).astype(jnp.bfloat16)
     outgoing = jnp.dot(picker, normed, preferred_element_type=jnp.float32).astype(jnp.bfloat16)
-    outgoing = outgoing.reshape(members, CAP, width)
-    incoming = lax.all_to_all(outgoing, "expert", split_axis=0, concat_axis=0, tiled=True)
-    inner = jnp.einsum("spd,fd->spf", incoming, up_block, preferred_element_type=jnp.float32)
+    outgoing = outgoing.reshape(CAP, members, width)
+    incoming = lax.all_to_all(outgoing, "expert", split_axis=1, concat_axis=1, tiled=True)
+    inner = jnp.einsum("psd,fd->psf", incoming, up_block, preferred_element_type=jnp.float32)
     active = jax.nn.silu(inner).astype(jnp.bfloat16)
-    partial = jnp.einsum("spf,fd->spd", active, down_block, preferred_element_type=jnp.float32).astype(jnp.bfloat16)
-    returned = lax.all_to_all(partial, "expert", split_axis=0, concat_axis=0, tiled=True)
-    combine = jnp.sum(jnp.where(hits, weights[None, :, :], 0.0), axis=2).T.reshape(rows_here, members, CAP)
-    mixture = jnp.einsum("rsp,spd->rd", combine, returned.astype(jnp.float32), precision=lax.Precision.HIGHEST)
+    partial = jnp.einsum("psf,fd->psd", active, down_block, preferred_element_type=jnp.float32).astype(jnp.bfloat16)
+    returned = lax.all_to_all(partial, "expert", split_axis=1, concat_axis=1, tiled=True)
+    combine = jnp.sum(jnp.where(hits, weights[None, :, :], 0.0), axis=2).T.reshape(rows_here, CAP, members)
+    mixture = jnp.einsum("rps,psd->rd", combine, returned.astype(jnp.float32), precision=lax.Precision.HIGHEST)
     section_out = (tokens.astype(jnp.float32) + mixture).astype(jnp.bfloat16)
     handed = passed_along(section_out, "segment", 1)
     return handed[None]

time: 117 us -> 114 us (0.974)
  matrix products: 11.2 us -> 7.9 us
    dot_general x3, matrix products: 9.49 us -> 6.05 us  [the longest x1 2.57 us: shards(): jnp.einsum('psd,fd->psf', incoming, up_block, preferred_element_type=jnp....]
where the time goes in v3:
time: 114 us
  blocking collectives  48.2 us (42%)
  waiting for transfers between devices  43.6 us (38%)
  matrix products  7.9 us (7%)
  starting transfers between devices  6.71 us (6%)
  local copies, waits for them, and re-layouts  4.86 us (4%)
  other arithmetic  2.76 us (2%)
    all_to_all x1, blocking collectives, shards(): lax.all_to_all(outgoing, 'expert', split_axis=1, concat_axis=1, tiled=True)  48.2 us
    all_to_all x1, waiting for transfers between devices, shards(): lax.all_to_all(partial, 'expert', split_axis=1, concat_axis=1, tiled=True)  42.5 us
    all_to_all x1, starting transfers between devices, shards(): lax.all_to_all(partial, 'expert', split_axis=1, concat_axis=1, tiled=True)  5.18 us
    dot_general x1, matrix products, shards(): jnp.einsum('psd,fd->psf', incoming, up_block, preferred_element_type=jnp....  2.57 us
    dot_general x1, matrix products, shards(): jnp.einsum('rps,psd->rd', combine, returned.astype(jnp.float32), precisio...  2.29 us
  transfers between devices with their start and end apart: 2, of which 2 were waited for; matrix products, arithmetic and copies ran while one was open for 0% of the time, Pallas kernels for 0%

profile of v3, /device:TPU:13, one launch (start us, length us, event | category | flops | bytes accessed | tf_op | source)
XLA Modules:
  0.0 114.1 jit_solution(4360576195402664200)
XLA Ops:
  0.0 0.8 copy.22
  0.8 0.1 eq.51
  0.9 0.1 fusion.7
  1.0 0.1 eq.55
  1.1 0.1 copy.23
  1.2 0.8 mul.36
  2.0 1.1 fusion.8
  3.1 0.8 fusion.20
  3.9 0.0 copy-start.3
  3.9 1.7 %convolution_convert_fusion.1 = bf16[112,7168]{1,0:T(8,128)(2,1)S(1)} fusion(pred[112,16]{0,1:T(8,128)(4,1)S(1)} %fusion.20, bf16[1,16,7168]{2,1,0:T(8,128)(2,1)} %param.6, f32[7168]{0:T(1024)S(1)} %bitcast.36, f32[16]{0:T(128)S(1)} %add_rsqrt_fusion), kind=kOutput, calls=%fused_computation.1 | convolution fusion | flops 26951680 | bytes 1865536 | tf_op jit(solution)/shard_map/dot_general | solution.py:42
  5.6 0.9 copy.24
  6.5 0.0 slice-start
  6.5 48.2 %all_to_all.10 = bf16[7,16,7168]{2,0,1:T(8,128)(2,1)S(1)} all-to-all(bf16[7,16,7168]{2,0,1:T(8,128)(2,1)S(1)} %copy.24), channel_id=1, replica_groups=mesh['segment'=2,'expert'=16] {'expert'}, dimensions={1} | all-to-all | bytes 3211264 | tf_op jit(solution)/shard_map/all_to_all | solution.py:44
  54.7 0.0 copy-done.3
  54.7 0.0 slice-start.1
  54.7 2.6 %multiply_convert_fusion = bf16[7,16,512]{2,1,0:T(8,128)(2,1)S(1)} fusion(bf16[1,512,7168]{2,1,0:T(8,128)(2,1)S(1)} %copy-done.3, bf16[7,16,7168]{2,0,1:T(8,128)(2,1)S(1)} %all_to_all.10), kind=kOutput, calls=%fused_computation.18 | convolution fusion | flops 822370304 | bytes 9060352 | tf_op jit(solution)/shard_map/psd,fd->psf/dot_general | solution.py:45
  57.2 0.0 slice-done
  57.3 0.0 slice-done.1
  57.3 1.2 %convolution_convert_fusion = bf16[7,16,7168]{2,1,0:T(8,128)(2,1)S(1)} fusion(bf16[7,16,512]{2,1,0:T(8,128)(2,1)S(1)} %multiply_convert_fusion, bf16[1,512,7168]{2,1,0:T(8,128)(2,1)S(1)} %bitcast.33), kind=kOutput, calls=%fused_computation | convolution fusion | flops 822886400 | bytes 9060352 | tf_op jit(solution)/shard_map/psf,fd->psd/dot_general | solution.py:47
  58.5 2.2 %copy.26 = bf16[7,16,7168]{2,0,1:T(8,128)(2,1)} copy(bf16[7,16,7168]{2,1,0:T(8,128)(2,1)S(1)} %convolution_convert_fusion) | data formatting | bytes 3211264 | tf_op jit(solution)/shard_map/convert_element_type | solution.py:47
  60.6 0.0 copy-start.1
  60.6 5.2 %all-to-all-start.1 = ((bf16[7,16,7168]{2,0,1:T(8,128)(2,1)}), bf16[7,16,7168]{2,0,1:T(8,128)(2,1)S(1)}, u32[]{:S(2)}, u32[]{:S(2)}) async-start(bf16[7,16,7168]{2,0,1:T(8,128)(2,1)} %copy.26), calls=%async_computation.1 | async-start | bytes 3670016 | tf_op jit(solution)/shard_map/all_to_all | solution.py:48
  65.8 0.0 copy-done.1
  65.8 0.0 copy-done.2
  65.8 0.1 select_reduce_fusion
  65.9 0.1 reshape.55
  66.0 42.5 %all-to-all-done.1 = bf16[7,16,7168]{2,0,1:T(8,128)(2,1)S(1)} async-done(((bf16[7,16,7168]{2,0,1:T(8,128)(2,1)}), bf16[7,16,7168]{2,0,1:T(8,128)(2,1)S(1)}, u32[]{:S(2)}, u32[]{:S(2)}) %all-to-all-start.1) | async-done | bytes 1605664 | tf_op jit(solution)/shard_map/all_to_all | solution.py:48
  108.5 0.0 copy-done
  108.5 2.3 %fusion.1 = bf16[16,7168]{1,0:T(8,128)(2,1)S(1)} fusion(bf16[7,16,7168]{2,0,1:T(8,128)(2,1)S(1)} %all-to-all-done.1, bf16[1,16,7168]{2,1,0:T(8,128)(2,1)S(1)} %copy-done, f32[16,7,16]{2,1,0:T(8,128)S(1)} %reshape.55), kind=kOutput, calls=%fused_computation.4 | convolution fusion | flops 154484736 | bytes 2071552 | tf_op jit(solution)/shard_map/rps,psd->rd/dot_general | solution.py:50
  110.8 1.5 %collective-permute-start = (bf16[16,7168]{1,0:T(8,128)(2,1)S(1)}, bf16[16,7168]{1,0:T(8,128)(2,1)S(1)}, u32[]{:S(2)}, u32[]{:S(2)}) collective-permute-start(bf16[16,7168]{1,0:T(8,128)(2,1)S(1)} %fusion.1), channel_id=1, source_target_pairs={{0,16},{16,0},{1,17},{17,1},{2,18},{18,2},{3,19},{19,3},{4,20},{20... | collective-permute-start | bytes 688136 | tf_op jit(solution)/shard_map/ppermute | solution.py:12
  112.3 1.1 collective-permute-done
  113.4 0.7 copy.38
  (5 shorter events, 0.0 us)
Async XLA Ops:
  3.9 50.8 %copy-start.3 = (bf16[1,512,7168]{2,1,0:T(8,128)(2,1)S(1)}, bf16[1,512,7168]{2,1,0:T(8,128)(2,1)}, u32[]{:S(2)}) copy-start(bf16[1,512,7168]{2,1,0:T(8,128)(2,1)} %param.8) | copy-start | bytes 22020100
  6.5 50.8 %slice-start = ((s8[7340032]{0:T(1024)(128)(4,1)}), s8[4194304]{0:T(1024)(128)(4,1)S(1)}, s32[]{:S(2)}) async-start(s8[7340032]{0:T(1024)(128)(4,1)} %bitcast.32), calls=%async_computation.2 | async-start | bytes 8388608
  54.7 2.6 %slice-start.1 = ((s8[7340032]{0:T(1024)(128)(4,1)}), s8[3145728]{0:T(1024)(128)(4,1)S(1)}, s32[]{:S(2)}) async-start(s8[7340032]{0:T(1024)(128)(4,1)} %bitcast.32), calls=%async_computation.3 | async-start | bytes 6291456
  60.6 5.2 %copy-start.1 = (s32[1,16,2]{1,2,0:T(2,128)S(1)}, s32[1,16,2]{1,2,0:T(2,128)}, u32[]{:S(2)}) copy-start(s32[1,16,2]{1,2,0:T(2,128)} %param.10) | copy-start | bytes 388
  60.6 5.2 %copy-start.2 = (f32[1,16,2]{1,2,0:T(2,128)S(1)}, f32[1,16,2]{1,2,0:T(2,128)}, u32[]{:S(2)}) copy-start(f32[1,16,2]{1,2,0:T(2,128)} %param.11) | copy-start | bytes 388
  60.6 47.8 %copy-start = (bf16[1,16,7168]{2,1,0:T(8,128)(2,1)S(1)}, bf16[1,16,7168]{2,1,0:T(8,128)(2,1)}, u32[]{:S(2)}) copy-start(bf16[1,16,7168]{2,1,0:T(8,128)(2,1)} %param.6) | copy-start | bytes 688132
  60.6 47.8 %all-to-all-start.1 = ((bf16[7,16,7168]{2,0,1:T(8,128)(2,1)}), bf16[7,16,7168]{2,0,1:T(8,128)(2,1)S(1)}, u32[]{:S(2)}, u32[]{:S(2)}) async-start(bf16[7,16,7168]{2,0,1:T(8,128)(2,1)} %copy.26), calls=%async_computation.1 | async-start | bytes 3670016 | tf_op jit(solution)/shard_map/all_to_all | solution.py:48
  110.8 2.6 %collective-permute-start = (bf16[16,7168]{1,0:T(8,128)(2,1)S(1)}, bf16[16,7168]{1,0:T(8,128)(2,1)S(1)}, u32[]{:S(2)}, u32[]{:S(2)}) collective-permute-start(bf16[16,7168]{1,0:T(8,128)(2,1)S(1)} %fusion.1), channel_id=1, source_target_pairs={{0,16},{16,0},{1,17},{17,1},{2,18},{18,2},{3,19},{19,3},{4,20},{20... | collective-permute-start | bytes 688136 | tf_op jit(solution)/shard_map/ppermute | solution.py:12

commit v4 on v3

--- a/solution.py
+++ b/solution.py
@@ -47,7 +47,10 @@
     partial = jnp.einsum("psf,fd->psd", active, down_block, preferred_element_type=jnp.float32).astype(jnp.bfloat16)
     returned = lax.all_to_all(partial, "expert", split_axis=1, concat_axis=1, tiled=True)
     combine = jnp.sum(jnp.where(hits, weights[None, :, :], 0.0), axis=2).T.reshape(rows_here, CAP, members)
-    mixture = jnp.einsum("rps,psd->rd", combine, returned.astype(jnp.float32), precision=lax.Precision.HIGHEST)
+    combine_hi = combine.astype(jnp.bfloat16)
+    combine_lo = (combine - combine_hi.astype(jnp.float32)).astype(jnp.bfloat16)
+    mixture = jnp.einsum("rps,psd->rd", combine_hi, returned, preferred_element_type=jnp.float32)
+    mixture = mixture + jnp.einsum("rps,psd->rd", combine_lo, returned, preferred_element_type=jnp.float32)
     section_out = (tokens.astype(jnp.float32) + mixture).astype(jnp.bfloat16)
     handed = passed_along(section_out, "segment", 1)
     return handed[None]

time: 114 us -> 114 us (level)
    dot_general x1 -> x2, matrix products: 2.29 us -> 2.22 us  [the longest x1 1.12 us: shards(): jnp.einsum('rps,psd->rd', combine_hi, returned, preferred_element_type=jn...]
where the time goes in v4:
time: 114 us
  blocking collectives  48.2 us (42%)
  waiting for transfers between devices  43.6 us (38%)
  matrix products  7.83 us (7%)
  starting transfers between devices  6.69 us (6%)
  local copies, waits for them, and re-layouts  4.86 us (4%)
  other arithmetic  2.76 us (2%)
    all_to_all x1, blocking collectives, shards(): lax.all_to_all(outgoing, 'expert', split_axis=1, concat_axis=1, tiled=True)  48.2 us
    all_to_all x1, waiting for transfers between devices, shards(): lax.all_to_all(partial, 'expert', split_axis=1, concat_axis=1, tiled=True)  42.5 us
    all_to_all x1, starting transfers between devices, shards(): lax.all_to_all(partial, 'expert', split_axis=1, concat_axis=1, tiled=True)  5.18 us
    dot_general x1, matrix products, shards(): jnp.einsum('psd,fd->psf', incoming, up_block, preferred_element_type=jnp....  2.57 us
  transfers between devices with their start and end apart: 2, of which 2 were waited for; matrix products, arithmetic and copies ran while one was open for 0% of the time, Pallas kernels for 0%

profile of v4, /device:TPU:13, one launch (start us, length us, event | category | flops | bytes accessed | tf_op | source)
XLA Modules:
  0.0 114.0 jit_solution(10299707540764809328)
XLA Ops:
  0.0 0.8 copy.34
  0.8 0.1 eq.51
  0.9 0.1 fusion.9
  1.0 0.1 eq.55
  1.1 0.1 copy.35
  1.2 0.8 mul.36
  2.0 1.1 fusion.10
  3.1 0.8 fusion.21
  3.9 0.0 copy-start.3
  3.9 1.7 %convolution_convert_fusion.1 = bf16[112,7168]{1,0:T(8,128)(2,1)S(1)} fusion(pred[112,16]{0,1:T(8,128)(4,1)S(1)} %fusion.21, bf16[1,16,7168]{2,1,0:T(8,128)(2,1)} %param.6, f32[7168]{0:T(1024)S(1)} %bitcast.40, f32[16]{0:T(128)S(1)} %add_rsqrt_fusion), kind=kOutput, calls=%fused_computation.1 | convolution fusion | flops 26951680 | bytes 1865536 | tf_op jit(solution)/shard_map/dot_general | solution.py:42
  5.6 0.9 copy.37
  6.5 0.0 slice-start
  6.5 48.2 %all_to_all.10 = bf16[7,16,7168]{2,0,1:T(8,128)(2,1)S(1)} all-to-all(bf16[7,16,7168]{2,0,1:T(8,128)(2,1)S(1)} %copy.37), channel_id=1, replica_groups=mesh['segment'=2,'expert'=16] {'expert'}, dimensions={1} | all-to-all | bytes 3211264 | tf_op jit(solution)/shard_map/all_to_all | solution.py:44
  54.7 0.0 copy-done.3
  54.7 0.0 slice-start.1
  54.7 2.6 %multiply_convert_fusion = bf16[7,16,512]{2,1,0:T(8,128)(2,1)S(1)} fusion(bf16[1,512,7168]{2,1,0:T(8,128)(2,1)S(1)} %copy-done.3, bf16[7,16,7168]{2,0,1:T(8,128)(2,1)S(1)} %all_to_all.10), kind=kOutput, calls=%fused_computation.21 | convolution fusion | flops 822370304 | bytes 9060352 | tf_op jit(solution)/shard_map/psd,fd->psf/dot_general | solution.py:45
  57.2 0.0 slice-done
  57.3 0.0 slice-done.1
  57.3 1.2 %convolution_convert_fusion = bf16[7,16,7168]{2,1,0:T(8,128)(2,1)S(1)} fusion(bf16[7,16,512]{2,1,0:T(8,128)(2,1)S(1)} %multiply_convert_fusion, bf16[1,512,7168]{2,1,0:T(8,128)(2,1)S(1)} %bitcast.37), kind=kOutput, calls=%fused_computation | convolution fusion | flops 822886400 | bytes 9060352 | tf_op jit(solution)/shard_map/psf,fd->psd/dot_general | solution.py:47
  58.5 2.2 %copy.39 = bf16[7,16,7168]{2,0,1:T(8,128)(2,1)} copy(bf16[7,16,7168]{2,1,0:T(8,128)(2,1)S(1)} %convolution_convert_fusion) | data formatting | bytes 3211264 | tf_op jit(solution)/shard_map/convert_element_type | solution.py:47
  60.6 5.2 %all-to-all-start.1 = ((bf16[7,16,7168]{2,0,1:T(8,128)(2,1)}), bf16[7,16,7168]{2,0,1:T(8,128)(2,1)S(1)}, u32[]{:S(2)}, u32[]{:S(2)}) async-start(bf16[7,16,7168]{2,0,1:T(8,128)(2,1)} %copy.39), calls=%async_computation.1 | async-start | bytes 3670016 | tf_op jit(solution)/shard_map/all_to_all | solution.py:48
  65.8 0.0 copy-done.1
  65.8 0.0 copy-done.2
  65.8 0.1 select_reduce_fusion
  65.9 0.1 reshape.55
  66.0 42.5 %all-to-all-done.1 = bf16[7,16,7168]{2,0,1:T(8,128)(2,1)S(1)} async-done(((bf16[7,16,7168]{2,0,1:T(8,128)(2,1)}), bf16[7,16,7168]{2,0,1:T(8,128)(2,1)S(1)}, u32[]{:S(2)}, u32[]{:S(2)}) %all-to-all-start.1) | async-done | bytes 1605664 | tf_op jit(solution)/shard_map/all_to_all | solution.py:48
  108.5 1.1 convolution_bitcast_fusion
  109.6 0.0 copy-done
  109.6 1.1 fusion.2
  110.7 1.5 %collective-permute-start = (bf16[16,7168]{1,0:T(8,128)(2,1)S(1)}, bf16[16,7168]{1,0:T(8,128)(2,1)S(1)}, u32[]{:S(2)}, u32[]{:S(2)}) collective-permute-start(bf16[16,7168]{1,0:T(8,128)(2,1)S(1)} %fusion.2), channel_id=1, source_target_pairs={{0,16},{16,0},{1,17},{17,1},{2,18},{18,2},{3,19},{19,3},{4,20},{20... | collective-permute-start | bytes 688136 | tf_op jit(solution)/shard_map/ppermute | solution.py:12
  112.2 1.1 collective-permute-done
  113.3 0.7 copy.58
  (6 shorter events, 0.0 us)
Async XLA Ops:
  3.9 50.8 %copy-start.3 = (bf16[1,512,7168]{2,1,0:T(8,128)(2,1)S(1)}, bf16[1,512,7168]{2,1,0:T(8,128)(2,1)}, u32[]{:S(2)}) copy-start(bf16[1,512,7168]{2,1,0:T(8,128)(2,1)} %param.8) | copy-start | bytes 22020100
  6.5 50.8 %slice-start = ((s8[7340032]{0:T(1024)(128)(4,1)}), s8[4194304]{0:T(1024)(128)(4,1)S(1)}, s32[]{:S(2)}) async-start(s8[7340032]{0:T(1024)(128)(4,1)} %bitcast.36), calls=%async_computation.2 | async-start | bytes 8388608
  54.7 2.6 %slice-start.1 = ((s8[7340032]{0:T(1024)(128)(4,1)}), s8[3145728]{0:T(1024)(128)(4,1)S(1)}, s32[]{:S(2)}) async-start(s8[7340032]{0:T(1024)(128)(4,1)} %bitcast.36), calls=%async_computation.3 | async-start | bytes 6291456
  60.6 5.2 %copy-start.1 = (s32[1,16,2]{1,2,0:T(2,128)S(1)}, s32[1,16,2]{1,2,0:T(2,128)}, u32[]{:S(2)}) copy-start(s32[1,16,2]{1,2,0:T(2,128)} %param.10) | copy-start | bytes 388
  60.6 5.2 %copy-start.2 = (f32[1,16,2]{1,2,0:T(2,128)S(1)}, f32[1,16,2]{1,2,0:T(2,128)}, u32[]{:S(2)}) copy-start(f32[1,16,2]{1,2,0:T(2,128)} %param.11) | copy-start | bytes 388
  60.6 47.8 %all-to-all-start.1 = ((bf16[7,16,7168]{2,0,1:T(8,128)(2,1)}), bf16[7,16,7168]{2,0,1:T(8,128)(2,1)S(1)}, u32[]{:S(2)}, u32[]{:S(2)}) async-start(bf16[7,16,7168]{2,0,1:T(8,128)(2,1)} %copy.39), calls=%async_computation.1 | async-start | bytes 3670016 | tf_op jit(solution)/shard_map/all_to_all | solution.py:48
  65.8 43.7 %copy-start = (bf16[1,16,7168]{2,1,0:T(8,128)(2,1)S(1)}, bf16[1,16,7168]{2,1,0:T(8,128)(2,1)}, u32[]{:S(2)}) copy-start(bf16[1,16,7168]{2,1,0:T(8,128)(2,1)} %param.6) | copy-start | bytes 688132
  110.7 2.6 %collective-permute-start = (bf16[16,7168]{1,0:T(8,128)(2,1)S(1)}, bf16[16,7168]{1,0:T(8,128)(2,1)S(1)}, u32[]{:S(2)}, u32[]{:S(2)}) collective-permute-start(bf16[16,7168]{1,0:T(8,128)(2,1)S(1)} %fusion.2), channel_id=1, source_target_pairs={{0,16},{16,0},{1,17},{17,1},{2,18},{18,2},{3,19},{19,3},{4,20},{20... | collective-permute-start | bytes 688136 | tf_op jit(solution)/shard_map/ppermute | solution.py:12

commit v5 on v4

--- a/solution.py
+++ b/solution.py
@@ -42,11 +42,12 @@
     outgoing = jnp.dot(picker, normed, preferred_element_type=jnp.float32).astype(jnp.bfloat16)
     outgoing = outgoing.reshape(CAP, members, width)
     incoming = lax.all_to_all(outgoing, "expert", split_axis=1, concat_axis=1, tiled=True)
+    combine = jnp.sum(jnp.where(hits, weights[None, :, :], 0.0), axis=2).T.reshape(rows_here, CAP, members)
+    incoming, combine = lax.optimization_barrier((incoming, combine))
     inner = jnp.einsum("psd,fd->psf", incoming, up_block, preferred_element_type=jnp.float32)
     active = jax.nn.silu(inner).astype(jnp.bfloat16)
     partial = jnp.einsum("psf,fd->psd", active, down_block, preferred_element_type=jnp.float32).astype(jnp.bfloat16)
     returned = lax.all_to_all(partial, "expert", split_axis=1, concat_axis=1, tiled=True)
-    combine = jnp.sum(jnp.where(hits, weights[None, :, :], 0.0), axis=2).T.reshape(rows_here, CAP, members)
     combine_hi = combine.astype(jnp.bfloat16)
     combine_lo = (combine - combine_hi.astype(jnp.float32)).astype(jnp.bfloat16)
     mixture = jnp.einsum("rps,psd->rd", combine_hi, returned, preferred_element_type=jnp.float32)

time: 114 us -> 122 us (1.070)
  blocking collectives: 48.2 us -> 0 us
  waiting for transfers between devices: 43.6 us -> 86 us
  matrix products: 7.83 us -> 13.9 us
  starting transfers between devices: 6.69 us -> 12.5 us
    all_to_all x1 -> x0, blocking collectives: 48.2 us -> none  [shards(): lax.all_to_all(outgoing, 'expert', split_axis=1, concat_axis=1, tiled=True)]
    all_to_all x0 -> x1, waiting for transfers between devices: none -> 42.2 us  [shards(): lax.all_to_all(outgoing, 'expert', split_axis=1, concat_axis=1, tiled=True)]
    all_to_all x0 -> x1, starting transfers between devices: none -> 6.74 us  [shards(): lax.all_to_all(outgoing, 'expert', split_axis=1, concat_axis=1, tiled=True)]
    dot_general x1, matrix products: 1.19 us -> 4.39 us  [shards(): jnp.einsum('psf,fd->psd', active, down_block, preferred_element_type=jnp....]
    dot_general x1, matrix products: 2.57 us -> 5.64 us  [shards(): jnp.einsum('psd,fd->psf', incoming, up_block, preferred_element_type=jnp....]
    reshape x1, local copies, waits for them, and re-layouts: 0.89 us -> 2.14 us  [shards(): outgoing = outgoing.reshape(CAP, members, width)]
  transfers between devices with their start and end apart: 2 -> 3, of which waited for: 2 -> 3; matrix products, arithmetic and copies ran while one was open for 0% -> 0% of each run, Pallas kernels for 0% -> 0%
where the time goes in v5:
time: 122 us; the launch traced here: 121 us
  waiting for transfers between devices  86 us (70%)
  matrix products  13.9 us (11%)
  starting transfers between devices  12.5 us (10%)
  local copies, waits for them, and re-layouts  6.08 us (5%)
  other arithmetic  2.77 us (2%)
    all_to_all x1, waiting for transfers between devices, shards(): lax.all_to_all(partial, 'expert', split_axis=1, concat_axis=1, tiled=True)  42.6 us
    all_to_all x1, waiting for transfers between devices, shards(): lax.all_to_all(outgoing, 'expert', split_axis=1, concat_axis=1, tiled=True)  42.2 us
    all_to_all x1, starting transfers between devices, shards(): lax.all_to_all(outgoing, 'expert', split_axis=1, concat_axis=1, tiled=True)  6.74 us
    dot_general x1, matrix products, shards(): jnp.einsum('psd,fd->psf', incoming, up_block, preferred_element_type=jnp....  5.64 us
    dot_general x1, matrix products, shards(): jnp.einsum('psf,fd->psd', active, down_block, preferred_element_type=jnp....  4.39 us
    all_to_all x1, starting transfers between devices, shards(): lax.all_to_all(partial, 'expert', split_axis=1, concat_axis=1, tiled=True)  4.23 us
  transfers between devices with their start and end apart: 3, of which 3 were waited for; matrix products, arithmetic and copies ran while one was open for 0% of the time, Pallas kernels for 0%

profile of v5, /device:TPU:13, one launch (start us, length us, event | category | flops | bytes accessed | tf_op | source)
XLA Modules:
  0.0 121.3 jit_solution(16753958111360851432)
XLA Ops:
  0.0 1.1 fusion.10
  1.1 0.8 copy.25
  1.9 0.1 eq.51
  2.0 0.1 fusion.9
  2.1 0.1 eq.55
  2.2 0.1 copy.26
  2.3 0.8 mul.36
  3.1 0.8 fusion.23
  3.9 1.6 %convolution_convert_fusion.1 = bf16[112,7168]{1,0:T(8,128)(2,1)S(1)} fusion(pred[112,16]{0,1:T(8,128)(4,1)S(1)} %fusion.23, bf16[1,16,7168]{2,1,0:T(8,128)(2,1)} %param.6, f32[7168]{0:T(1024)S(1)} %bitcast.38, f32[16]{0:T(128)S(1)} %add_rsqrt_fusion), kind=kOutput, calls=%fused_computation.1 | convolution fusion | flops 26951680 | bytes 1865536 | tf_op jit(solution)/shard_map/dot_general | solution.py:42
  5.4 2.1 %copy.27 = bf16[7,16,7168]{2,0,1:T(8,128)(2,1)} copy(bf16[7,16,7168]{2,1,0:T(8,128)(2,1)S(1)} %bitcast.36) | data formatting | bytes 3211264 | tf_op jit(solution)/shard_map/reshape | solution.py:43
  7.6 0.0 copy-start.1
  7.6 0.0 copy-start.2
  7.6 6.7 %all-to-all-start = ((bf16[7,16,7168]{2,0,1:T(8,128)(2,1)}), bf16[7,16,7168]{2,0,1:T(8,128)(2,1)S(1)}, u32[]{:S(2)}, u32[]{:S(2)}) async-start(bf16[7,16,7168]{2,0,1:T(8,128)(2,1)} %copy.27), calls=%async_computation | async-start | bytes 3670016 | tf_op jit(solution)/shard_map/all_to_all | solution.py:44
  14.3 0.0 copy-done.1
  14.3 0.0 copy-done.2
  14.3 0.1 select_reduce_fusion
  14.4 0.1 reshape.56
  14.5 42.2 %all-to-all-done = bf16[7,16,7168]{2,0,1:T(8,128)(2,1)S(1)} async-done(((bf16[7,16,7168]{2,0,1:T(8,128)(2,1)}), bf16[7,16,7168]{2,0,1:T(8,128)(2,1)S(1)}, u32[]{:S(2)}, u32[]{:S(2)}) %all-to-all-start) | async-done | bytes 1605664 | tf_op jit(solution)/shard_map/all_to_all | solution.py:44
  56.7 5.6 %multiply_convert_fusion = bf16[7,16,512]{2,1,0:T(8,128)(2,1)S(1)} fusion(bf16[1,512,7168]{2,1,0:T(8,128)(2,1)} %param.8, bf16[7,16,7168]{2,0,1:T(8,128)(2,1)S(1)} %all-to-all-done), kind=kOutput, calls=%fused_computation.21 | convolution fusion | flops 822370304 | bytes 9060352 | tf_op jit(solution)/shard_map/psd,fd->psf/dot_general | solution.py:47
  62.4 4.4 %convolution_convert_fusion = bf16[7,16,7168]{2,1,0:T(8,128)(2,1)S(1)} fusion(bf16[7,16,512]{2,1,0:T(8,128)(2,1)S(1)} %multiply_convert_fusion, bf16[1,512,7168]{2,1,0:T(8,128)(2,1)} %param.9), kind=kOutput, calls=%fused_computation | convolution fusion | flops 822886400 | bytes 9060352 | tf_op jit(solution)/shard_map/psf,fd->psd/dot_general | solution.py:49
  66.8 2.1 %copy.29 = bf16[7,16,7168]{2,0,1:T(8,128)(2,1)} copy(bf16[7,16,7168]{2,1,0:T(8,128)(2,1)S(1)} %convolution_convert_fusion) | data formatting | bytes 3211264 | tf_op jit(solution)/shard_map/convert_element_type | solution.py:49
  68.9 4.2 %all-to-all-start.1 = ((bf16[7,16,7168]{2,0,1:T(8,128)(2,1)}), bf16[7,16,7168]{2,0,1:T(8,128)(2,1)S(1)}, u32[]{:S(2)}, u32[]{:S(2)}) async-start(bf16[7,16,7168]{2,0,1:T(8,128)(2,1)} %copy.29), calls=%async_computation.1 | async-start | bytes 3670016 | tf_op jit(solution)/shard_map/all_to_all | solution.py:50
  73.1 0.0 copy-start
  73.2 42.6 %all-to-all-done.1 = bf16[7,16,7168]{2,0,1:T(8,128)(2,1)S(1)} async-done(((bf16[7,16,7168]{2,0,1:T(8,128)(2,1)}), bf16[7,16,7168]{2,0,1:T(8,128)(2,1)S(1)}, u32[]{:S(2)}, u32[]{:S(2)}) %all-to-all-start.1) | async-done | bytes 1605664 | tf_op jit(solution)/shard_map/all_to_all | solution.py:50
  115.8 1.1 convolution_bitcast_fusion
  116.9 0.0 copy-done
  116.9 1.1 fusion.2
  118.0 1.5 %collective-permute-start = (bf16[16,7168]{1,0:T(8,128)(2,1)S(1)}, bf16[16,7168]{1,0:T(8,128)(2,1)S(1)}, u32[]{:S(2)}, u32[]{:S(2)}) collective-permute-start(bf16[16,7168]{1,0:T(8,128)(2,1)S(1)} %fusion.2), channel_id=1, source_target_pairs={{0,16},{16,0},{1,17},{17,1},{2,18},{18,2},{3,19},{19,3},{4,20},{20... | collective-permute-start | bytes 688136 | tf_op jit(solution)/shard_map/ppermute | solution.py:12
  119.5 1.1 collective-permute-done
  120.6 0.7 copy.47
  (3 shorter events, 0.0 us)
Async XLA Ops:
  7.6 6.7 %copy-start.1 = (s32[1,16,2]{1,2,0:T(2,128)S(1)}, s32[1,16,2]{1,2,0:T(2,128)}, u32[]{:S(2)}) copy-start(s32[1,16,2]{1,2,0:T(2,128)} %param.10) | copy-start | bytes 388
  7.6 6.7 %copy-start.2 = (f32[1,16,2]{1,2,0:T(2,128)S(1)}, f32[1,16,2]{1,2,0:T(2,128)}, u32[]{:S(2)}) copy-start(f32[1,16,2]{1,2,0:T(2,128)} %param.11) | copy-start | bytes 388
  7.6 49.1 %all-to-all-start = ((bf16[7,16,7168]{2,0,1:T(8,128)(2,1)}), bf16[7,16,7168]{2,0,1:T(8,128)(2,1)S(1)}, u32[]{:S(2)}, u32[]{:S(2)}) async-start(bf16[7,16,7168]{2,0,1:T(8,128)(2,1)} %copy.27), calls=%async_computation | async-start | bytes 3670016 | tf_op jit(solution)/shard_map/all_to_all | solution.py:44
  68.9 46.9 %all-to-all-start.1 = ((bf16[7,16,7168]{2,0,1:T(8,128)(2,1)}), bf16[7,16,7168]{2,0,1:T(8,128)(2,1)S(1)}, u32[]{:S(2)}, u32[]{:S(2)}) async-start(bf16[7,16,7168]{2,0,1:T(8,128)(2,1)} %copy.29), calls=%async_computation.1 | async-start | bytes 3670016 | tf_op jit(solution)/shard_map/all_to_all | solution.py:50
  73.1 43.7 %copy-start = (bf16[1,16,7168]{2,1,0:T(8,128)(2,1)S(1)}, bf16[1,16,7168]{2,1,0:T(8,128)(2,1)}, u32[]{:S(2)}) copy-start(bf16[1,16,7168]{2,1,0:T(8,128)(2,1)} %param.6) | copy-start | bytes 688132
  118.0 2.6 %collective-permute-start = (bf16[16,7168]{1,0:T(8,128)(2,1)S(1)}, bf16[16,7168]{1,0:T(8,128)(2,1)S(1)}, u32[]{:S(2)}, u32[]{:S(2)}) collective-permute-start(bf16[16,7168]{1,0:T(8,128)(2,1)S(1)} %fusion.2), channel_id=1, source_target_pairs={{0,16},{16,0},{1,17},{17,1},{2,18},{18,2},{3,19},{19,3},{4,20},{20... | collective-permute-start | bytes 688136 | tf_op jit(solution)/shard_map/ppermute | solution.py:12

commit v6 on v4

--- a/solution.py
+++ b/solution.py
@@ -27,12 +27,12 @@
     normed = (
         tokens.astype(jnp.float32) * lax.rsqrt(square + 1e-06) * gain.astype(jnp.float32)
     ).astype(jnp.bfloat16)
-    flat = routes.reshape(-1)
-    onehot = (flat[:, None] == jnp.arange(EXPERTS)[None, :]).astype(jnp.int32)
-    positions = jnp.arange(flat.shape[0])
+    chosen = routes[:, :, None] == jnp.arange(EXPERTS)[None, None, :]
+    named = jnp.sum(chosen.astype(jnp.int32), axis=1)
+    positions = jnp.arange(rows_here)
     earlier = (positions[None, :] < positions[:, None]).astype(jnp.int32)
-    rank = jnp.sum(jnp.dot(earlier, onehot, preferred_element_type=jnp.int32) * onehot, axis=1)
-    rank = rank.reshape(rows_here, top)
+    before = jnp.dot(earlier, named, preferred_element_type=jnp.int32)
+    rank = jnp.sum(jnp.where(chosen, before[:, None, :], 0), axis=2)
     slot = jnp.arange(members * CAP)
     slot_device = slot % members
     slot_rank = slot // members

time: 114 us -> 115 us (level)
  other arithmetic: 2.76 us -> 4.13 us
    reduce_sum x0 -> x2, other arithmetic: none -> 1.39 us  [the longest x1 0.7 us: shards(): rank = jnp.sum(jnp.where(chosen, before[:, None, :], 0), axis=2)]
where the time goes in v6:
time: 115 us; the launch traced here: 114 us
  blocking collectives  48.2 us (42%)
  waiting for transfers between devices  43.6 us (38%)
  matrix products  7.82 us (7%)
  starting transfers between devices  6.69 us (6%)
  other arithmetic  4.13 us (4%)
  local copies, waits for them, and re-layouts  3.83 us (3%)
    all_to_all x1, blocking collectives, shards(): lax.all_to_all(outgoing, 'expert', split_axis=1, concat_axis=1, tiled=True)  48.2 us
    all_to_all x1, waiting for transfers between devices, shards(): lax.all_to_all(partial, 'expert', split_axis=1, concat_axis=1, tiled=True)  42.5 us
    all_to_all x1, starting transfers between devices, shards(): lax.all_to_all(partial, 'expert', split_axis=1, concat_axis=1, tiled=True)  5.18 us
    dot_general x1, matrix products, shards(): jnp.einsum('psd,fd->psf', incoming, up_block, preferred_element_type=jnp....  2.57 us
  transfers between devices with their start and end apart: 2, of which 2 were waited for; matrix products, arithmetic and copies ran while one was open for 0% of the time, Pallas kernels for 0%

profile of v6, /device:TPU:13, one launch (start us, length us, event | category | flops | bytes accessed | tf_op | source)
XLA Modules:
  0.0 114.3 jit_solution(6446949412328378701)
XLA Ops:
  0.0 0.7 convert_reduce_fusion
  0.7 0.1 fusion.21
  0.8 0.7 select_reduce_fusion.1
  1.5 0.8 mul.32
  2.3 1.1 fusion.9
  3.4 0.8 fusion.20
  4.2 0.0 copy-start.3
  4.2 1.7 %convolution_convert_fusion.1 = bf16[112,7168]{1,0:T(8,128)(2,1)S(1)} fusion(pred[112,16]{0,1:T(8,128)(4,1)S(1)} %fusion.20, bf16[1,16,7168]{2,1,0:T(8,128)(2,1)} %param.6, f32[7168]{0:T(1024)S(1)} %bitcast.41, f32[16]{0:T(128)S(1)} %add_rsqrt_fusion), kind=kOutput, calls=%fused_computation.1 | convolution fusion | flops 26951680 | bytes 1865536 | tf_op jit(solution)/shard_map/dot_general | solution.py:42
  5.9 0.9 copy.36
  6.8 0.0 slice-start
  6.8 48.2 %all_to_all.10 = bf16[7,16,7168]{2,0,1:T(8,128)(2,1)S(1)} all-to-all(bf16[7,16,7168]{2,0,1:T(8,128)(2,1)S(1)} %copy.36), channel_id=1, replica_groups=mesh['segment'=2,'expert'=16] {'expert'}, dimensions={1} | all-to-all | bytes 3211264 | tf_op jit(solution)/shard_map/all_to_all | solution.py:44
  55.0 0.0 copy-done.3
  55.0 0.0 slice-start.1
  55.0 2.6 %multiply_convert_fusion = bf16[7,16,512]{2,1,0:T(8,128)(2,1)S(1)} fusion(bf16[1,512,7168]{2,1,0:T(8,128)(2,1)S(1)} %copy-done.3, bf16[7,16,7168]{2,0,1:T(8,128)(2,1)S(1)} %all_to_all.10), kind=kOutput, calls=%fused_computation.19 | convolution fusion | flops 822370304 | bytes 9060352 | tf_op jit(solution)/shard_map/psd,fd->psf/dot_general | solution.py:45
  57.6 0.0 slice-done
  57.6 0.0 slice-done.1
  57.6 1.2 %convolution_convert_fusion = bf16[7,16,7168]{2,1,0:T(8,128)(2,1)S(1)} fusion(bf16[7,16,512]{2,1,0:T(8,128)(2,1)S(1)} %multiply_convert_fusion, bf16[1,512,7168]{2,1,0:T(8,128)(2,1)S(1)} %bitcast.38), kind=kOutput, calls=%fused_computation | convolution fusion | flops 822886400 | bytes 9060352 | tf_op jit(solution)/shard_map/psf,fd->psd/dot_general | solution.py:47
  58.8 2.1 %copy.38 = bf16[7,16,7168]{2,0,1:T(8,128)(2,1)} copy(bf16[7,16,7168]{2,1,0:T(8,128)(2,1)S(1)} %convolution_convert_fusion) | data formatting | bytes 3211264 | tf_op jit(solution)/shard_map/convert_element_type | solution.py:47
  61.0 0.0 copy-start.1
  61.0 0.0 copy-start.2
  61.0 5.2 %all-to-all-start.1 = ((bf16[7,16,7168]{2,0,1:T(8,128)(2,1)}), bf16[7,16,7168]{2,0,1:T(8,128)(2,1)S(1)}, u32[]{:S(2)}, u32[]{:S(2)}) async-start(bf16[7,16,7168]{2,0,1:T(8,128)(2,1)} %copy.38), calls=%async_computation.1 | async-start | bytes 3670016 | tf_op jit(solution)/shard_map/all_to_all | solution.py:48
  66.2 0.0 copy-done.1
  66.2 0.0 copy-done.2
  66.2 0.1 select_reduce_fusion
  66.3 0.1 reshape.56
  66.3 42.5 %all-to-all-done.1 = bf16[7,16,7168]{2,0,1:T(8,128)(2,1)S(1)} async-done(((bf16[7,16,7168]{2,0,1:T(8,128)(2,1)}), bf16[7,16,7168]{2,0,1:T(8,128)(2,1)S(1)}, u32[]{:S(2)}, u32[]{:S(2)}) %all-to-all-start.1) | async-done | bytes 1605664 | tf_op jit(solution)/shard_map/all_to_all | solution.py:48
  108.8 1.1 convolution_bitcast_fusion
  109.9 0.0 copy-done
  109.9 1.1 fusion.2
  111.0 1.5 %collective-permute-start = (bf16[16,7168]{1,0:T(8,128)(2,1)S(1)}, bf16[16,7168]{1,0:T(8,128)(2,1)S(1)}, u32[]{:S(2)}, u32[]{:S(2)}) collective-permute-start(bf16[16,7168]{1,0:T(8,128)(2,1)S(1)} %fusion.2), channel_id=1, source_target_pairs={{0,16},{16,0},{1,17},{17,1},{2,18},{18,2},{3,19},{19,3},{4,20},{20... | collective-permute-start | bytes 688136 | tf_op jit(solution)/shard_map/ppermute | solution.py:12
  112.5 1.1 collective-permute-done
  113.6 0.7 copy.57
  (4 shorter events, 0.0 us)
Async XLA Ops:
  4.2 50.8 %copy-start.3 = (bf16[1,512,7168]{2,1,0:T(8,128)(2,1)S(1)}, bf16[1,512,7168]{2,1,0:T(8,128)(2,1)}, u32[]{:S(2)}) copy-start(bf16[1,512,7168]{2,1,0:T(8,128)(2,1)} %param.8) | copy-start | bytes 22020100
  6.8 50.8 %slice-start = ((s8[7340032]{0:T(1024)(128)(4,1)}), s8[4194304]{0:T(1024)(128)(4,1)S(1)}, s32[]{:S(2)}) async-start(s8[7340032]{0:T(1024)(128)(4,1)} %bitcast.37), calls=%async_computation.2 | async-start | bytes 8388608
  55.0 2.6 %slice-start.1 = ((s8[7340032]{0:T(1024)(128)(4,1)}), s8[3145728]{0:T(1024)(128)(4,1)S(1)}, s32[]{:S(2)}) async-start(s8[7340032]{0:T(1024)(128)(4,1)} %bitcast.37), calls=%async_computation.3 | async-start | bytes 6291456
  61.0 5.2 %copy-start.1 = (s32[1,16,2]{1,2,0:T(2,128)S(1)}, s32[1,16,2]{1,2,0:T(2,128)}, u32[]{:S(2)}) copy-start(s32[1,16,2]{1,2,0:T(2,128)} %param.10) | copy-start | bytes 388
  61.0 5.2 %copy-start.2 = (f32[1,16,2]{1,2,0:T(2,128)S(1)}, f32[1,16,2]{1,2,0:T(2,128)}, u32[]{:S(2)}) copy-start(f32[1,16,2]{1,2,0:T(2,128)} %param.11) | copy-start | bytes 388
  61.0 47.8 %all-to-all-start.1 = ((bf16[7,16,7168]{2,0,1:T(8,128)(2,1)}), bf16[7,16,7168]{2,0,1:T(8,128)(2,1)S(1)}, u32[]{:S(2)}, u32[]{:S(2)}) async-start(bf16[7,16,7168]{2,0,1:T(8,128)(2,1)} %copy.38), calls=%async_computation.1 | async-start | bytes 3670016 | tf_op jit(solution)/shard_map/all_to_all | solution.py:48
  66.1 43.7 %copy-start = (bf16[1,16,7168]{2,1,0:T(8,128)(2,1)S(1)}, bf16[1,16,7168]{2,1,0:T(8,128)(2,1)}, u32[]{:S(2)}) copy-start(bf16[1,16,7168]{2,1,0:T(8,128)(2,1)} %param.6) | copy-start | bytes 688132
  111.0 2.6 %collective-permute-start = (bf16[16,7168]{1,0:T(8,128)(2,1)S(1)}, bf16[16,7168]{1,0:T(8,128)(2,1)S(1)}, u32[]{:S(2)}, u32[]{:S(2)}) collective-permute-start(bf16[16,7168]{1,0:T(8,128)(2,1)S(1)} %fusion.2), channel_id=1, source_target_pairs={{0,16},{16,0},{1,17},{17,1},{2,18},{18,2},{3,19},{19,3},{4,20},{20... | collective-permute-start | bytes 688136 | tf_op jit(solution)/shard_map/ppermute | solution.py:12

commit v7 on v6

--- a/solution.py
+++ b/solution.py
@@ -5,6 +5,7 @@
 
 EXPERTS = 8
 CAP = 7
+LANES = 128
 
 
 def passed_along(shard, axis, by):
@@ -40,12 +41,14 @@
     hits = (routes[None, :, :] == slot_expert[:, None, None]) & (rank[None, :, :] == slot_rank[:, None, None])
     picker = jnp.any(hits, axis=2).astype(jnp.bfloat16)
     outgoing = jnp.dot(picker, normed, preferred_element_type=jnp.float32).astype(jnp.bfloat16)
-    outgoing = outgoing.reshape(CAP, members, width)
-    incoming = lax.all_to_all(outgoing, "expert", split_axis=1, concat_axis=1, tiled=True)
-    inner = jnp.einsum("psd,fd->psf", incoming, up_block, preferred_element_type=jnp.float32)
+    outgoing = outgoing.reshape(CAP, members, width).transpose(1, 0, 2).reshape(members, -1, LANES)
+    incoming = lax.all_to_all(outgoing, "expert", split_axis=0, concat_axis=0, tiled=True)
+    incoming = incoming.reshape(members, CAP, width)
+    inner = jnp.einsum("spd,fd->spf", incoming, up_block, preferred_element_type=jnp.float32)
     active = jax.nn.silu(inner).astype(jnp.bfloat16)
-    partial = jnp.einsum("psf,fd->psd", active, down_block, preferred_element_type=jnp.float32).astype(jnp.bfloat16)
-    returned = lax.all_to_all(partial, "expert", split_axis=1, concat_axis=1, tiled=True)
+    partial = jnp.einsum("spf,fd->spd", active, down_block, preferred_element_type=jnp.float32).astype(jnp.bfloat16)
+    returned = lax.all_to_all(partial.reshape(members, -1, LANES), "expert", split_axis=0, concat_axis=0, tiled=True)
+    returned = returned.reshape(members, CAP, width).transpose(1, 0, 2)
     combine = jnp.sum(jnp.where(hits, weights[None, :, :], 0.0), axis=2).T.reshape(rows_here, CAP, members)
     combine_hi = combine.astype(jnp.bfloat16)
     combine_lo = (combine - combine_hi.astype(jnp.float32)).astype(jnp.bfloat16)

time: 115 us -> 119 us (1.035)
  local copies, waits for them, and re-layouts: 3.83 us -> 13.9 us
  blocking collectives: 48.2 us -> 43.1 us
  waiting for transfers between devices: 43.6 us -> 38.8 us
  matrix products: 7.82 us -> 11.5 us
    reshape x1 -> x5, local copies, waits for them, and re-layouts: 0.89 us -> 12.2 us  [the longest x1 4.44 us: shards(): incoming = incoming.reshape(members, CAP, width)]
    all_to_all x1, blocking collectives: 48.2 us -> 43.1 us  [shards(): lax.all_to_all(outgoing, 'expert', split_axis=0, concat_axis=0, tiled=True)]
    all_to_all x1, waiting for transfers between devices: 42.5 us -> 37.7 us  [shards(): lax.all_to_all(partial.reshape(members, -1, LANES), 'expert', split_axis=...]
    dot_general x2, matrix products: 3.76 us -> 7.63 us  [the longest x1 6.33 us: shards(): jnp.einsum('spd,fd->spf', incoming, up_block, preferred_element_type=jnp....]
    convert_element_type x1, local copies, waits for them, and re-layouts: 2.14 us -> 0.89 us  [shards(): jnp.einsum('spf,fd->spd', active, down_block, preferred_element_type=jnp....]
where the time goes in v7:
time: 119 us
  blocking collectives  43.1 us (36%)
  waiting for transfers between devices  38.8 us (33%)
  local copies, waits for them, and re-layouts  13.9 us (12%)
  matrix products  11.5 us (10%)
  starting transfers between devices  7.23 us (6%)
  other arithmetic  4.13 us (3%)
    all_to_all x1, blocking collectives, shards(): lax.all_to_all(outgoing, 'expert', split_axis=0, concat_axis=0, tiled=True)  43.1 us
    all_to_all x1, waiting for transfers between devices, shards(): lax.all_to_all(partial.reshape(members, -1, LANES), 'expert', split_axis=...  37.7 us
    dot_general x1, matrix products, shards(): jnp.einsum('spd,fd->spf', incoming, up_block, preferred_element_type=jnp....  6.33 us
    all_to_all x1, starting transfers between devices, shards(): lax.all_to_all(partial.reshape(members, -1, LANES), 'expert', split_axis=...  5.69 us
    reshape x1, local copies, waits for them, and re-layouts, shards(): incoming = incoming.reshape(members, CAP, width)  4.44 us
    reshape x1, local copies, waits for them, and re-layouts, shards(): partial.reshape(members, -1, LANES)  3.03 us
    reshape x2, local copies, waits for them, and re-layouts, shards(): outgoing.reshape(CAP, members, width).transpose(1, 0, 2)  3.03 us
  transfers between devices with their start and end apart: 2, of which 2 were waited for; matrix products, arithmetic and copies ran while one was open for 0% of the time, Pallas kernels for 0%

profile of v7, /device:TPU:13, one launch (start us, length us, event | category | flops | bytes accessed | tf_op | source)
XLA Modules:
  0.0 118.9 jit_solution(8891743757348953543)
XLA Ops:
  0.0 0.7 convert_reduce_fusion
  0.7 0.1 fusion.23
  0.8 0.7 select_reduce_fusion.1
  1.5 0.8 mul.32
  2.3 1.1 fusion.11
  3.4 0.8 fusion.22
  4.2 1.6 %convolution_convert_fusion.1 = bf16[112,7168]{1,0:T(8,128)(2,1)S(1)} fusion(pred[112,16]{0,1:T(8,128)(4,1)S(1)} %fusion.22, bf16[1,16,7168]{2,1,0:T(8,128)(2,1)} %param.6, f32[7168]{0:T(1024)S(1)} %bitcast.50, f32[16]{0:T(128)S(1)} %add_rsqrt_fusion), kind=kOutput, calls=%fused_computation.1 | convolution fusion | flops 26951680 | bytes 1865536 | tf_op jit(solution)/shard_map/dot_general | solution.py:43
  5.8 0.9 copy.52
  6.7 2.1 %reshape.70 = bf16[16,392,128]{2,1,0:T(8,128)(2,1)S(1)} reshape(bf16[16,7,7168]{2,1,0:T(8,128)(2,1)S(1)} %bitcast.47) | data formatting | bytes 3211264 | tf_op jit(solution)/shard_map/reshape | solution.py:44
  8.8 43.1 %all_to_all.10 = bf16[16,392,128]{2,1,0:T(8,128)(2,1)} all-to-all(bf16[16,392,128]{2,1,0:T(8,128)(2,1)S(1)} %reshape.70), channel_id=1, replica_groups=mesh['segment'=2,'expert'=16] {'expert'}, dimensions={0} | all-to-all | bytes 3211264 | tf_op jit(solution)/shard_map/all_to_all | solution.py:45
  51.9 0.0 slice-start
  51.9 4.4 %reshape.71 = bf16[16,7,7168]{2,1,0:T(8,128)(2,1)} reshape(bf16[16,392,128]{2,1,0:T(8,128)(2,1)} %all_to_all.10) | data formatting | bytes 3211264 | tf_op jit(solution)/shard_map/reshape | solution.py:46
  56.3 6.3 %multiply_convert_fusion = bf16[16,7,512]{2,0,1:T(8,128)(2,1)S(1)} fusion(bf16[1,512,7168]{2,1,0:T(8,128)(2,1)} %param.8, bf16[16,7,7168]{2,1,0:T(8,128)(2,1)} %reshape.71), kind=kOutput, calls=%fused_computation.22 | convolution fusion | flops 822370304 | bytes 9060352 | tf_op jit(solution)/shard_map/spd,fd->spf/dot_general | solution.py:47
  62.7 0.0 slice-done
  62.7 0.0 slice-done.1
  62.7 1.3 %convolution_convert_fusion = bf16[16,7,7168]{2,0,1:T(8,128)(2,1)S(1)} fusion(bf16[16,7,512]{2,0,1:T(8,128)(2,1)S(1)} %multiply_convert_fusion, bf16[1,512,7168]{2,1,0:T(8,128)(2,1)S(1)} %bitcast.46), kind=kOutput, calls=%fused_computation | convolution fusion | flops 822886400 | bytes 9060352 | tf_op jit(solution)/shard_map/spf,fd->spd/dot_general | solution.py:49
  64.0 0.9 copy.30
  64.9 3.0 %reshape.72 = bf16[16,392,128]{2,1,0:T(8,128)(2,1)} reshape(bf16[16,7,7168]{2,1,0:T(8,128)(2,1)S(1)} %copy.30) | data formatting | bytes 3211264 | tf_op jit(solution)/shard_map/reshape | solution.py:50
  68.0 5.7 %all-to-all-start.1 = ((bf16[16,392,128]{2,1,0:T(8,128)(2,1)}), bf16[16,392,128]{2,1,0:T(8,128)(2,1)S(1)}, u32[]{:S(2)}, u32[]{:S(2)}) async-start(bf16[16,392,128]{2,1,0:T(8,128)(2,1)} %reshape.72), calls=%async_computation.1 | async-start | bytes 3211264 | tf_op jit(solution)/shard_map/all_to_all | solution.py:50
  73.7 0.0 copy-done.1
  73.7 0.0 copy-done.2
  73.7 0.1 select_reduce_fusion
  73.8 0.1 reshape.68
  73.8 37.7 %all-to-all-done.1 = bf16[16,392,128]{2,1,0:T(8,128)(2,1)S(1)} async-done(((bf16[16,392,128]{2,1,0:T(8,128)(2,1)}), bf16[16,392,128]{2,1,0:T(8,128)(2,1)S(1)}, u32[]{:S(2)}, u32[]{:S(2)}) %all-to-all-start.1) | async-done | bytes 1605664 | tf_op jit(solution)/shard_map/all_to_all | solution.py:50
  111.5 1.7 %reshape.73 = bf16[16,7,7168]{2,1,0:T(8,128)(2,1)S(1)} reshape(bf16[16,392,128]{2,1,0:T(8,128)(2,1)S(1)} %all-to-all-done.1) | data formatting | bytes 3211264 | tf_op jit(solution)/shard_map/reshape | solution.py:51
  113.3 0.0 copy-start
  113.3 1.1 convolution_bitcast_fusion
  114.4 0.0 copy-done
  114.4 1.1 fusion.2
  115.5 1.5 %collective-permute-start = (bf16[16,7168]{1,0:T(8,128)(2,1)S(1)}, bf16[16,7168]{1,0:T(8,128)(2,1)S(1)}, u32[]{:S(2)}, u32[]{:S(2)}) collective-permute-start(bf16[16,7168]{1,0:T(8,128)(2,1)S(1)} %fusion.2), channel_id=1, source_target_pairs={{0,16},{16,0},{1,17},{17,1},{2,18},{18,2},{3,19},{19,3},{4,20},{20... | collective-permute-start | bytes 688136 | tf_op jit(solution)/shard_map/ppermute | solution.py:13
  117.0 1.1 collective-permute-done
  118.2 0.7 copy.54
  (6 shorter events, 0.0 us)
Async XLA Ops:
  51.9 10.8 %slice-start = ((s8[7340032]{0:T(1024)(128)(4,1)}), s8[3145728]{0:T(1024)(128)(4,1)S(1)}, s32[]{:S(2)}) async-start(s8[7340032]{0:T(1024)(128)(4,1)} %bitcast.45), calls=%async_computation.2 | async-start | bytes 6291456
  56.3 6.3 %slice-start.1 = ((s8[7340032]{0:T(1024)(128)(4,1)}), s8[4194304]{0:T(1024)(128)(4,1)S(1)}, s32[]{:S(2)}) async-start(s8[7340032]{0:T(1024)(128)(4,1)} %bitcast.45), calls=%async_computation.3 | async-start | bytes 8388608
  68.0 5.7 %copy-start.1 = (s32[1,16,2]{1,2,0:T(2,128)S(1)}, s32[1,16,2]{1,2,0:T(2,128)}, u32[]{:S(2)}) copy-start(s32[1,16,2]{1,2,0:T(2,128)} %param.10) | copy-start | bytes 388
  68.0 5.7 %copy-start.2 = (f32[1,16,2]{1,2,0:T(2,128)S(1)}, f32[1,16,2]{1,2,0:T(2,128)}, u32[]{:S(2)}) copy-start(f32[1,16,2]{1,2,0:T(2,128)} %param.11) | copy-start | bytes 388
  68.0 43.6 %all-to-all-start.1 = ((bf16[16,392,128]{2,1,0:T(8,128)(2,1)}), bf16[16,392,128]{2,1,0:T(8,128)(2,1)S(1)}, u32[]{:S(2)}, u32[]{:S(2)}) async-start(bf16[16,392,128]{2,1,0:T(8,128)(2,1)} %reshape.72), calls=%async_computation.1 | async-start | bytes 3211264 | tf_op jit(solution)/shard_map/all_to_all | solution.py:50
  113.3 1.1 copy-start
  115.5 2.6 %collective-permute-start = (bf16[16,7168]{1,0:T(8,128)(2,1)S(1)}, bf16[16,7168]{1,0:T(8,128)(2,1)S(1)}, u32[]{:S(2)}, u32[]{:S(2)}) collective-permute-start(bf16[16,7168]{1,0:T(8,128)(2,1)S(1)} %fusion.2), channel_id=1, source_target_pairs={{0,16},{16,0},{1,17},{17,1},{2,18},{18,2},{3,19},{19,3},{4,20},{20... | collective-permute-start | bytes 688136 | tf_op jit(solution)/shard_map/ppermute | solution.py:13

commit v8 on v6

--- a/solution.py
+++ b/solution.py
@@ -5,6 +5,7 @@
 
 EXPERTS = 8
 CAP = 7
+SLOTS = 8
 
 
 def passed_along(shard, axis, by):
@@ -33,20 +34,20 @@
     earlier = (positions[None, :] < positions[:, None]).astype(jnp.int32)
     before = jnp.dot(earlier, named, preferred_element_type=jnp.int32)
     rank = jnp.sum(jnp.where(chosen, before[:, None, :], 0), axis=2)
-    slot = jnp.arange(members * CAP)
+    slot = jnp.arange(members * SLOTS)
     slot_device = slot % members
     slot_rank = slot // members
     slot_expert = slot_device // per_group
     hits = (routes[None, :, :] == slot_expert[:, None, None]) & (rank[None, :, :] == slot_rank[:, None, None])
     picker = jnp.any(hits, axis=2).astype(jnp.bfloat16)
     outgoing = jnp.dot(picker, normed, preferred_element_type=jnp.float32).astype(jnp.bfloat16)
-    outgoing = outgoing.reshape(CAP, members, width)
+    outgoing = outgoing.reshape(SLOTS, members, width)
     incoming = lax.all_to_all(outgoing, "expert", split_axis=1, concat_axis=1, tiled=True)
     inner = jnp.einsum("psd,fd->psf", incoming, up_block, preferred_element_type=jnp.float32)
     active = jax.nn.silu(inner).astype(jnp.bfloat16)
     partial = jnp.einsum("psf,fd->psd", active, down_block, preferred_element_type=jnp.float32).astype(jnp.bfloat16)
     returned = lax.all_to_all(partial, "expert", split_axis=1, concat_axis=1, tiled=True)
-    combine = jnp.sum(jnp.where(hits, weights[None, :, :], 0.0), axis=2).T.reshape(rows_here, CAP, members)
+    combine = jnp.sum(jnp.where(hits, weights[None, :, :], 0.0), axis=2).T.reshape(rows_here, SLOTS, members)
     combine_hi = combine.astype(jnp.bfloat16)
     combine_lo = (combine - combine_hi.astype(jnp.float32)).astype(jnp.bfloat16)
     mixture = jnp.einsum("rps,psd->rd", combine_hi, returned, preferred_element_type=jnp.float32)

time: 115 us -> 113 us (0.983)
  matrix products: 7.82 us -> 6.4 us
where the time goes in v8:
time: 113 us
  blocking collectives  48.2 us (43%)
  waiting for transfers between devices  43.3 us (38%)
  starting transfers between devices  6.71 us (6%)
  matrix products  6.4 us (6%)
  local copies, waits for them, and re-layouts  4.3 us (4%)
  other arithmetic  4.14 us (4%)
    all_to_all x1, blocking collectives, shards(): lax.all_to_all(outgoing, 'expert', split_axis=1, concat_axis=1, tiled=True)  48.2 us
    all_to_all x1, waiting for transfers between devices, shards(): lax.all_to_all(partial, 'expert', split_axis=1, concat_axis=1, tiled=True)  42.2 us
    all_to_all x1, starting transfers between devices, shards(): lax.all_to_all(partial, 'expert', split_axis=1, concat_axis=1, tiled=True)  5.18 us
    dot_general x1, matrix products, shards(): jnp.einsum('psd,fd->psf', incoming, up_block, preferred_element_type=jnp....  2.55 us
    convert_element_type x1, local copies, waits for them, and re-layouts, shards(): jnp.einsum('psf,fd->psd', active, down_block, preferred_element_type=jnp....  2.27 us
  transfers between devices with their start and end apart: 2, of which 2 were waited for; matrix products, arithmetic and copies ran while one was open for 0% of the time, Pallas kernels for 0%

profile of v8, /device:TPU:13, one launch (start us, length us, event | category | flops | bytes accessed | tf_op | source)
XLA Modules:
  0.0 113.2 jit_solution(3848891221636207872)
XLA Ops:
  0.0 0.7 convert_reduce_fusion
  0.7 0.1 fusion.17
  0.8 0.7 select_reduce_fusion.1
  1.5 0.8 mul.32
  2.3 1.1 fusion.6
  3.4 0.8 fusion.16
  4.2 0.0 copy-start
  4.2 1.8 %convolution_convert_fusion.1 = bf16[128,7168]{1,0:T(8,128)(2,1)S(1)} fusion(pred[128,16]{0,1:T(8,128)(4,1)S(1)} %fusion.16, bf16[1,16,7168]{2,1,0:T(8,128)(2,1)} %param.6, f32[7168]{0:T(1024)S(1)} %bitcast.45, f32[16]{0:T(128)S(1)} %add_rsqrt_fusion), kind=kOutput, calls=%fused_computation.1 | convolution fusion | flops 30736384 | bytes 2095168 | tf_op jit(solution)/shard_map/dot_general | solution.py:43
  6.0 1.0 copy.28
  7.0 0.0 slice-start
  7.0 48.2 %all_to_all.10 = bf16[8,16,7168]{2,0,1:T(8,128)(2,1)S(1)} all-to-all(bf16[8,16,7168]{2,0,1:T(8,128)(2,1)S(1)} %copy.28), channel_id=1, replica_groups=mesh['segment'=2,'expert'=16] {'expert'}, dimensions={1} | all-to-all | bytes 3670016 | tf_op jit(solution)/shard_map/all_to_all | solution.py:45
  55.2 0.0 copy-done
  55.2 0.0 slice-start.1
  55.2 2.5 %multiply_convert_fusion = bf16[8,16,512]{2,0,1:T(8,128)(2,1)S(1)} fusion(bf16[8,16,7168]{2,0,1:T(8,128)(2,1)S(1)} %all_to_all.10, bf16[1,512,7168]{2,1,0:T(8,128)(2,1)S(1)} %copy-done), kind=kOutput, calls=%fused_computation.15 | convolution fusion | flops 939851776 | bytes 9306112 | tf_op jit(solution)/shard_map/psd,fd->psf/dot_general | solution.py:46
  57.7 0.0 slice-done
  57.8 0.0 slice-done.1
  57.8 1.1 convolution_convert_fusion
  58.9 2.3 %copy.30 = bf16[8,16,7168]{2,0,1:T(8,128)(2,1)} copy(bf16[8,16,7168]{2,1,0:T(8,128)(2,1)S(1)} %convolution_convert_fusion) | data formatting | bytes 3670016 | tf_op jit(solution)/shard_map/convert_element_type | solution.py:48
  61.2 5.2 %all-to-all-start.1 = ((bf16[8,16,7168]{2,0,1:T(8,128)(2,1)}), bf16[8,16,7168]{2,0,1:T(8,128)(2,1)S(1)}, u32[]{:S(2)}, u32[]{:S(2)}) async-start(bf16[8,16,7168]{2,0,1:T(8,128)(2,1)} %copy.30), calls=%async_computation.1 | async-start | bytes 3670016 | tf_op jit(solution)/shard_map/all_to_all | solution.py:49
  66.4 0.0 copy-done.2
  66.4 0.0 copy-done.3
  66.4 0.1 select_reduce_fusion
  66.5 0.1 reshape.56
  66.6 0.1 copy.32
  66.7 0.1 copy.31
  66.8 42.2 %all-to-all-done.1 = bf16[8,16,7168]{2,0,1:T(8,128)(2,1)S(1)} async-done(((bf16[8,16,7168]{2,0,1:T(8,128)(2,1)}), bf16[8,16,7168]{2,0,1:T(8,128)(2,1)S(1)}, u32[]{:S(2)}, u32[]{:S(2)}) %all-to-all-start.1) | async-done | bytes 1835040 | tf_op jit(solution)/shard_map/all_to_all | solution.py:49
  109.0 0.4 convolution_bitcast_fusion
  109.4 0.0 copy-done.1
  109.4 0.4 fusion.2
  109.8 1.5 %collective-permute-start = (bf16[16,7168]{1,0:T(8,128)(2,1)S(1)}, bf16[16,7168]{1,0:T(8,128)(2,1)S(1)}, u32[]{:S(2)}, u32[]{:S(2)}) collective-permute-start(bf16[16,7168]{1,0:T(8,128)(2,1)S(1)} %fusion.2), channel_id=1, source_target_pairs={{0,16},{16,0},{1,17},{17,1},{2,18},{18,2},{3,19},{19,3},{4,20},{20... | collective-permute-start | bytes 688136 | tf_op jit(solution)/shard_map/ppermute | solution.py:13
  111.4 1.1 collective-permute-done
  112.5 0.7 copy.36
  (7 shorter events, 0.0 us)
Async XLA Ops:
  4.2 51.0 %copy-start = (bf16[1,512,7168]{2,1,0:T(8,128)(2,1)S(1)}, bf16[1,512,7168]{2,1,0:T(8,128)(2,1)}, u32[]{:S(2)}) copy-start(bf16[1,512,7168]{2,1,0:T(8,128)(2,1)} %param.8) | copy-start | bytes 22020100
  7.0 50.7 %slice-start = ((s8[7340032]{0:T(1024)(128)(4,1)}), s8[4194304]{0:T(1024)(128)(4,1)S(1)}, s32[]{:S(2)}) async-start(s8[7340032]{0:T(1024)(128)(4,1)} %bitcast.41), calls=%async_computation.2 | async-start | bytes 8388608
  55.2 2.6 %slice-start.1 = ((s8[7340032]{0:T(1024)(128)(4,1)}), s8[3145728]{0:T(1024)(128)(4,1)S(1)}, s32[]{:S(2)}) async-start(s8[7340032]{0:T(1024)(128)(4,1)} %bitcast.41), calls=%async_computation.3 | async-start | bytes 6291456
  61.2 5.2 %copy-start.2 = (s32[1,16,2]{1,2,0:T(2,128)S(1)}, s32[1,16,2]{1,2,0:T(2,128)}, u32[]{:S(2)}) copy-start(s32[1,16,2]{1,2,0:T(2,128)} %param.10) | copy-start | bytes 388
  61.2 5.2 %copy-start.3 = (f32[1,16,2]{1,2,0:T(2,128)S(1)}, f32[1,16,2]{1,2,0:T(2,128)}, u32[]{:S(2)}) copy-start(f32[1,16,2]{1,2,0:T(2,128)} %param.11) | copy-start | bytes 388
  61.2 47.8 %all-to-all-start.1 = ((bf16[8,16,7168]{2,0,1:T(8,128)(2,1)}), bf16[8,16,7168]{2,0,1:T(8,128)(2,1)S(1)}, u32[]{:S(2)}, u32[]{:S(2)}) async-start(bf16[8,16,7168]{2,0,1:T(8,128)(2,1)} %copy.30), calls=%async_computation.1 | async-start | bytes 3670016 | tf_op jit(solution)/shard_map/all_to_all | solution.py:49
  66.4 43.0 %copy-start.1 = (bf16[1,16,7168]{2,1,0:T(8,128)(2,1)S(1)}, bf16[1,16,7168]{2,1,0:T(8,128)(2,1)}, u32[]{:S(2)}) copy-start(bf16[1,16,7168]{2,1,0:T(8,128)(2,1)} %param.6) | copy-start | bytes 688132
  109.8 2.6 %collective-permute-start = (bf16[16,7168]{1,0:T(8,128)(2,1)S(1)}, bf16[16,7168]{1,0:T(8,128)(2,1)S(1)}, u32[]{:S(2)}, u32[]{:S(2)}) collective-permute-start(bf16[16,7168]{1,0:T(8,128)(2,1)S(1)} %fusion.2), channel_id=1, source_target_pairs={{0,16},{16,0},{1,17},{17,1},{2,18},{18,2},{3,19},{19,3},{4,20},{20... | collective-permute-start | bytes 688136 | tf_op jit(solution)/shard_map/ppermute | solution.py:13

commit v9 on v8

--- a/solution.py
+++ b/solution.py
@@ -35,23 +35,22 @@
     before = jnp.dot(earlier, named, preferred_element_type=jnp.int32)
     rank = jnp.sum(jnp.where(chosen, before[:, None, :], 0), axis=2)
     slot = jnp.arange(members * SLOTS)
-    slot_device = slot % members
-    slot_rank = slot // members
+    slot_device = slot // SLOTS
+    slot_rank = slot % SLOTS
     slot_expert = slot_device // per_group
     hits = (routes[None, :, :] == slot_expert[:, None, None]) & (rank[None, :, :] == slot_rank[:, None, None])
     picker = jnp.any(hits, axis=2).astype(jnp.bfloat16)
     outgoing = jnp.dot(picker, normed, preferred_element_type=jnp.float32).astype(jnp.bfloat16)
-    outgoing = outgoing.reshape(SLOTS, members, width)
-    incoming = lax.all_to_all(outgoing, "expert", split_axis=1, concat_axis=1, tiled=True)
-    inner = jnp.einsum("psd,fd->psf", incoming, up_block, preferred_element_type=jnp.float32)
-    active = jax.nn.silu(inner).astype(jnp.bfloat16)
-    partial = jnp.einsum("psf,fd->psd", active, down_block, preferred_element_type=jnp.float32).astype(jnp.bfloat16)
-    returned = lax.all_to_all(partial, "expert", split_axis=1, concat_axis=1, tiled=True)
-    combine = jnp.sum(jnp.where(hits, weights[None, :, :], 0.0), axis=2).T.reshape(rows_here, SLOTS, members)
+    incoming = lax.all_to_all(outgoing, "expert", split_axis=0, concat_axis=0, tiled=True)
+    inner = jnp.dot(incoming, up_block.T, preferred_element_type=jnp.float32)
+    active = lax.optimization_barrier(jax.nn.silu(inner).astype(jnp.bfloat16))
+    partial = jnp.dot(active, down_block, preferred_element_type=jnp.float32).astype(jnp.bfloat16)
+    returned = lax.all_to_all(partial, "expert", split_axis=0, concat_axis=0, tiled=True)
+    combine = jnp.sum(jnp.where(hits, weights[None, :, :], 0.0), axis=2).T
     combine_hi = combine.astype(jnp.bfloat16)
     combine_lo = (combine - combine_hi.astype(jnp.float32)).astype(jnp.bfloat16)
-    mixture = jnp.einsum("rps,psd->rd", combine_hi, returned, preferred_element_type=jnp.float32)
-    mixture = mixture + jnp.einsum("rps,psd->rd", combine_lo, returned, preferred_element_type=jnp.float32)
+    mixture = jnp.einsum("rj,jd->rd", combine_hi, returned, preferred_element_type=jnp.float32)
+    mixture = mixture + jnp.einsum("rj,jd->rd", combine_lo, returned, preferred_element_type=jnp.float32)
     section_out = (tokens.astype(jnp.float32) + mixture).astype(jnp.bfloat16)
     handed = passed_along(section_out, "segment", 1)
     return handed[None]

time: 113 us -> 114 us (level)
  matrix products: 6.4 us -> 10.8 us
  local copies, waits for them, and re-layouts: 4.3 us -> 0.71 us
    dot_general x4, matrix products: 4.49 us -> 8.94 us  [the longest x1 5.85 us: shards(): inner = jnp.dot(incoming, up_block.T, preferred_element_type=jnp.float32)]
    convert_element_type x3 -> x0, local copies, waits for them, and re-layouts: 2.49 us -> none  [the longest x1 2.27 us: shards(): jnp.einsum('psf,fd->psd', active, down_block, preferred_element_type=jnp....]
where the time goes in v9:
time: 114 us
  blocking collectives  47.9 us (42%)
  waiting for transfers between devices  43.6 us (38%)
  matrix products  10.8 us (9%)
  starting transfers between devices  6.71 us (6%)
  other arithmetic  4.13 us (4%)
    all_to_all x1, blocking collectives, shards(): lax.all_to_all(outgoing, 'expert', split_axis=0, concat_axis=0, tiled=True)  47.9 us
    all_to_all x1, waiting for transfers between devices, shards(): lax.all_to_all(partial, 'expert', split_axis=0, concat_axis=0, tiled=True)  42.5 us
    dot_general x1, matrix products, shards(): inner = jnp.dot(incoming, up_block.T, preferred_element_type=jnp.float32)  5.85 us
    all_to_all x1, starting transfers between devices, shards(): lax.all_to_all(partial, 'expert', split_axis=0, concat_axis=0, tiled=True)  5.18 us
    dot_general x1, matrix products, shards(): jnp.dot(active, down_block, preferred_element_type=jnp.float32)  2.38 us
  transfers between devices with their start and end apart: 2, of which 2 were waited for; matrix products, arithmetic and copies ran while one was open for 0% of the time, Pallas kernels for 0%

profile of v9, /device:TPU:13, one launch (start us, length us, event | category | flops | bytes accessed | tf_op | source)
XLA Modules:
  0.0 114.0 jit_solution(12258804305989815306)
XLA Ops:
  0.0 0.7 convert_reduce_fusion
  0.7 0.1 fusion.24
  0.8 0.7 select_reduce_fusion.1
  1.5 0.8 mul.32
  2.3 1.1 fusion.11
  3.4 0.8 fusion.22
  4.2 0.0 slice-start
  4.2 1.8 %fusion.1 = bf16[16,8,7168]{2,1,0:T(8,128)(2,1)S(1)} fusion(pred[128,16]{0,1:T(8,128)(4,1)S(1)} %fusion.22, bf16[1,16,7168]{2,1,0:T(8,128)(2,1)} %param.6, f32[7168]{0:T(1024)S(1)} %bitcast.59, f32[16]{0:T(128)S(1)} %add_rsqrt_fusion), kind=kOutput, calls=%fused_computation.3 | convolution fusion | flops 30736384 | bytes 2095168 | tf_op jit(solution)/shard_map/dot_general | solution.py:43
  6.0 47.9 %all_to_all.24 = bf16[16,8,7168]{2,1,0:T(8,128)(2,1)S(1)} all-to-all(bf16[16,8,7168]{2,1,0:T(8,128)(2,1)S(1)} %fusion.1), channel_id=1, replica_groups=mesh['segment'=2,'expert'=16] {'expert'}, dimensions={0} | all-to-all | bytes 3670016 | tf_op jit(solution)/shard_map/all_to_all | solution.py:44
  53.9 0.0 slice-start.1
  53.9 5.8 %multiply_convert_fusion = bf16[128,512]{1,0:T(8,128)(2,1)S(1)} fusion(bf16[1,512,7168]{2,1,0:T(8,128)(2,1)} %param.8, bf16[16,8,7168]{2,1,0:T(8,128)(2,1)S(1)} %all_to_all.24), kind=kOutput, calls=%fused_computation.19 | convolution fusion | flops 939851776 | bytes 9306112 | tf_op jit(solution)/shard_map/dot_general | solution.py:45
  59.7 0.0 slice-done
  59.8 0.0 slice-done.1
  59.8 2.4 %fusion = bf16[16,8,7168]{2,1,0:T(8,128)(2,1)} fusion(bf16[128,512]{1,0:T(8,128)(2,1)S(1)} %multiply_convert_fusion, bf16[1,512,7168]{2,1,0:T(8,128)(2,1)S(1)} %bitcast.57), kind=kOutput, calls=%fused_computation.2 | convolution fusion | flops 940441600 | bytes 9306112 | tf_op jit(solution)/shard_map/dot_general | solution.py:47
  62.2 0.0 copy-start.1
  62.2 0.0 copy-start.2
  62.2 5.2 %all-to-all-start.1 = ((bf16[16,8,7168]{2,1,0:T(8,128)(2,1)}), bf16[16,8,7168]{2,1,0:T(8,128)(2,1)S(1)}, u32[]{:S(2)}, u32[]{:S(2)}) async-start(bf16[16,8,7168]{2,1,0:T(8,128)(2,1)} %fusion), calls=%async_computation.1 | async-start | bytes 3670016 | tf_op jit(solution)/shard_map/all_to_all | solution.py:48
  67.3 0.0 copy-start
  67.4 0.0 copy-done.1
  67.4 0.0 copy-done.2
  67.4 0.1 select_reduce_fusion
  67.5 42.5 %all-to-all-done.1 = bf16[16,8,7168]{2,1,0:T(8,128)(2,1)S(1)} async-done(((bf16[16,8,7168]{2,1,0:T(8,128)(2,1)}), bf16[16,8,7168]{2,1,0:T(8,128)(2,1)S(1)}, u32[]{:S(2)}, u32[]{:S(2)}) %all-to-all-start.1) | async-done | bytes 1835040 | tf_op jit(solution)/shard_map/all_to_all | solution.py:48
  110.0 0.4 fusion.8
  110.3 0.0 copy-done
  110.3 0.4 fusion.3
  110.7 1.5 %collective-permute-start = (bf16[16,7168]{1,0:T(8,128)(2,1)S(1)}, bf16[16,7168]{1,0:T(8,128)(2,1)S(1)}, u32[]{:S(2)}, u32[]{:S(2)}) collective-permute-start(bf16[16,7168]{1,0:T(8,128)(2,1)S(1)} %fusion.3), channel_id=1, source_target_pairs={{0,16},{16,0},{1,17},{17,1},{2,18},{18,2},{3,19},{19,3},{4,20},{20... | collective-permute-start | bytes 688136 | tf_op jit(solution)/shard_map/ppermute | solution.py:13
  112.2 1.1 collective-permute-done
  113.3 0.7 copy.12
  (3 shorter events, 0.0 us)
Async XLA Ops:
  4.2 55.5 %slice-start = ((s8[7340032]{0:T(1024)(128)(4,1)}), s8[4194304]{0:T(1024)(128)(4,1)S(1)}, s32[]{:S(2)}) async-start(s8[7340032]{0:T(1024)(128)(4,1)} %bitcast.56), calls=%async_computation.2 | async-start | bytes 8388608
  53.9 5.9 %slice-start.1 = ((s8[7340032]{0:T(1024)(128)(4,1)}), s8[3145728]{0:T(1024)(128)(4,1)S(1)}, s32[]{:S(2)}) async-start(s8[7340032]{0:T(1024)(128)(4,1)} %bitcast.56), calls=%async_computation.3 | async-start | bytes 6291456
  62.2 5.2 %copy-start.1 = (s32[1,16,2]{1,2,0:T(2,128)S(1)}, s32[1,16,2]{1,2,0:T(2,128)}, u32[]{:S(2)}) copy-start(s32[1,16,2]{1,2,0:T(2,128)} %param.10) | copy-start | bytes 388
  62.2 5.2 %copy-start.2 = (f32[1,16,2]{1,2,0:T(2,128)S(1)}, f32[1,16,2]{1,2,0:T(2,128)}, u32[]{:S(2)}) copy-start(f32[1,16,2]{1,2,0:T(2,128)} %param.11) | copy-start | bytes 388
  62.2 47.8 %all-to-all-start.1 = ((bf16[16,8,7168]{2,1,0:T(8,128)(2,1)}), bf16[16,8,7168]{2,1,0:T(8,128)(2,1)S(1)}, u32[]{:S(2)}, u32[]{:S(2)}) async-start(bf16[16,8,7168]{2,1,0:T(8,128)(2,1)} %fusion), calls=%async_computation.1 | async-start | bytes 3670016 | tf_op jit(solution)/shard_map/all_to_all | solution.py:48
  67.3 43.0 %copy-start = (bf16[1,16,7168]{2,1,0:T(8,128)(2,1)S(1)}, bf16[1,16,7168]{2,1,0:T(8,128)(2,1)}, u32[]{:S(2)}) copy-start(bf16[1,16,7168]{2,1,0:T(8,128)(2,1)} %param.6) | copy-start | bytes 688132
  110.7 2.6 %collective-permute-start = (bf16[16,7168]{1,0:T(8,128)(2,1)S(1)}, bf16[16,7168]{1,0:T(8,128)(2,1)S(1)}, u32[]{:S(2)}, u32[]{:S(2)}) collective-permute-start(bf16[16,7168]{1,0:T(8,128)(2,1)S(1)} %fusion.3), channel_id=1, source_target_pairs={{0,16},{16,0},{1,17},{17,1},{2,18},{18,2},{3,19},{19,3},{4,20},{20... | collective-permute-start | bytes 688136 | tf_op jit(solution)/shard_map/ppermute | solution.py:13

commit v10 on v9

--- a/solution.py
+++ b/solution.py
@@ -2,15 +2,69 @@
 import jax.numpy as jnp
 from jax import lax
 from jax.sharding import PartitionSpec as P
+from jax.experimental import pallas as pl
+from jax.experimental.pallas import tpu as pltpu
 
 EXPERTS = 8
 CAP = 7
 SLOTS = 8
+CHUNK = 1024
 
 
 def passed_along(shard, axis, by):
     count = lax.axis_size(axis)
     return lax.ppermute(shard, axis, [(i, (i + by) % count) for i in range(count)])
+
+
+def up_kernel(rows_ref, weights_ref, out_ref, total_ref):
+    step = pl.program_id(0)
+
+    @pl.when(step == 0)
+    def _():
+        total_ref[...] = jnp.zeros_like(total_ref)
+
+    total_ref[...] += lax.dot_general(
+        rows_ref[...], weights_ref[...], (((1,), (1,)), ((), ())), preferred_element_type=jnp.float32
+    )
+
+    @pl.when(step == pl.num_programs(0) - 1)
+    def _():
+        out_ref[...] = jax.nn.silu(total_ref[...]).astype(out_ref.dtype)
+
+
+def up_projection(rows, weights):
+    count, width = rows.shape
+    units = weights.shape[0]
+    return pl.pallas_call(
+        up_kernel,
+        grid=(width // CHUNK,),
+        in_specs=[
+            pl.BlockSpec((count, CHUNK), lambda k: (0, k)),
+            pl.BlockSpec((units, CHUNK), lambda k: (0, k)),
+        ],
+        out_specs=pl.BlockSpec((count, units), lambda k: (0, 0)),
+        out_shape=jax.ShapeDtypeStruct((count, units), rows.dtype),
+        scratch_shapes=[pltpu.VMEM((count, units), jnp.float32)],
+    )(rows, weights)
+
+
+def down_kernel(active_ref, weights_ref, out_ref):
+    out_ref[...] = jnp.dot(active_ref[...], weights_ref[...], preferred_element_type=jnp.float32).astype(out_ref.dtype)
+
+
+def down_projection(active, weights):
+    count, units = active.shape
+    width = weights.shape[1]
+    return pl.pallas_call(
+        down_kernel,
+        grid=(width // CHUNK,),
+        in_specs=[
+            pl.BlockSpec((count, units), lambda n: (0, 0)),
+            pl.BlockSpec((units, CHUNK), lambda n: (0, n)),
+        ],
+        out_specs=pl.BlockSpec((count, CHUNK), lambda n: (0, n)),
+        out_shape=jax.ShapeDtypeStruct((count, width), active.dtype),
+    )(active, weights)
 
 
 def shards(hidden_in, norm_gain, up_proj, down_proj, expert_ids, gate_weights):
@@ -42,9 +96,8 @@
     picker = jnp.any(hits, axis=2).astype(jnp.bfloat16)
     outgoing = jnp.dot(picker, normed, preferred_element_type=jnp.float32).astype(jnp.bfloat16)
     incoming = lax.all_to_all(outgoing, "expert", split_axis=0, concat_axis=0, tiled=True)
-    inner = jnp.dot(incoming, up_block.T, preferred_element_type=jnp.float32)
-    active = lax.optimization_barrier(jax.nn.silu(inner).astype(jnp.bfloat16))
-    partial = jnp.dot(active, down_block, preferred_element_type=jnp.float32).astype(jnp.bfloat16)
+    active = up_projection(incoming, up_block)
+    partial = down_projection(active, down_block)
     returned = lax.all_to_all(partial, "expert", split_axis=0, concat_axis=0, tiled=True)
     combine = jnp.sum(jnp.where(hits, weights[None, :, :], 0.0), axis=2).T
     combine_hi = combine.astype(jnp.bfloat16)

time: 114 us -> 122 us (1.070)
  Pallas kernels: 0 us -> 15.4 us
  matrix products: 10.8 us -> 2.47 us
    pallas_call x0 -> x2, Pallas kernels: none -> 15.4 us  [the longest x1 7.98 us: up_projection(): pl.pallas_call(up_kernel, grid=(width // CHUNK,), in_specs=[pl.BlockSpec(...]
    dot_general x2 -> x0, matrix products: 8.23 us -> none  [the longest x1 5.85 us: shards(): inner = jnp.dot(incoming, up_block.T, preferred_element_type=jnp.float32)]
where the time goes in v10:
time: 122 us; the launch traced here: 121 us
  blocking collectives  48 us (39%)
  waiting for transfers between devices  43.6 us (36%)
  Pallas kernels  15.4 us (13%)
  starting transfers between devices  6.7 us (5%)
  other arithmetic  4.13 us (3%)
  matrix products  2.47 us (2%)
    all_to_all x1, blocking collectives, shards(): lax.all_to_all(outgoing, 'expert', split_axis=0, concat_axis=0, tiled=True)  48 us
    all_to_all x1, waiting for transfers between devices, shards(): lax.all_to_all(partial, 'expert', split_axis=0, concat_axis=0, tiled=True)  42.5 us
    pallas_call x1, Pallas kernels, up_projection(): pl.pallas_call(up_kernel, grid=(width // CHUNK,), in_specs=[pl.BlockSpec(...  7.98 us
    pallas_call x1, Pallas kernels, down_projection(): pl.pallas_call(down_kernel, grid=(width // CHUNK,), in_specs=[pl.BlockSpe...  7.43 us
    all_to_all x1, starting transfers between devices, shards(): lax.all_to_all(partial, 'expert', split_axis=0, concat_axis=0, tiled=True)  5.18 us
  transfers between devices with their start and end apart: 2, of which 2 were waited for; matrix products, arithmetic and copies ran while one was open for 0% of the time, Pallas kernels for 0%

profile of v10, /device:TPU:13, one launch (start us, length us, event | category | flops | bytes accessed | tf_op | source)
XLA Modules:
  0.0 121.1 jit_solution(7763705988503744506)
XLA Ops:
  0.0 0.7 convert_reduce_fusion
  0.7 0.1 fusion.15
  0.8 0.7 select_reduce_fusion.1
  1.5 0.8 mul.27
  2.3 1.1 fusion.6
  3.4 0.8 fusion.13
  4.2 1.6 %fusion = bf16[16,8,7168]{2,1,0:T(8,128)(2,1)S(1)} fusion(pred[128,16]{0,1:T(8,128)(4,1)S(1)} %fusion.13, bf16[1,16,7168]{2,1,0:T(8,128)(2,1)} %param.6, f32[7168]{0:T(1024)S(1)} %bitcast.49, f32[16]{0:T(128)S(1)} %add_rsqrt_fusion), kind=kOutput, calls=%fused_computation.1 | convolution fusion | flops 30736384 | bytes 2095168 | tf_op jit(solution)/shard_map/dot_general | solution.py:97
  5.8 48.0 %all_to_all.23 = bf16[16,8,7168]{2,1,0:T(8,128)(2,1)} all-to-all(bf16[16,8,7168]{2,1,0:T(8,128)(2,1)S(1)} %fusion), channel_id=1, replica_groups=mesh['segment'=2,'expert'=16] {'expert'}, dimensions={0} | all-to-all | bytes 3670016 | tf_op jit(solution)/shard_map/all_to_all | solution.py:98
  53.8 8.0 %shard_map.64.active_ref = bf16[128,512]{1,0:T(8,128)(2,1)} custom-call(bf16[128,7168]{1,0:T(8,128)(2,1)} %bitcast.47, bf16[512,7168]{1,0:T(8,128)(2,1)} %bitcast.44), custom_call_target="tpu_custom_call" | custom-call | tf_op jit(solution)/shard_map/pallas_call | solution.py:38
  61.8 7.4 %shard_map.65 = bf16[128,7168]{1,0:T(8,128)(2,1)} custom-call(bf16[128,512]{1,0:T(8,128)(2,1)} %shard_map.64.active_ref, bf16[512,7168]{1,0:T(8,128)(2,1)} %bitcast.45), custom_call_target="tpu_custom_call" | custom-call | tf_op jit(solution)/shard_map/pallas_call | solution.py:58
  69.2 0.0 copy-start.1
  69.2 0.0 copy-start.2
  69.2 5.2 %all-to-all-start.1 = ((bf16[16,8,7168]{2,1,0:T(8,128)(2,1)}), bf16[16,8,7168]{2,1,0:T(8,128)(2,1)S(1)}, u32[]{:S(2)}, u32[]{:S(2)}) async-start(bf16[16,8,7168]{2,1,0:T(8,128)(2,1)} %bitcast.46), calls=%async_computation.1 | async-start | bytes 3670016 | tf_op jit(solution)/shard_map/all_to_all | solution.py:101
  74.4 0.0 copy-start
  74.4 0.0 copy-done.1
  74.4 0.0 copy-done.2
  74.4 0.1 select_reduce_fusion
  74.5 42.5 %all-to-all-done.1 = bf16[16,8,7168]{2,1,0:T(8,128)(2,1)S(1)} async-done(((bf16[16,8,7168]{2,1,0:T(8,128)(2,1)}), bf16[16,8,7168]{2,1,0:T(8,128)(2,1)S(1)}, u32[]{:S(2)}, u32[]{:S(2)}) %all-to-all-start.1) | async-done | bytes 1835040 | tf_op jit(solution)/shard_map/all_to_all | solution.py:101
  117.1 0.4 fusion.4
  117.4 0.0 copy-done
  117.4 0.4 fusion.2
  117.8 1.5 %collective-permute-start = (bf16[16,7168]{1,0:T(8,128)(2,1)S(1)}, bf16[16,7168]{1,0:T(8,128)(2,1)S(1)}, u32[]{:S(2)}, u32[]{:S(2)}) collective-permute-start(bf16[16,7168]{1,0:T(8,128)(2,1)S(1)} %fusion.2), channel_id=1, source_target_pairs={{0,16},{16,0},{1,17},{17,1},{2,18},{18,2},{3,19},{19,3},{4,20},{20... | collective-permute-start | bytes 688136 | tf_op jit(solution)/shard_map/ppermute | solution.py:16
  119.3 1.1 collective-permute-done
  120.4 0.7 copy.12
  (2 shorter events, 0.0 us)
Async XLA Ops:
  69.2 5.2 %copy-start.1 = (s32[1,16,2]{1,2,0:T(2,128)S(1)}, s32[1,16,2]{1,2,0:T(2,128)}, u32[]{:S(2)}) copy-start(s32[1,16,2]{1,2,0:T(2,128)} %param.10) | copy-start | bytes 388
  69.2 5.2 %copy-start.2 = (f32[1,16,2]{1,2,0:T(2,128)S(1)}, f32[1,16,2]{1,2,0:T(2,128)}, u32[]{:S(2)}) copy-start(f32[1,16,2]{1,2,0:T(2,128)} %param.11) | copy-start | bytes 388
  69.2 47.8 %all-to-all-start.1 = ((bf16[16,8,7168]{2,1,0:T(8,128)(2,1)}), bf16[16,8,7168]{2,1,0:T(8,128)(2,1)S(1)}, u32[]{:S(2)}, u32[]{:S(2)}) async-start(bf16[16,8,7168]{2,1,0:T(8,128)(2,1)} %bitcast.46), calls=%async_computation.1 | async-start | bytes 3670016 | tf_op jit(solution)/shard_map/all_to_all | solution.py:101
  74.4 43.0 %copy-start = (bf16[1,16,7168]{2,1,0:T(8,128)(2,1)S(1)}, bf16[1,16,7168]{2,1,0:T(8,128)(2,1)}, u32[]{:S(2)}) copy-start(bf16[1,16,7168]{2,1,0:T(8,128)(2,1)} %param.6) | copy-start | bytes 688132
  117.8 2.6 %collective-permute-start = (bf16[16,7168]{1,0:T(8,128)(2,1)S(1)}, bf16[16,7168]{1,0:T(8,128)(2,1)S(1)}, u32[]{:S(2)}, u32[]{:S(2)}) collective-permute-start(bf16[16,7168]{1,0:T(8,128)(2,1)S(1)} %fusion.2), channel_id=1, source_target_pairs={{0,16},{16,0},{1,17},{17,1},{2,18},{18,2},{3,19},{19,3},{4,20},{20... | collective-permute-start | bytes 688136 | tf_op jit(solution)/shard_map/ppermute | solution.py:16

commit v11 on v10

--- a/solution.py
+++ b/solution.py
@@ -8,7 +8,7 @@
 EXPERTS = 8
 CAP = 7
 SLOTS = 8
-CHUNK = 1024
+CHUNK = 3584
 
 
 def passed_along(shard, axis, by):

time: 122 us -> 117 us (0.959)
  Pallas kernels: 15.4 us -> 10.5 us
    pallas_call x1, Pallas kernels: 7.43 us -> 4.79 us  [down_projection(): pl.pallas_call(down_kernel, grid=(width // CHUNK,), in_specs=[pl.BlockSpe...]
    pallas_call x1, Pallas kernels: 7.98 us -> 5.7 us  [up_projection(): pl.pallas_call(up_kernel, grid=(width // CHUNK,), in_specs=[pl.BlockSpec(...]
where the time goes in v11:
time: 117 us; the launch traced here: 116 us
  blocking collectives  48 us (41%)
  waiting for transfers between devices  43.6 us (37%)
  Pallas kernels  10.5 us (9%)
  starting transfers between devices  6.69 us (6%)
  other arithmetic  4.13 us (4%)
  matrix products  2.47 us (2%)
    all_to_all x1, blocking collectives, shards(): lax.all_to_all(outgoing, 'expert', split_axis=0, concat_axis=0, tiled=True)  48 us
    all_to_all x1, waiting for transfers between devices, shards(): lax.all_to_all(partial, 'expert', split_axis=0, concat_axis=0, tiled=True)  42.5 us
    pallas_call x1, Pallas kernels, up_projection(): pl.pallas_call(up_kernel, grid=(width // CHUNK,), in_specs=[pl.BlockSpec(...  5.7 us
    all_to_all x1, starting transfers between devices, shards(): lax.all_to_all(partial, 'expert', split_axis=0, concat_axis=0, tiled=True)  5.17 us
    pallas_call x1, Pallas kernels, down_projection(): pl.pallas_call(down_kernel, grid=(width // CHUNK,), in_specs=[pl.BlockSpe...  4.79 us
  transfers between devices with their start and end apart: 2, of which 2 were waited for; matrix products, arithmetic and copies ran while one was open for 0% of the time, Pallas kernels for 0%

profile of v11, /device:TPU:13, one launch (start us, length us, event | category | flops | bytes accessed | tf_op | source)
XLA Modules:
  0.0 116.2 jit_solution(8032812507102809766)
XLA Ops:
  0.0 0.7 convert_reduce_fusion
  0.7 0.1 fusion.15
  0.8 0.7 select_reduce_fusion.1
  1.5 0.8 mul.27
  2.3 1.1 fusion.6
  3.4 0.8 fusion.13
  4.2 1.6 %fusion = bf16[16,8,7168]{2,1,0:T(8,128)(2,1)S(1)} fusion(pred[128,16]{0,1:T(8,128)(4,1)S(1)} %fusion.13, bf16[1,16,7168]{2,1,0:T(8,128)(2,1)} %param.6, f32[7168]{0:T(1024)S(1)} %bitcast.49, f32[16]{0:T(128)S(1)} %add_rsqrt_fusion), kind=kOutput, calls=%fused_computation.1 | convolution fusion | flops 30736384 | bytes 2095168 | tf_op jit(solution)/shard_map/dot_general | solution.py:97
  5.8 48.0 %all_to_all.23 = bf16[16,8,7168]{2,1,0:T(8,128)(2,1)} all-to-all(bf16[16,8,7168]{2,1,0:T(8,128)(2,1)S(1)} %fusion), channel_id=1, replica_groups=mesh['segment'=2,'expert'=16] {'expert'}, dimensions={0} | all-to-all | bytes 3670016 | tf_op jit(solution)/shard_map/all_to_all | solution.py:98
  53.8 5.7 %shard_map.64.active_ref = bf16[128,512]{1,0:T(8,128)(2,1)} custom-call(bf16[128,7168]{1,0:T(8,128)(2,1)} %bitcast.47, bf16[512,7168]{1,0:T(8,128)(2,1)} %bitcast.44), custom_call_target="tpu_custom_call" | custom-call | tf_op jit(solution)/shard_map/pallas_call | solution.py:38
  59.5 4.8 %shard_map.65 = bf16[128,7168]{1,0:T(8,128)(2,1)} custom-call(bf16[128,512]{1,0:T(8,128)(2,1)} %shard_map.64.active_ref, bf16[512,7168]{1,0:T(8,128)(2,1)} %bitcast.45), custom_call_target="tpu_custom_call" | custom-call | tf_op jit(solution)/shard_map/pallas_call | solution.py:58
  64.3 0.0 copy-start.1
  64.3 0.0 copy-start.2
  64.3 5.2 %all-to-all-start.1 = ((bf16[16,8,7168]{2,1,0:T(8,128)(2,1)}), bf16[16,8,7168]{2,1,0:T(8,128)(2,1)S(1)}, u32[]{:S(2)}, u32[]{:S(2)}) async-start(bf16[16,8,7168]{2,1,0:T(8,128)(2,1)} %bitcast.46), calls=%async_computation.1 | async-start | bytes 3670016 | tf_op jit(solution)/shard_map/all_to_all | solution.py:101
  69.5 0.0 copy-start
  69.5 0.0 copy-done.1
  69.5 0.0 copy-done.2
  69.5 0.1 select_reduce_fusion
  69.6 42.5 %all-to-all-done.1 = bf16[16,8,7168]{2,1,0:T(8,128)(2,1)S(1)} async-done(((bf16[16,8,7168]{2,1,0:T(8,128)(2,1)}), bf16[16,8,7168]{2,1,0:T(8,128)(2,1)S(1)}, u32[]{:S(2)}, u32[]{:S(2)}) %all-to-all-start.1) | async-done | bytes 1835040 | tf_op jit(solution)/shard_map/all_to_all | solution.py:101
  112.1 0.4 fusion.4
  112.5 0.0 copy-done
  112.5 0.4 fusion.2
  112.9 1.5 %collective-permute-start = (bf16[16,7168]{1,0:T(8,128)(2,1)S(1)}, bf16[16,7168]{1,0:T(8,128)(2,1)S(1)}, u32[]{:S(2)}, u32[]{:S(2)}) collective-permute-start(bf16[16,7168]{1,0:T(8,128)(2,1)S(1)} %fusion.2), channel_id=1, source_target_pairs={{0,16},{16,0},{1,17},{17,1},{2,18},{18,2},{3,19},{19,3},{4,20},{20... | collective-permute-start | bytes 688136 | tf_op jit(solution)/shard_map/ppermute | solution.py:16
  114.4 1.1 collective-permute-done
  115.5 0.7 copy.12
  (2 shorter events, 0.0 us)
Async XLA Ops:
  64.3 5.2 %copy-start.1 = (s32[1,16,2]{1,2,0:T(2,128)S(1)}, s32[1,16,2]{1,2,0:T(2,128)}, u32[]{:S(2)}) copy-start(s32[1,16,2]{1,2,0:T(2,128)} %param.10) | copy-start | bytes 388
  64.3 5.2 %copy-start.2 = (f32[1,16,2]{1,2,0:T(2,128)S(1)}, f32[1,16,2]{1,2,0:T(2,128)}, u32[]{:S(2)}) copy-start(f32[1,16,2]{1,2,0:T(2,128)} %param.11) | copy-start | bytes 388
  64.3 47.8 %all-to-all-start.1 = ((bf16[16,8,7168]{2,1,0:T(8,128)(2,1)}), bf16[16,8,7168]{2,1,0:T(8,128)(2,1)S(1)}, u32[]{:S(2)}, u32[]{:S(2)}) async-start(bf16[16,8,7168]{2,1,0:T(8,128)(2,1)} %bitcast.46), calls=%async_computation.1 | async-start | bytes 3670016 | tf_op jit(solution)/shard_map/all_to_all | solution.py:101
  69.5 43.0 %copy-start = (bf16[1,16,7168]{2,1,0:T(8,128)(2,1)S(1)}, bf16[1,16,7168]{2,1,0:T(8,128)(2,1)}, u32[]{:S(2)}) copy-start(bf16[1,16,7168]{2,1,0:T(8,128)(2,1)} %param.6) | copy-start | bytes 688132
  112.9 2.6 %collective-permute-start = (bf16[16,7168]{1,0:T(8,128)(2,1)S(1)}, bf16[16,7168]{1,0:T(8,128)(2,1)S(1)}, u32[]{:S(2)}, u32[]{:S(2)}) collective-permute-start(bf16[16,7168]{1,0:T(8,128)(2,1)S(1)} %fusion.2), channel_id=1, source_target_pairs={{0,16},{16,0},{1,17},{17,1},{2,18},{18,2},{3,19},{19,3},{4,20},{20... | collective-permute-start | bytes 688136 | tf_op jit(solution)/shard_map/ppermute | solution.py:16

commit v12 on v8

--- a/solution.py
+++ b/solution.py
@@ -45,8 +45,10 @@
     incoming = lax.all_to_all(outgoing, "expert", split_axis=1, concat_axis=1, tiled=True)
     inner = jnp.einsum("psd,fd->psf", incoming, up_block, preferred_element_type=jnp.float32)
     active = jax.nn.silu(inner).astype(jnp.bfloat16)
-    partial = jnp.einsum("psf,fd->psd", active, down_block, preferred_element_type=jnp.float32).astype(jnp.bfloat16)
-    returned = lax.all_to_all(partial, "expert", split_axis=1, concat_axis=1, tiled=True)
+    active = lax.optimization_barrier(active.transpose(1, 0, 2).reshape(members * SLOTS, -1))
+    partial = jnp.dot(active, down_block, preferred_element_type=jnp.float32).astype(jnp.bfloat16)
+    partial = partial.reshape(members, SLOTS, width)
+    returned = lax.all_to_all(partial, "expert", split_axis=0, concat_axis=0, tiled=True).transpose(1, 0, 2)
     combine = jnp.sum(jnp.where(hits, weights[None, :, :], 0.0), axis=2).T.reshape(rows_here, SLOTS, members)
     combine_hi = combine.astype(jnp.bfloat16)
     combine_lo = (combine - combine_hi.astype(jnp.float32)).astype(jnp.bfloat16)

time: 113 us -> 112 us (level)
  local copies, waits for them, and re-layouts: 4.3 us -> 2.03 us
  matrix products: 6.4 us -> 7.65 us
    convert_element_type x1 -> x0, local copies, waits for them, and re-layouts: 2.27 us -> none  [shards(): jnp.einsum('psf,fd->psd', active, down_block, preferred_element_type=jnp....]
    dot_general x1, matrix products: 1.13 us -> 2.38 us  [shards(): jnp.dot(active, down_block, preferred_element_type=jnp.float32)]
where the time goes in v12:
time: 112 us
  blocking collectives  48.2 us (43%)
  waiting for transfers between devices  43.3 us (39%)
  matrix products  7.65 us (7%)
  starting transfers between devices  6.71 us (6%)
  other arithmetic  4.14 us (4%)
  local copies, waits for them, and re-layouts  2.03 us (2%)
    all_to_all x1, blocking collectives, shards(): lax.all_to_all(outgoing, 'expert', split_axis=1, concat_axis=1, tiled=True)  48.2 us
    all_to_all x1, waiting for transfers between devices, shards(): lax.all_to_all(partial, 'expert', split_axis=0, concat_axis=0, tiled=True)  42.2 us
    all_to_all x1, starting transfers between devices, shards(): lax.all_to_all(partial, 'expert', split_axis=0, concat_axis=0, tiled=True)  5.18 us
    dot_general x1, matrix products, shards(): jnp.einsum('psd,fd->psf', incoming, up_block, preferred_element_type=jnp....  2.55 us
    dot_general x1, matrix products, shards(): jnp.dot(active, down_block, preferred_element_type=jnp.float32)  2.38 us
  transfers between devices with their start and end apart: 2, of which 2 were waited for; matrix products, arithmetic and copies ran while one was open for 0% of the time, Pallas kernels for 0%

profile of v12, /device:TPU:13, one launch (start us, length us, event | category | flops | bytes accessed | tf_op | source)
XLA Modules:
  0.0 112.1 jit_solution(11656460788458586614)
XLA Ops:
  0.0 0.7 convert_reduce_fusion
  0.7 0.1 fusion.25
  0.8 0.7 select_reduce_fusion.1
  1.5 0.8 mul.33
  2.3 1.1 fusion.12
  3.4 0.8 fusion.24
  4.2 0.0 copy-start
  4.2 1.8 %convolution_convert_fusion.1 = bf16[128,7168]{1,0:T(8,128)(2,1)S(1)} fusion(pred[128,16]{0,1:T(8,128)(4,1)S(1)} %fusion.24, bf16[1,16,7168]{2,1,0:T(8,128)(2,1)} %param.6, f32[7168]{0:T(1024)S(1)} %bitcast.62, f32[16]{0:T(128)S(1)} %add_rsqrt_fusion), kind=kOutput, calls=%fused_computation.1 | convolution fusion | flops 30736384 | bytes 2095168 | tf_op jit(solution)/shard_map/dot_general | solution.py:43
  6.0 1.0 copy.30
  7.0 0.0 slice-start
  7.0 48.2 %all_to_all.10 = bf16[8,16,7168]{2,0,1:T(8,128)(2,1)S(1)} all-to-all(bf16[8,16,7168]{2,0,1:T(8,128)(2,1)S(1)} %copy.30), channel_id=1, replica_groups=mesh['segment'=2,'expert'=16] {'expert'}, dimensions={1} | all-to-all | bytes 3670016 | tf_op jit(solution)/shard_map/all_to_all | solution.py:45
  55.2 0.0 copy-done
  55.2 0.0 slice-start.1
  55.2 2.5 %fusion.17 = bf16[128,512]{1,0:T(8,128)(2,1)S(1)} fusion(bf16[8,16,7168]{2,0,1:T(8,128)(2,1)S(1)} %all_to_all.10, bf16[1,512,7168]{2,1,0:T(8,128)(2,1)S(1)} %copy-done), kind=kOutput, calls=%fused_computation.20 | convolution fusion | flops 939851776 | bytes 9306112 | tf_op jit(solution)/shard_map/psd,fd->psf/dot_general | solution.py:46
  57.7 0.0 slice-done
  57.8 0.0 slice-done.1
  57.8 2.4 %fusion = bf16[16,8,7168]{2,1,0:T(8,128)(2,1)} fusion(bf16[128,512]{1,0:T(8,128)(2,1)S(1)} %fusion.17, bf16[1,512,7168]{2,1,0:T(8,128)(2,1)S(1)} %bitcast.59), kind=kOutput, calls=%fused_computation.2 | convolution fusion | flops 940441600 | bytes 9306112 | tf_op jit(solution)/shard_map/dot_general | solution.py:49
  60.2 0.0 copy-start.2
  60.2 5.2 %all-to-all-start.1 = ((bf16[16,8,7168]{2,1,0:T(8,128)(2,1)}), bf16[16,8,7168]{2,1,0:T(8,128)(2,1)S(1)}, u32[]{:S(2)}, u32[]{:S(2)}) async-start(bf16[16,8,7168]{2,1,0:T(8,128)(2,1)} %fusion), calls=%async_computation.1 | async-start | bytes 3670016 | tf_op jit(solution)/shard_map/all_to_all | solution.py:51
  65.4 0.0 copy-done.2
  65.4 0.0 copy-done.3
  65.4 0.1 select_reduce_fusion
  65.5 0.1 reshape.62
  65.6 0.1 copy.32
  65.7 0.1 copy.31
  65.8 42.2 %all-to-all-done.1 = bf16[16,8,7168]{2,1,0:T(8,128)(2,1)S(1)} async-done(((bf16[16,8,7168]{2,1,0:T(8,128)(2,1)}), bf16[16,8,7168]{2,1,0:T(8,128)(2,1)S(1)}, u32[]{:S(2)}, u32[]{:S(2)}) %all-to-all-start.1) | async-done | bytes 1835040 | tf_op jit(solution)/shard_map/all_to_all | solution.py:51
  108.0 0.4 convolution_bitcast_fusion
  108.4 0.0 copy-done.1
  108.4 0.4 fusion.3
  108.8 1.5 %collective-permute-start = (bf16[16,7168]{1,0:T(8,128)(2,1)S(1)}, bf16[16,7168]{1,0:T(8,128)(2,1)S(1)}, u32[]{:S(2)}, u32[]{:S(2)}) collective-permute-start(bf16[16,7168]{1,0:T(8,128)(2,1)S(1)} %fusion.3), channel_id=1, source_target_pairs={{0,16},{16,0},{1,17},{17,1},{2,18},{18,2},{3,19},{19,3},{4,20},{20... | collective-permute-start | bytes 688136 | tf_op jit(solution)/shard_map/ppermute | solution.py:13
  110.3 1.1 collective-permute-done
  111.5 0.7 copy.34
  (6 shorter events, 0.0 us)
Async XLA Ops:
  4.2 51.0 %copy-start = (bf16[1,512,7168]{2,1,0:T(8,128)(2,1)S(1)}, bf16[1,512,7168]{2,1,0:T(8,128)(2,1)}, u32[]{:S(2)}) copy-start(bf16[1,512,7168]{2,1,0:T(8,128)(2,1)} %param.8) | copy-start | bytes 22020100
  7.0 50.7 %slice-start = ((s8[7340032]{0:T(1024)(128)(4,1)}), s8[4194304]{0:T(1024)(128)(4,1)S(1)}, s32[]{:S(2)}) async-start(s8[7340032]{0:T(1024)(128)(4,1)} %bitcast.58), calls=%async_computation.2 | async-start | bytes 8388608
  55.2 2.6 %slice-start.1 = ((s8[7340032]{0:T(1024)(128)(4,1)}), s8[3145728]{0:T(1024)(128)(4,1)S(1)}, s32[]{:S(2)}) async-start(s8[7340032]{0:T(1024)(128)(4,1)} %bitcast.58), calls=%async_computation.3 | async-start | bytes 6291456
  60.2 5.2 %copy-start.2 = (s32[1,16,2]{1,2,0:T(2,128)S(1)}, s32[1,16,2]{1,2,0:T(2,128)}, u32[]{:S(2)}) copy-start(s32[1,16,2]{1,2,0:T(2,128)} %param.10) | copy-start | bytes 388
  60.2 5.2 %copy-start.3 = (f32[1,16,2]{1,2,0:T(2,128)S(1)}, f32[1,16,2]{1,2,0:T(2,128)}, u32[]{:S(2)}) copy-start(f32[1,16,2]{1,2,0:T(2,128)} %param.11) | copy-start | bytes 388
  60.2 47.8 %all-to-all-start.1 = ((bf16[16,8,7168]{2,1,0:T(8,128)(2,1)}), bf16[16,8,7168]{2,1,0:T(8,128)(2,1)S(1)}, u32[]{:S(2)}, u32[]{:S(2)}) async-start(bf16[16,8,7168]{2,1,0:T(8,128)(2,1)} %fusion), calls=%async_computation.1 | async-start | bytes 3670016 | tf_op jit(solution)/shard_map/all_to_all | solution.py:51
  65.3 43.0 %copy-start.1 = (bf16[1,16,7168]{2,1,0:T(8,128)(2,1)S(1)}, bf16[1,16,7168]{2,1,0:T(8,128)(2,1)}, u32[]{:S(2)}) copy-start(bf16[1,16,7168]{2,1,0:T(8,128)(2,1)} %param.6) | copy-start | bytes 688132
  108.8 2.6 %collective-permute-start = (bf16[16,7168]{1,0:T(8,128)(2,1)S(1)}, bf16[16,7168]{1,0:T(8,128)(2,1)S(1)}, u32[]{:S(2)}, u32[]{:S(2)}) collective-permute-start(bf16[16,7168]{1,0:T(8,128)(2,1)S(1)} %fusion.3), channel_id=1, source_target_pairs={{0,16},{16,0},{1,17},{17,1},{2,18},{18,2},{3,19},{19,3},{4,20},{20... | collective-permute-start | bytes 688136 | tf_op jit(solution)/shard_map/ppermute | solution.py:13

commit v13 on v12

--- a/solution.py
+++ b/solution.py
@@ -33,12 +33,13 @@
     positions = jnp.arange(rows_here)
     earlier = (positions[None, :] < positions[:, None]).astype(jnp.int32)
     before = jnp.dot(earlier, named, preferred_element_type=jnp.int32)
-    rank = jnp.sum(jnp.where(chosen, before[:, None, :], 0), axis=2)
+    places = jnp.arange(EXPERTS)[None, None, :] * SLOTS + before[:, None, :]
+    key = jnp.sum(jnp.where(chosen, places, 0), axis=2)
     slot = jnp.arange(members * SLOTS)
     slot_device = slot % members
     slot_rank = slot // members
     slot_expert = slot_device // per_group
-    hits = (routes[None, :, :] == slot_expert[:, None, None]) & (rank[None, :, :] == slot_rank[:, None, None])
+    hits = key[None, :, :] == (slot_expert * SLOTS + slot_rank)[:, None, None]
     picker = jnp.any(hits, axis=2).astype(jnp.bfloat16)
     outgoing = jnp.dot(picker, normed, preferred_element_type=jnp.float32).astype(jnp.bfloat16)
     outgoing = outgoing.reshape(SLOTS, members, width)

time: 112 us -> 112 us (level)
  no operation moved by 1% of the time
where the time goes in v13:
time: 112 us; the launch traced here: 111 us
  blocking collectives  48.2 us (43%)
  waiting for transfers between devices  43.3 us (39%)
  matrix products  7.61 us (7%)
  starting transfers between devices  6.71 us (6%)
  other arithmetic  3.51 us (3%)
  local copies, waits for them, and re-layouts  2.03 us (2%)
    all_to_all x1, blocking collectives, shards(): lax.all_to_all(outgoing, 'expert', split_axis=1, concat_axis=1, tiled=True)  48.2 us
    all_to_all x1, waiting for transfers between devices, shards(): lax.all_to_all(partial, 'expert', split_axis=0, concat_axis=0, tiled=True)  42.2 us
    all_to_all x1, starting transfers between devices, shards(): lax.all_to_all(partial, 'expert', split_axis=0, concat_axis=0, tiled=True)  5.18 us
    dot_general x1, matrix products, shards(): jnp.einsum('psd,fd->psf', incoming, up_block, preferred_element_type=jnp....  2.55 us
    dot_general x1, matrix products, shards(): jnp.dot(active, down_block, preferred_element_type=jnp.float32)  2.38 us
  transfers between devices with their start and end apart: 2, of which 2 were waited for; matrix products, arithmetic and copies ran while one was open for 0% of the time, Pallas kernels for 0%

profile of v13, /device:TPU:13, one launch (start us, length us, event | category | flops | bytes accessed | tf_op | source)
XLA Modules:
  0.0 111.5 jit_solution(15314927607937047433)
XLA Ops:
  0.0 0.7 convert_reduce_fusion
  0.7 0.1 convolution_add_fusion
  0.8 0.8 select_reduce_fusion
  1.5 0.8 mul.54
  2.3 1.1 fusion.12
  3.4 0.1 compare_reduce_fusion
  3.5 0.0 copy-start
  3.5 1.8 %convolution_convert_fusion.1 = bf16[128,7168]{1,0:T(8,128)(2,1)S(1)} fusion(pred[128,16]{0,1:T(8,128)(4,1)S(1)} %compare_reduce_fusion, bf16[1,16,7168]{2,1,0:T(8,128)(2,1)} %param.6, f32[7168]{0:T(1024)S(1)} %bitcast.62, f32[16]{0:T(128)S(1)} %add_rsqrt_fusion), kind=kOutput, calls=%fused_computation.1 | convolution fusion | flops 30736384 | bytes 2095168 | tf_op jit(solution)/shard_map/dot_general | solution.py:44
  5.3 1.0 copy.27
  6.3 0.0 slice-start
  6.3 48.2 %all_to_all.10 = bf16[8,16,7168]{2,0,1:T(8,128)(2,1)S(1)} all-to-all(bf16[8,16,7168]{2,0,1:T(8,128)(2,1)S(1)} %copy.27), channel_id=1, replica_groups=mesh['segment'=2,'expert'=16] {'expert'}, dimensions={1} | all-to-all | bytes 3670016 | tf_op jit(solution)/shard_map/all_to_all | solution.py:46
  54.5 0.0 copy-done
  54.5 0.0 slice-start.1
  54.5 2.5 %fusion.17 = bf16[128,512]{1,0:T(8,128)(2,1)S(1)} fusion(bf16[8,16,7168]{2,0,1:T(8,128)(2,1)S(1)} %all_to_all.10, bf16[1,512,7168]{2,1,0:T(8,128)(2,1)S(1)} %copy-done), kind=kOutput, calls=%fused_computation.21 | convolution fusion | flops 939851776 | bytes 9306112 | tf_op jit(solution)/shard_map/psd,fd->psf/dot_general | solution.py:47
  57.1 0.0 slice-done
  57.1 0.0 slice-done.1
  57.1 2.4 %fusion = bf16[16,8,7168]{2,1,0:T(8,128)(2,1)} fusion(bf16[128,512]{1,0:T(8,128)(2,1)S(1)} %fusion.17, bf16[1,512,7168]{2,1,0:T(8,128)(2,1)S(1)} %bitcast.59), kind=kOutput, calls=%fused_computation.2 | convolution fusion | flops 940441600 | bytes 9306112 | tf_op jit(solution)/shard_map/dot_general | solution.py:50
  59.5 0.0 copy-start.2
  59.5 5.2 %all-to-all-start.1 = ((bf16[16,8,7168]{2,1,0:T(8,128)(2,1)}), bf16[16,8,7168]{2,1,0:T(8,128)(2,1)S(1)}, u32[]{:S(2)}, u32[]{:S(2)}) async-start(bf16[16,8,7168]{2,1,0:T(8,128)(2,1)} %fusion), calls=%async_computation.1 | async-start | bytes 3670016 | tf_op jit(solution)/shard_map/all_to_all | solution.py:52
  64.7 0.0 copy-start.1
  64.7 0.0 copy-done.2
  64.7 0.1 fusion.24
  64.8 0.1 reshape.70
  64.9 0.1 copy.29
  65.0 0.1 copy.28
  65.1 42.2 %all-to-all-done.1 = bf16[16,8,7168]{2,1,0:T(8,128)(2,1)S(1)} async-done(((bf16[16,8,7168]{2,1,0:T(8,128)(2,1)}), bf16[16,8,7168]{2,1,0:T(8,128)(2,1)S(1)}, u32[]{:S(2)}, u32[]{:S(2)}) %all-to-all-start.1) | async-done | bytes 1835040 | tf_op jit(solution)/shard_map/all_to_all | solution.py:52
  107.3 0.4 convolution_bitcast_fusion
  107.7 0.0 copy-done.1
  107.7 0.4 fusion.3
  108.1 1.5 %collective-permute-start = (bf16[16,7168]{1,0:T(8,128)(2,1)S(1)}, bf16[16,7168]{1,0:T(8,128)(2,1)S(1)}, u32[]{:S(2)}, u32[]{:S(2)}) collective-permute-start(bf16[16,7168]{1,0:T(8,128)(2,1)S(1)} %fusion.3), channel_id=1, source_target_pairs={{0,16},{16,0},{1,17},{17,1},{2,18},{18,2},{3,19},{19,3},{4,20},{20... | collective-permute-start | bytes 688136 | tf_op jit(solution)/shard_map/ppermute | solution.py:13
  109.7 1.1 %collective-permute-done = bf16[16,7168]{1,0:T(8,128)(2,1)S(1)} collective-permute-done((bf16[16,7168]{1,0:T(8,128)(2,1)S(1)}, bf16[16,7168]{1,0:T(8,128)(2,1)S(1)}, u32[]{:S(2)}, u32[]{:S(2)}) %collective-permute-start) | collective-permute-done | bytes 229408 | tf_op jit(solution)/shard_map/ppermute | solution.py:13
  110.8 0.7 copy.31
  (5 shorter events, 0.0 us)
Async XLA Ops:
  3.5 51.0 %copy-start = (bf16[1,512,7168]{2,1,0:T(8,128)(2,1)S(1)}, bf16[1,512,7168]{2,1,0:T(8,128)(2,1)}, u32[]{:S(2)}) copy-start(bf16[1,512,7168]{2,1,0:T(8,128)(2,1)} %param.8) | copy-start | bytes 22020100
  6.3 50.7 %slice-start = ((s8[7340032]{0:T(1024)(128)(4,1)}), s8[4194304]{0:T(1024)(128)(4,1)S(1)}, s32[]{:S(2)}) async-start(s8[7340032]{0:T(1024)(128)(4,1)} %bitcast.58), calls=%async_computation.2 | async-start | bytes 8388608
  54.5 2.6 %slice-start.1 = ((s8[7340032]{0:T(1024)(128)(4,1)}), s8[3145728]{0:T(1024)(128)(4,1)S(1)}, s32[]{:S(2)}) async-start(s8[7340032]{0:T(1024)(128)(4,1)} %bitcast.58), calls=%async_computation.3 | async-start | bytes 6291456
  59.5 5.2 %copy-start.2 = (f32[1,16,2]{1,2,0:T(2,128)S(1)}, f32[1,16,2]{1,2,0:T(2,128)}, u32[]{:S(2)}) copy-start(f32[1,16,2]{1,2,0:T(2,128)} %param.11) | copy-start | bytes 388
  59.5 47.8 %all-to-all-start.1 = ((bf16[16,8,7168]{2,1,0:T(8,128)(2,1)}), bf16[16,8,7168]{2,1,0:T(8,128)(2,1)S(1)}, u32[]{:S(2)}, u32[]{:S(2)}) async-start(bf16[16,8,7168]{2,1,0:T(8,128)(2,1)} %fusion), calls=%async_computation.1 | async-start | bytes 3670016 | tf_op jit(solution)/shard_map/all_to_all | solution.py:52
  64.7 43.0 %copy-start.1 = (bf16[1,16,7168]{2,1,0:T(8,128)(2,1)S(1)}, bf16[1,16,7168]{2,1,0:T(8,128)(2,1)}, u32[]{:S(2)}) copy-start(bf16[1,16,7168]{2,1,0:T(8,128)(2,1)} %param.6) | copy-start | bytes 688132
  108.1 2.6 %collective-permute-start = (bf16[16,7168]{1,0:T(8,128)(2,1)S(1)}, bf16[16,7168]{1,0:T(8,128)(2,1)S(1)}, u32[]{:S(2)}, u32[]{:S(2)}) collective-permute-start(bf16[16,7168]{1,0:T(8,128)(2,1)S(1)} %fusion.3), channel_id=1, source_target_pairs={{0,16},{16,0},{1,17},{17,1},{2,18},{18,2},{3,19},{19,3},{4,20},{20... | collective-permute-start | bytes 688136 | tf_op jit(solution)/shard_map/ppermute | solution.py:13

commit v14 on v13

--- a/solution.py
+++ b/solution.py
@@ -25,9 +25,9 @@
     rows_here, width = tokens.shape
     top = routes.shape[1]
     square = jnp.mean(tokens.astype(jnp.float32) ** 2, axis=-1, keepdims=True)
-    normed = (
+    normed = lax.optimization_barrier((
         tokens.astype(jnp.float32) * lax.rsqrt(square + 1e-06) * gain.astype(jnp.float32)
-    ).astype(jnp.bfloat16)
+    ).astype(jnp.bfloat16))
     chosen = routes[:, :, None] == jnp.arange(EXPERTS)[None, None, :]
     named = jnp.sum(chosen.astype(jnp.int32), axis=1)
     positions = jnp.arange(rows_here)

time: 112 us -> 112 us (level)
  no operation moved by 1% of the time
where the time goes in v14:
time: 112 us; the launch traced here: 111 us
  blocking collectives  48.2 us (43%)
  waiting for transfers between devices  43.3 us (39%)
  starting transfers between devices  6.7 us (6%)
  matrix products  6.51 us (6%)
  other arithmetic  4.58 us (4%)
  local copies, waits for them, and re-layouts  2.03 us (2%)
    all_to_all x1, blocking collectives, shards(): lax.all_to_all(outgoing, 'expert', split_axis=1, concat_axis=1, tiled=True)  48.2 us
    all_to_all x1, waiting for transfers between devices, shards(): lax.all_to_all(partial, 'expert', split_axis=0, concat_axis=0, tiled=True)  42.2 us
    all_to_all x1, starting transfers between devices, shards(): lax.all_to_all(partial, 'expert', split_axis=0, concat_axis=0, tiled=True)  5.17 us
    dot_general x1, matrix products, shards(): jnp.einsum('psd,fd->psf', incoming, up_block, preferred_element_type=jnp....  2.55 us
    dot_general x1, matrix products, shards(): jnp.dot(active, down_block, preferred_element_type=jnp.float32)  2.38 us
  transfers between devices with their start and end apart: 2, of which 2 were waited for; matrix products, arithmetic and copies ran while one was open for 0% of the time, Pallas kernels for 0%

profile of v14, /device:TPU:13, one launch (start us, length us, event | category | flops | bytes accessed | tf_op | source)
XLA Modules:
  0.0 111.4 jit_solution(12918490732830532153)
XLA Ops:
  0.0 0.7 convert_reduce_fusion
  0.7 0.1 convolution_add_fusion
  0.8 0.8 select_reduce_fusion
  1.5 0.8 mul.54
  2.3 1.1 fusion.12
  3.4 1.1 fusion.14
  4.5 0.1 compare_reduce_fusion
  4.6 0.0 copy-start
  4.6 0.7 convolution_convert_fusion.1
  5.3 1.0 copy.27
  6.3 0.0 slice-start
  6.3 48.2 %all_to_all.10 = bf16[8,16,7168]{2,0,1:T(8,128)(2,1)S(1)} all-to-all(bf16[8,16,7168]{2,0,1:T(8,128)(2,1)S(1)} %copy.27), channel_id=1, replica_groups=mesh['segment'=2,'expert'=16] {'expert'}, dimensions={1} | all-to-all | bytes 3670016 | tf_op jit(solution)/shard_map/all_to_all | solution.py:46
  54.5 0.0 copy-done
  54.5 0.0 slice-start.1
  54.5 2.5 %fusion.17 = bf16[128,512]{1,0:T(8,128)(2,1)S(1)} fusion(bf16[8,16,7168]{2,0,1:T(8,128)(2,1)S(1)} %all_to_all.10, bf16[1,512,7168]{2,1,0:T(8,128)(2,1)S(1)} %copy-done), kind=kOutput, calls=%fused_computation.21 | convolution fusion | flops 939851776 | bytes 9306112 | tf_op jit(solution)/shard_map/psd,fd->psf/dot_general | solution.py:47
  57.0 0.0 slice-done
  57.0 0.0 slice-done.1
  57.1 2.4 %fusion = bf16[16,8,7168]{2,1,0:T(8,128)(2,1)} fusion(bf16[128,512]{1,0:T(8,128)(2,1)S(1)} %fusion.17, bf16[1,512,7168]{2,1,0:T(8,128)(2,1)S(1)} %bitcast.57), kind=kOutput, calls=%fused_computation.2 | convolution fusion | flops 940441600 | bytes 9306112 | tf_op jit(solution)/shard_map/dot_general | solution.py:50
  59.4 0.0 copy-start.2
  59.5 5.2 %all-to-all-start.1 = ((bf16[16,8,7168]{2,1,0:T(8,128)(2,1)}), bf16[16,8,7168]{2,1,0:T(8,128)(2,1)S(1)}, u32[]{:S(2)}, u32[]{:S(2)}) async-start(bf16[16,8,7168]{2,1,0:T(8,128)(2,1)} %fusion), calls=%async_computation.1 | async-start | bytes 3670016 | tf_op jit(solution)/shard_map/all_to_all | solution.py:52
  64.6 0.0 copy-done.2
  64.6 0.1 fusion.20
  64.7 0.1 reshape.70
  64.8 0.1 copy.29
  64.9 0.1 copy.28
  65.1 42.2 %all-to-all-done.1 = bf16[16,8,7168]{2,1,0:T(8,128)(2,1)S(1)} async-done(((bf16[16,8,7168]{2,1,0:T(8,128)(2,1)}), bf16[16,8,7168]{2,1,0:T(8,128)(2,1)S(1)}, u32[]{:S(2)}, u32[]{:S(2)}) %all-to-all-start.1) | async-done | bytes 1835040 | tf_op jit(solution)/shard_map/all_to_all | solution.py:52
  107.3 0.4 convolution_bitcast_fusion
  107.7 0.0 copy-done.1
  107.7 0.4 fusion.3
  108.1 1.5 %collective-permute-start = (bf16[16,7168]{1,0:T(8,128)(2,1)S(1)}, bf16[16,7168]{1,0:T(8,128)(2,1)S(1)}, u32[]{:S(2)}, u32[]{:S(2)}) collective-permute-start(bf16[16,7168]{1,0:T(8,128)(2,1)S(1)} %fusion.3), channel_id=1, source_target_pairs={{0,16},{16,0},{1,17},{17,1},{2,18},{18,2},{3,19},{19,3},{4,20},{20... | collective-permute-start | bytes 688136 | tf_op jit(solution)/shard_map/ppermute | solution.py:13
  109.6 1.1 %collective-permute-done = bf16[16,7168]{1,0:T(8,128)(2,1)S(1)} collective-permute-done((bf16[16,7168]{1,0:T(8,128)(2,1)S(1)}, bf16[16,7168]{1,0:T(8,128)(2,1)S(1)}, u32[]{:S(2)}, u32[]{:S(2)}) %collective-permute-start) | collective-permute-done | bytes 229408 | tf_op jit(solution)/shard_map/ppermute | solution.py:13
  110.7 0.7 copy.31
  (6 shorter events, 0.0 us)
Async XLA Ops:
  4.6 49.9 %copy-start = (bf16[1,512,7168]{2,1,0:T(8,128)(2,1)S(1)}, bf16[1,512,7168]{2,1,0:T(8,128)(2,1)}, u32[]{:S(2)}) copy-start(bf16[1,512,7168]{2,1,0:T(8,128)(2,1)} %param.8) | copy-start | bytes 22020100
  6.3 50.7 %slice-start = ((s8[7340032]{0:T(1024)(128)(4,1)}), s8[4194304]{0:T(1024)(128)(4,1)S(1)}, s32[]{:S(2)}) async-start(s8[7340032]{0:T(1024)(128)(4,1)} %bitcast.56), calls=%async_computation.2 | async-start | bytes 8388608
  54.5 2.6 %slice-start.1 = ((s8[7340032]{0:T(1024)(128)(4,1)}), s8[3145728]{0:T(1024)(128)(4,1)S(1)}, s32[]{:S(2)}) async-start(s8[7340032]{0:T(1024)(128)(4,1)} %bitcast.56), calls=%async_computation.3 | async-start | bytes 6291456
  59.4 5.2 %copy-start.2 = (f32[1,16,2]{1,2,0:T(2,128)S(1)}, f32[1,16,2]{1,2,0:T(2,128)}, u32[]{:S(2)}) copy-start(f32[1,16,2]{1,2,0:T(2,128)} %param.11) | copy-start | bytes 388
  59.5 47.8 %all-to-all-start.1 = ((bf16[16,8,7168]{2,1,0:T(8,128)(2,1)}), bf16[16,8,7168]{2,1,0:T(8,128)(2,1)S(1)}, u32[]{:S(2)}, u32[]{:S(2)}) async-start(bf16[16,8,7168]{2,1,0:T(8,128)(2,1)} %fusion), calls=%async_computation.1 | async-start | bytes 3670016 | tf_op jit(solution)/shard_map/all_to_all | solution.py:52
  64.6 43.0 %copy-start.1 = (bf16[1,16,7168]{2,1,0:T(8,128)(2,1)S(1)}, bf16[1,16,7168]{2,1,0:T(8,128)(2,1)}, u32[]{:S(2)}) copy-start(bf16[1,16,7168]{2,1,0:T(8,128)(2,1)} %param.6) | copy-start | bytes 688132
  108.1 2.6 %collective-permute-start = (bf16[16,7168]{1,0:T(8,128)(2,1)S(1)}, bf16[16,7168]{1,0:T(8,128)(2,1)S(1)}, u32[]{:S(2)}, u32[]{:S(2)}) collective-permute-start(bf16[16,7168]{1,0:T(8,128)(2,1)S(1)} %fusion.3), channel_id=1, source_target_pairs={{0,16},{16,0},{1,17},{17,1},{2,18},{18,2},{3,19},{19,3},{4,20},{20... | collective-permute-start | bytes 688136 | tf_op jit(solution)/shard_map/ppermute | solution.py:13

commit v15 on v13

--- a/solution.py
+++ b/solution.py
@@ -28,13 +28,13 @@
     normed = (
         tokens.astype(jnp.float32) * lax.rsqrt(square + 1e-06) * gain.astype(jnp.float32)
     ).astype(jnp.bfloat16)
-    chosen = routes[:, :, None] == jnp.arange(EXPERTS)[None, None, :]
-    named = jnp.sum(chosen.astype(jnp.int32), axis=1)
+    chosen = lax.optimization_barrier((routes[:, :, None] == jnp.arange(EXPERTS)[None, None, :]).astype(jnp.int32))
+    named = jnp.sum(chosen, axis=1)
     positions = jnp.arange(rows_here)
     earlier = (positions[None, :] < positions[:, None]).astype(jnp.int32)
     before = jnp.dot(earlier, named, preferred_element_type=jnp.int32)
     places = jnp.arange(EXPERTS)[None, None, :] * SLOTS + before[:, None, :]
-    key = jnp.sum(jnp.where(chosen, places, 0), axis=2)
+    key = jnp.sum(chosen * places, axis=2)
     slot = jnp.arange(members * SLOTS)
     slot_device = slot % members
     slot_rank = slot // members

time: 112 us -> 111 us (level)
    reduce_sum x2, other arithmetic: 1.44 us -> 0.07 us  [the longest x1 0.07 us: shards(): key = jnp.sum(chosen * places, axis=2)]
where the time goes in v15:
time: 111 us
  blocking collectives  48.2 us (43%)
  waiting for transfers between devices  43.3 us (39%)
  matrix products  7.61 us (7%)
  starting transfers between devices  6.7 us (6%)
  other arithmetic  2.84 us (3%)
  local copies, waits for them, and re-layouts  2.03 us (2%)
    all_to_all x1, blocking collectives, shards(): lax.all_to_all(outgoing, 'expert', split_axis=1, concat_axis=1, tiled=True)  48.2 us
    all_to_all x1, waiting for transfers between devices, shards(): lax.all_to_all(partial, 'expert', split_axis=0, concat_axis=0, tiled=True)  42.2 us
    all_to_all x1, starting transfers between devices, shards(): lax.all_to_all(partial, 'expert', split_axis=0, concat_axis=0, tiled=True)  5.17 us
    dot_general x1, matrix products, shards(): jnp.einsum('psd,fd->psf', incoming, up_block, preferred_element_type=jnp....  2.55 us
    dot_general x1, matrix products, shards(): jnp.dot(active, down_block, preferred_element_type=jnp.float32)  2.38 us
  transfers between devices with their start and end apart: 2, of which 2 were waited for; matrix products, arithmetic and copies ran while one was open for 0% of the time, Pallas kernels for 0%

profile of v15, /device:TPU:13, one launch (start us, length us, event | category | flops | bytes accessed | tf_op | source)
XLA Modules:
  0.0 110.8 jit_solution(11627353596237726410)
XLA Ops:
  0.0 0.7 fusion.25
  0.7 0.1 convolution_add_fusion
  0.8 0.1 multiply_reduce_fusion
  0.9 0.8 mul.64
  1.6 1.1 %fusion.12 = f32[16]{0:T(128)S(1)} fusion(bf16[1,16,7168]{2,1,0:T(8,128)(2,1)} %param.6), kind=kLoop, calls=%fused_computation.17 | loop fusion | flops 344048 | bytes 229440 | tf_op jit(solution)/shard_map/reduce_sum | solution.py:27
  2.8 0.1 compare_reduce_fusion
  2.8 0.0 copy-start
  2.8 1.8 %convolution_convert_fusion.1 = bf16[128,7168]{1,0:T(8,128)(2,1)S(1)} fusion(pred[128,16]{0,1:T(8,128)(4,1)S(1)} %compare_reduce_fusion, bf16[1,16,7168]{2,1,0:T(8,128)(2,1)} %param.6, f32[7168]{0:T(1024)S(1)} %bitcast.62, f32[16]{0:T(128)S(1)} %add_rsqrt_fusion), kind=kOutput, calls=%fused_computation.1 | convolution fusion | flops 30736384 | bytes 2095168 | tf_op jit(solution)/shard_map/dot_general | solution.py:44
  4.6 1.0 copy.30
  5.7 0.0 slice-start
  5.7 48.2 %all_to_all.10 = bf16[8,16,7168]{2,0,1:T(8,128)(2,1)S(1)} all-to-all(bf16[8,16,7168]{2,0,1:T(8,128)(2,1)S(1)} %copy.30), channel_id=1, replica_groups=mesh['segment'=2,'expert'=16] {'expert'}, dimensions={1} | all-to-all | bytes 3670016 | tf_op jit(solution)/shard_map/all_to_all | solution.py:46
  53.8 0.0 copy-done
  53.8 0.0 slice-start.1
  53.8 2.5 %fusion.17 = bf16[128,512]{1,0:T(8,128)(2,1)S(1)} fusion(bf16[8,16,7168]{2,0,1:T(8,128)(2,1)S(1)} %all_to_all.10, bf16[1,512,7168]{2,1,0:T(8,128)(2,1)S(1)} %copy-done), kind=kOutput, calls=%fused_computation.21 | convolution fusion | flops 939851776 | bytes 9306112 | tf_op jit(solution)/shard_map/psd,fd->psf/dot_general | solution.py:47
  56.4 0.0 slice-done
  56.4 0.0 slice-done.1
  56.4 2.4 %fusion = bf16[16,8,7168]{2,1,0:T(8,128)(2,1)} fusion(bf16[128,512]{1,0:T(8,128)(2,1)S(1)} %fusion.17, bf16[1,512,7168]{2,1,0:T(8,128)(2,1)S(1)} %bitcast.59), kind=kOutput, calls=%fused_computation.2 | convolution fusion | flops 940441600 | bytes 9306112 | tf_op jit(solution)/shard_map/dot_general | solution.py:50
  58.8 0.0 copy-start.2
  58.8 5.2 %all-to-all-start.1 = ((bf16[16,8,7168]{2,1,0:T(8,128)(2,1)}), bf16[16,8,7168]{2,1,0:T(8,128)(2,1)S(1)}, u32[]{:S(2)}, u32[]{:S(2)}) async-start(bf16[16,8,7168]{2,1,0:T(8,128)(2,1)} %fusion), calls=%async_computation.1 | async-start | bytes 3670016 | tf_op jit(solution)/shard_map/all_to_all | solution.py:52
  64.0 0.0 copy-start.1
  64.0 0.0 copy-done.2
  64.0 0.1 fusion.24
  64.1 0.1 reshape.70
  64.2 0.1 copy.32
  64.3 0.1 copy.31
  64.4 42.2 %all-to-all-done.1 = bf16[16,8,7168]{2,1,0:T(8,128)(2,1)S(1)} async-done(((bf16[16,8,7168]{2,1,0:T(8,128)(2,1)}), bf16[16,8,7168]{2,1,0:T(8,128)(2,1)S(1)}, u32[]{:S(2)}, u32[]{:S(2)}) %all-to-all-start.1) | async-done | bytes 1835040 | tf_op jit(solution)/shard_map/all_to_all | solution.py:52
  106.6 0.4 convolution_bitcast_fusion
  107.0 0.0 copy-done.1
  107.0 0.4 fusion.3
  107.5 1.5 %collective-permute-start = (bf16[16,7168]{1,0:T(8,128)(2,1)S(1)}, bf16[16,7168]{1,0:T(8,128)(2,1)S(1)}, u32[]{:S(2)}, u32[]{:S(2)}) collective-permute-start(bf16[16,7168]{1,0:T(8,128)(2,1)S(1)} %fusion.3), channel_id=1, source_target_pairs={{0,16},{16,0},{1,17},{17,1},{2,18},{18,2},{3,19},{19,3},{4,20},{20... | collective-permute-start | bytes 688136 | tf_op jit(solution)/shard_map/ppermute | solution.py:13
  109.0 1.1 %collective-permute-done = bf16[16,7168]{1,0:T(8,128)(2,1)S(1)} collective-permute-done((bf16[16,7168]{1,0:T(8,128)(2,1)S(1)}, bf16[16,7168]{1,0:T(8,128)(2,1)S(1)}, u32[]{:S(2)}, u32[]{:S(2)}) %collective-permute-start) | collective-permute-done | bytes 229408 | tf_op jit(solution)/shard_map/ppermute | solution.py:13
  110.1 0.7 copy.34
  (6 shorter events, 0.0 us)
Async XLA Ops:
  2.8 51.0 %copy-start = (bf16[1,512,7168]{2,1,0:T(8,128)(2,1)S(1)}, bf16[1,512,7168]{2,1,0:T(8,128)(2,1)}, u32[]{:S(2)}) copy-start(bf16[1,512,7168]{2,1,0:T(8,128)(2,1)} %param.8) | copy-start | bytes 22020100
  5.7 50.7 %slice-start = ((s8[7340032]{0:T(1024)(128)(4,1)}), s8[4194304]{0:T(1024)(128)(4,1)S(1)}, s32[]{:S(2)}) async-start(s8[7340032]{0:T(1024)(128)(4,1)} %bitcast.58), calls=%async_computation.2 | async-start | bytes 8388608
  53.8 2.6 %slice-start.1 = ((s8[7340032]{0:T(1024)(128)(4,1)}), s8[3145728]{0:T(1024)(128)(4,1)S(1)}, s32[]{:S(2)}) async-start(s8[7340032]{0:T(1024)(128)(4,1)} %bitcast.58), calls=%async_computation.3 | async-start | bytes 6291456
  58.8 5.2 %copy-start.2 = (f32[1,16,2]{1,2,0:T(2,128)S(1)}, f32[1,16,2]{1,2,0:T(2,128)}, u32[]{:S(2)}) copy-start(f32[1,16,2]{1,2,0:T(2,128)} %param.11) | copy-start | bytes 388
  58.8 47.8 %all-to-all-start.1 = ((bf16[16,8,7168]{2,1,0:T(8,128)(2,1)}), bf16[16,8,7168]{2,1,0:T(8,128)(2,1)S(1)}, u32[]{:S(2)}, u32[]{:S(2)}) async-start(bf16[16,8,7168]{2,1,0:T(8,128)(2,1)} %fusion), calls=%async_computation.1 | async-start | bytes 3670016 | tf_op jit(solution)/shard_map/all_to_all | solution.py:52
  64.0 43.0 %copy-start.1 = (bf16[1,16,7168]{2,1,0:T(8,128)(2,1)S(1)}, bf16[1,16,7168]{2,1,0:T(8,128)(2,1)}, u32[]{:S(2)}) copy-start(bf16[1,16,7168]{2,1,0:T(8,128)(2,1)} %param.6) | copy-start | bytes 688132
  107.5 2.6 %collective-permute-start = (bf16[16,7168]{1,0:T(8,128)(2,1)S(1)}, bf16[16,7168]{1,0:T(8,128)(2,1)S(1)}, u32[]{:S(2)}, u32[]{:S(2)}) collective-permute-start(bf16[16,7168]{1,0:T(8,128)(2,1)S(1)} %fusion.3), channel_id=1, source_target_pairs={{0,16},{16,0},{1,17},{17,1},{2,18},{18,2},{3,19},{19,3},{4,20},{20... | collective-permute-start | bytes 688136 | tf_op jit(solution)/shard_map/ppermute | solution.py:13

commit v16 on v15

--- a/solution.py
+++ b/solution.py
@@ -24,10 +24,9 @@
     weights = gate_weights[0]
     rows_here, width = tokens.shape
     top = routes.shape[1]
-    square = jnp.mean(tokens.astype(jnp.float32) ** 2, axis=-1, keepdims=True)
-    normed = (
-        tokens.astype(jnp.float32) * lax.rsqrt(square + 1e-06) * gain.astype(jnp.float32)
-    ).astype(jnp.bfloat16)
+    wide = lax.optimization_barrier(tokens.astype(jnp.float32))
+    square = jnp.mean(wide ** 2, axis=-1, keepdims=True)
+    normed = (wide * lax.rsqrt(square + 1e-06) * gain.astype(jnp.float32)).astype(jnp.bfloat16)
     chosen = lax.optimization_barrier((routes[:, :, None] == jnp.arange(EXPERTS)[None, None, :]).astype(jnp.int32))
     named = jnp.sum(chosen, axis=1)
     positions = jnp.arange(rows_here)

time: 111 us -> 110 us (level)
  no operation moved by 1% of the time
where the time goes in v16:
time: 110 us
  blocking collectives  48.2 us (44%)
  waiting for transfers between devices  43.3 us (39%)
  starting transfers between devices  6.7 us (6%)
  matrix products  6.52 us (6%)
  other arithmetic  2.88 us (3%)
  local copies, waits for them, and re-layouts  2.03 us (2%)
    all_to_all x1, blocking collectives, shards(): lax.all_to_all(outgoing, 'expert', split_axis=1, concat_axis=1, tiled=True)  48.2 us
    all_to_all x1, waiting for transfers between devices, shards(): lax.all_to_all(partial, 'expert', split_axis=0, concat_axis=0, tiled=True)  42.2 us
    all_to_all x1, starting transfers between devices, shards(): lax.all_to_all(partial, 'expert', split_axis=0, concat_axis=0, tiled=True)  5.17 us
    dot_general x1, matrix products, shards(): jnp.einsum('psd,fd->psf', incoming, up_block, preferred_element_type=jnp....  2.55 us
    dot_general x1, matrix products, shards(): jnp.dot(active, down_block, preferred_element_type=jnp.float32)  2.38 us
  transfers between devices with their start and end apart: 2, of which 2 were waited for; matrix products, arithmetic and copies ran while one was open for 0% of the time, Pallas kernels for 0%

profile of v16, /device:TPU:13, one launch (start us, length us, event | category | flops | bytes accessed | tf_op | source)
XLA Modules:
  0.0 109.7 jit_solution(17214440703948489546)
XLA Ops:
  0.0 0.7 fusion.20
  0.7 0.1 convolution_add_fusion
  0.8 0.1 multiply_reduce_fusion.1
  0.9 1.0 bitcast_convert_fusion
  1.8 0.2 multiply_reduce_fusion
  2.0 0.8 mul.64
  2.8 0.1 compare_reduce_fusion
  2.9 0.0 copy-start
  2.9 0.7 convolution_convert_fusion.1
  3.6 1.0 copy.30
  4.6 0.0 slice-start
  4.6 48.2 %all_to_all.10 = bf16[8,16,7168]{2,0,1:T(8,128)(2,1)S(1)} all-to-all(bf16[8,16,7168]{2,0,1:T(8,128)(2,1)S(1)} %copy.30), channel_id=1, replica_groups=mesh['segment'=2,'expert'=16] {'expert'}, dimensions={1} | all-to-all | bytes 3670016 | tf_op jit(solution)/shard_map/all_to_all | solution.py:45
  52.8 0.0 copy-done
  52.8 0.0 slice-start.1
  52.8 2.5 %fusion.14 = bf16[128,512]{1,0:T(8,128)(2,1)S(1)} fusion(bf16[8,16,7168]{2,0,1:T(8,128)(2,1)S(1)} %all_to_all.10, bf16[1,512,7168]{2,1,0:T(8,128)(2,1)S(1)} %copy-done), kind=kOutput, calls=%fused_computation.18 | convolution fusion | flops 939851776 | bytes 9306112 | tf_op jit(solution)/shard_map/psd,fd->psf/dot_general | solution.py:46
  55.3 0.0 slice-done
  55.4 0.0 slice-done.1
  55.4 2.4 %fusion = bf16[16,8,7168]{2,1,0:T(8,128)(2,1)} fusion(bf16[128,512]{1,0:T(8,128)(2,1)S(1)} %fusion.14, bf16[1,512,7168]{2,1,0:T(8,128)(2,1)S(1)} %bitcast.56), kind=kOutput, calls=%fused_computation.2 | convolution fusion | flops 940441600 | bytes 9306112 | tf_op jit(solution)/shard_map/dot_general | solution.py:49
  57.8 0.0 copy-start.2
  57.8 5.2 %all-to-all-start.1 = ((bf16[16,8,7168]{2,1,0:T(8,128)(2,1)}), bf16[16,8,7168]{2,1,0:T(8,128)(2,1)S(1)}, u32[]{:S(2)}, u32[]{:S(2)}) async-start(bf16[16,8,7168]{2,1,0:T(8,128)(2,1)} %fusion), calls=%async_computation.1 | async-start | bytes 3670016 | tf_op jit(solution)/shard_map/all_to_all | solution.py:51
  62.9 0.0 copy-done.2
  63.0 0.1 fusion.19
  63.0 0.1 reshape.70
  63.1 0.1 copy.32
  63.2 0.1 copy.31
  63.4 42.2 %all-to-all-done.1 = bf16[16,8,7168]{2,1,0:T(8,128)(2,1)S(1)} async-done(((bf16[16,8,7168]{2,1,0:T(8,128)(2,1)}), bf16[16,8,7168]{2,1,0:T(8,128)(2,1)S(1)}, u32[]{:S(2)}, u32[]{:S(2)}) %all-to-all-start.1) | async-done | bytes 1835040 | tf_op jit(solution)/shard_map/all_to_all | solution.py:51
  105.6 0.4 convolution_bitcast_fusion
  106.0 0.0 copy-done.1
  106.0 0.4 fusion.3
  106.4 1.5 %collective-permute-start = (bf16[16,7168]{1,0:T(8,128)(2,1)S(1)}, bf16[16,7168]{1,0:T(8,128)(2,1)S(1)}, u32[]{:S(2)}, u32[]{:S(2)}) collective-permute-start(bf16[16,7168]{1,0:T(8,128)(2,1)S(1)} %fusion.3), channel_id=1, source_target_pairs={{0,16},{16,0},{1,17},{17,1},{2,18},{18,2},{3,19},{19,3},{4,20},{20... | collective-permute-start | bytes 688136 | tf_op jit(solution)/shard_map/ppermute | solution.py:13
  107.9 1.1 %collective-permute-done = bf16[16,7168]{1,0:T(8,128)(2,1)S(1)} collective-permute-done((bf16[16,7168]{1,0:T(8,128)(2,1)S(1)}, bf16[16,7168]{1,0:T(8,128)(2,1)S(1)}, u32[]{:S(2)}, u32[]{:S(2)}) %collective-permute-start) | collective-permute-done | bytes 229408 | tf_op jit(solution)/shard_map/ppermute | solution.py:13
  109.0 0.7 copy.34
  (7 shorter events, 0.0 us)
Async XLA Ops:
  2.9 49.9 %copy-start = (bf16[1,512,7168]{2,1,0:T(8,128)(2,1)S(1)}, bf16[1,512,7168]{2,1,0:T(8,128)(2,1)}, u32[]{:S(2)}) copy-start(bf16[1,512,7168]{2,1,0:T(8,128)(2,1)} %param.8) | copy-start | bytes 22020100
  4.6 50.7 %slice-start = ((s8[7340032]{0:T(1024)(128)(4,1)}), s8[4194304]{0:T(1024)(128)(4,1)S(1)}, s32[]{:S(2)}) async-start(s8[7340032]{0:T(1024)(128)(4,1)} %bitcast.55), calls=%async_computation.2 | async-start | bytes 8388608
  52.8 2.6 %slice-start.1 = ((s8[7340032]{0:T(1024)(128)(4,1)}), s8[3145728]{0:T(1024)(128)(4,1)S(1)}, s32[]{:S(2)}) async-start(s8[7340032]{0:T(1024)(128)(4,1)} %bitcast.55), calls=%async_computation.3 | async-start | bytes 6291456
  57.8 5.2 %copy-start.2 = (f32[1,16,2]{1,2,0:T(2,128)S(1)}, f32[1,16,2]{1,2,0:T(2,128)}, u32[]{:S(2)}) copy-start(f32[1,16,2]{1,2,0:T(2,128)} %param.11) | copy-start | bytes 388
  57.8 47.8 %all-to-all-start.1 = ((bf16[16,8,7168]{2,1,0:T(8,128)(2,1)}), bf16[16,8,7168]{2,1,0:T(8,128)(2,1)S(1)}, u32[]{:S(2)}, u32[]{:S(2)}) async-start(bf16[16,8,7168]{2,1,0:T(8,128)(2,1)} %fusion), calls=%async_computation.1 | async-start | bytes 3670016 | tf_op jit(solution)/shard_map/all_to_all | solution.py:51
  62.9 43.0 %copy-start.1 = (bf16[1,16,7168]{2,1,0:T(8,128)(2,1)S(1)}, bf16[1,16,7168]{2,1,0:T(8,128)(2,1)}, u32[]{:S(2)}) copy-start(bf16[1,16,7168]{2,1,0:T(8,128)(2,1)} %param.6) | copy-start | bytes 688132
  106.4 2.6 %collective-permute-start = (bf16[16,7168]{1,0:T(8,128)(2,1)S(1)}, bf16[16,7168]{1,0:T(8,128)(2,1)S(1)}, u32[]{:S(2)}, u32[]{:S(2)}) collective-permute-start(bf16[16,7168]{1,0:T(8,128)(2,1)S(1)} %fusion.3), channel_id=1, source_target_pairs={{0,16},{16,0},{1,17},{17,1},{2,18},{18,2},{3,19},{19,3},{4,20},{20... | collective-permute-start | bytes 688136 | tf_op jit(solution)/shard_map/ppermute | solution.py:13

commit v17 on v16

--- a/solution.py
+++ b/solution.py
@@ -24,9 +24,10 @@
     weights = gate_weights[0]
     rows_here, width = tokens.shape
     top = routes.shape[1]
-    wide = lax.optimization_barrier(tokens.astype(jnp.float32))
+    stacked = lax.optimization_barrier(jnp.concatenate([tokens, gain[None, :]], axis=0).astype(jnp.float32))
+    wide = stacked[:rows_here]
     square = jnp.mean(wide ** 2, axis=-1, keepdims=True)
-    normed = (wide * lax.rsqrt(square + 1e-06) * gain.astype(jnp.float32)).astype(jnp.bfloat16)
+    normed = (wide * lax.rsqrt(square + 1e-06) * stacked[rows_here:]).astype(jnp.bfloat16)
     chosen = lax.optimization_barrier((routes[:, :, None] == jnp.arange(EXPERTS)[None, None, :]).astype(jnp.int32))
     named = jnp.sum(chosen, axis=1)
     positions = jnp.arange(rows_here)

time: 110 us -> 109 us (level)
  no operation moved by 1% of the time
where the time goes in v17:
time: 109 us
  blocking collectives  48.2 us (44%)
  waiting for transfers between devices  43.3 us (40%)
  starting transfers between devices  6.71 us (6%)
  matrix products  6.52 us (6%)
  other arithmetic  2.12 us (2%)
  local copies, waits for them, and re-layouts  2.05 us (2%)
    all_to_all x1, blocking collectives, shards(): lax.all_to_all(outgoing, 'expert', split_axis=1, concat_axis=1, tiled=True)  48.2 us
    all_to_all x1, waiting for transfers between devices, shards(): lax.all_to_all(partial, 'expert', split_axis=0, concat_axis=0, tiled=True)  42.2 us
    all_to_all x1, starting transfers between devices, shards(): lax.all_to_all(partial, 'expert', split_axis=0, concat_axis=0, tiled=True)  5.18 us
    dot_general x1, matrix products, shards(): jnp.einsum('psd,fd->psf', incoming, up_block, preferred_element_type=jnp....  2.54 us
    dot_general x1, matrix products, shards(): jnp.dot(active, down_block, preferred_element_type=jnp.float32)  2.39 us
  transfers between devices with their start and end apart: 2, of which 2 were waited for; matrix products, arithmetic and copies ran while one was open for 0% of the time, Pallas kernels for 0%

profile of v17, /device:TPU:13, one launch (start us, length us, event | category | flops | bytes accessed | tf_op | source)
XLA Modules:
  0.0 109.0 jit_solution(15758558621225353829)
XLA Ops:
  0.0 1.0 maximum_convert_fusion
  1.0 0.2 multiply_reduce_fusion
  1.2 0.7 fusion.20
  1.9 0.1 convolution_add_fusion
  2.0 0.1 multiply_reduce_fusion.1
  2.1 0.1 compare_reduce_fusion
  2.2 0.0 copy-start
  2.2 0.7 convolution_convert_fusion.1
  2.9 1.0 copy.30
  3.9 0.0 slice-start
  3.9 48.2 %all_to_all.10 = bf16[8,16,7168]{2,0,1:T(8,128)(2,1)S(1)} all-to-all(bf16[8,16,7168]{2,0,1:T(8,128)(2,1)S(1)} %copy.30), channel_id=1, replica_groups=mesh['segment'=2,'expert'=16] {'expert'}, dimensions={1} | all-to-all | bytes 3670016 | tf_op jit(solution)/shard_map/all_to_all | solution.py:46
  52.1 0.0 copy-done
  52.1 0.0 slice-start.1
  52.1 2.5 %fusion.14 = bf16[128,512]{1,0:T(8,128)(2,1)S(1)} fusion(bf16[8,16,7168]{2,0,1:T(8,128)(2,1)S(1)} %all_to_all.10, bf16[1,512,7168]{2,1,0:T(8,128)(2,1)S(1)} %copy-done), kind=kOutput, calls=%fused_computation.19 | convolution fusion | flops 939851776 | bytes 9306112 | tf_op jit(solution)/shard_map/psd,fd->psf/dot_general | solution.py:47
  54.6 0.0 slice-done
  54.6 0.0 slice-done.1
  54.6 2.4 %fusion = bf16[16,8,7168]{2,1,0:T(8,128)(2,1)} fusion(bf16[128,512]{1,0:T(8,128)(2,1)S(1)} %fusion.14, bf16[1,512,7168]{2,1,0:T(8,128)(2,1)S(1)} %bitcast.53), kind=kOutput, calls=%fused_computation.2 | convolution fusion | flops 940441600 | bytes 9306112 | tf_op jit(solution)/shard_map/dot_general | solution.py:50
  57.0 0.0 copy-start.2
  57.0 5.2 %all-to-all-start.1 = ((bf16[16,8,7168]{2,1,0:T(8,128)(2,1)}), bf16[16,8,7168]{2,1,0:T(8,128)(2,1)S(1)}, u32[]{:S(2)}, u32[]{:S(2)}) async-start(bf16[16,8,7168]{2,1,0:T(8,128)(2,1)} %fusion), calls=%async_computation.1 | async-start | bytes 3670016 | tf_op jit(solution)/shard_map/all_to_all | solution.py:52
  62.2 0.0 copy-start.1
  62.2 0.0 copy-done.2
  62.2 0.1 fusion.19
  62.3 0.1 reshape.68
  62.4 0.1 copy.32
  62.5 0.1 copy.31
  62.6 42.2 %all-to-all-done.1 = bf16[16,8,7168]{2,1,0:T(8,128)(2,1)S(1)} async-done(((bf16[16,8,7168]{2,1,0:T(8,128)(2,1)}), bf16[16,8,7168]{2,1,0:T(8,128)(2,1)S(1)}, u32[]{:S(2)}, u32[]{:S(2)}) %all-to-all-start.1) | async-done | bytes 1835040 | tf_op jit(solution)/shard_map/all_to_all | solution.py:52
  104.9 0.4 convolution_bitcast_fusion
  105.2 0.0 copy-done.1
  105.3 0.4 fusion.3
  105.7 1.5 %collective-permute-start = (bf16[16,7168]{1,0:T(8,128)(2,1)S(1)}, bf16[16,7168]{1,0:T(8,128)(2,1)S(1)}, u32[]{:S(2)}, u32[]{:S(2)}) collective-permute-start(bf16[16,7168]{1,0:T(8,128)(2,1)S(1)} %fusion.3), channel_id=1, source_target_pairs={{0,16},{16,0},{1,17},{17,1},{2,18},{18,2},{3,19},{19,3},{4,20},{20... | collective-permute-start | bytes 688136 | tf_op jit(solution)/shard_map/ppermute | solution.py:13
  107.2 1.1 %collective-permute-done = bf16[16,7168]{1,0:T(8,128)(2,1)S(1)} collective-permute-done((bf16[16,7168]{1,0:T(8,128)(2,1)S(1)}, bf16[16,7168]{1,0:T(8,128)(2,1)S(1)}, u32[]{:S(2)}, u32[]{:S(2)}) %collective-permute-start) | collective-permute-done | bytes 229408 | tf_op jit(solution)/shard_map/ppermute | solution.py:13
  108.3 0.7 copy.34
  (7 shorter events, 0.1 us)
Async XLA Ops:
  2.2 49.9 %copy-start = (bf16[1,512,7168]{2,1,0:T(8,128)(2,1)S(1)}, bf16[1,512,7168]{2,1,0:T(8,128)(2,1)}, u32[]{:S(2)}) copy-start(bf16[1,512,7168]{2,1,0:T(8,128)(2,1)} %param.8) | copy-start | bytes 22020100
  3.9 50.7 %slice-start = ((s8[7340032]{0:T(1024)(128)(4,1)}), s8[4194304]{0:T(1024)(128)(4,1)S(1)}, s32[]{:S(2)}) async-start(s8[7340032]{0:T(1024)(128)(4,1)} %bitcast.52), calls=%async_computation.2 | async-start | bytes 8388608
  52.1 2.6 %slice-start.1 = ((s8[7340032]{0:T(1024)(128)(4,1)}), s8[3145728]{0:T(1024)(128)(4,1)S(1)}, s32[]{:S(2)}) async-start(s8[7340032]{0:T(1024)(128)(4,1)} %bitcast.52), calls=%async_computation.3 | async-start | bytes 6291456
  57.0 5.2 %copy-start.2 = (f32[1,16,2]{1,2,0:T(2,128)S(1)}, f32[1,16,2]{1,2,0:T(2,128)}, u32[]{:S(2)}) copy-start(f32[1,16,2]{1,2,0:T(2,128)} %param.11) | copy-start | bytes 388
  57.0 47.8 %all-to-all-start.1 = ((bf16[16,8,7168]{2,1,0:T(8,128)(2,1)}), bf16[16,8,7168]{2,1,0:T(8,128)(2,1)S(1)}, u32[]{:S(2)}, u32[]{:S(2)}) async-start(bf16[16,8,7168]{2,1,0:T(8,128)(2,1)} %fusion), calls=%async_computation.1 | async-start | bytes 3670016 | tf_op jit(solution)/shard_map/all_to_all | solution.py:52
  62.2 43.0 %copy-start.1 = (bf16[1,16,7168]{2,1,0:T(8,128)(2,1)S(1)}, bf16[1,16,7168]{2,1,0:T(8,128)(2,1)}, u32[]{:S(2)}) copy-start(bf16[1,16,7168]{2,1,0:T(8,128)(2,1)} %param.6) | copy-start | bytes 688132
  105.7 2.6 %collective-permute-start = (bf16[16,7168]{1,0:T(8,128)(2,1)S(1)}, bf16[16,7168]{1,0:T(8,128)(2,1)S(1)}, u32[]{:S(2)}, u32[]{:S(2)}) collective-permute-start(bf16[16,7168]{1,0:T(8,128)(2,1)S(1)} %fusion.3), channel_id=1, source_target_pairs={{0,16},{16,0},{1,17},{17,1},{2,18},{18,2},{3,19},{19,3},{4,20},{20... | collective-permute-start | bytes 688136 | tf_op jit(solution)/shard_map/ppermute | solution.py:13

commit v18 on v17

--- a/solution.py
+++ b/solution.py
@@ -53,8 +53,9 @@
     combine = jnp.sum(jnp.where(hits, weights[None, :, :], 0.0), axis=2).T.reshape(rows_here, SLOTS, members)
     combine_hi = combine.astype(jnp.bfloat16)
     combine_lo = (combine - combine_hi.astype(jnp.float32)).astype(jnp.bfloat16)
-    mixture = jnp.einsum("rps,psd->rd", combine_hi, returned, preferred_element_type=jnp.float32)
-    mixture = mixture + jnp.einsum("rps,psd->rd", combine_lo, returned, preferred_element_type=jnp.float32)
+    both = jnp.concatenate([combine_hi, combine_lo], axis=0)
+    mixed = jnp.einsum("rps,psd->rd", both, returned, preferred_element_type=jnp.float32)
+    mixture = mixed[:rows_here] + mixed[rows_here:]
     section_out = (tokens.astype(jnp.float32) + mixture).astype(jnp.bfloat16)
     handed = passed_along(section_out, "segment", 1)
     return handed[None]

time: 109 us -> 110 us (level)
  no operation moved by 1% of the time
where the time goes in v18:
time: 110 us; the launch traced here: 109 us
  blocking collectives  48.2 us (44%)
  waiting for transfers between devices  43.5 us (40%)
  matrix products  6.92 us (6%)
  starting transfers between devices  6.71 us (6%)
  other arithmetic  2.18 us (2%)
  local copies, waits for them, and re-layouts  1.85 us (2%)
    all_to_all x1, blocking collectives, shards(): lax.all_to_all(outgoing, 'expert', split_axis=1, concat_axis=1, tiled=True)  48.2 us
    all_to_all x1, waiting for transfers between devices, shards(): lax.all_to_all(partial, 'expert', split_axis=0, concat_axis=0, tiled=True)  42.4 us
    all_to_all x1, starting transfers between devices, shards(): lax.all_to_all(partial, 'expert', split_axis=0, concat_axis=0, tiled=True)  5.18 us
    dot_general x1, matrix products, shards(): jnp.einsum('psd,fd->psf', incoming, up_block, preferred_element_type=jnp....  2.54 us
    dot_general x1, matrix products, shards(): jnp.dot(active, down_block, preferred_element_type=jnp.float32)  2.39 us
  transfers between devices with their start and end apart: 2, of which 2 were waited for; matrix products, arithmetic and copies ran while one was open for 0% of the time, Pallas kernels for 0%

profile of v18, /device:TPU:13, one launch (start us, length us, event | category | flops | bytes accessed | tf_op | source)
XLA Modules:
  0.0 109.5 jit_solution(4149751839204530228)
XLA Ops:
  0.0 1.0 maximum_convert_fusion
  1.0 0.2 multiply_reduce_fusion
  1.2 0.7 fusion.22
  1.9 0.1 convolution_add_fusion
  2.0 0.1 multiply_reduce_fusion.1
  2.1 0.1 compare_reduce_fusion
  2.2 0.0 copy-start
  2.2 0.7 convolution_convert_fusion.1
  2.9 1.0 copy.27
  3.9 0.0 slice-start
  3.9 48.2 %all_to_all.10 = bf16[8,16,7168]{2,0,1:T(8,128)(2,1)S(1)} all-to-all(bf16[8,16,7168]{2,0,1:T(8,128)(2,1)S(1)} %copy.27), channel_id=1, replica_groups=mesh['segment'=2,'expert'=16] {'expert'}, dimensions={1} | all-to-all | bytes 3670016 | tf_op jit(solution)/shard_map/all_to_all | solution.py:46
  52.1 0.0 copy-done
  52.1 0.0 slice-start.1
  52.1 2.5 %fusion.13 = bf16[128,512]{1,0:T(8,128)(2,1)S(1)} fusion(bf16[8,16,7168]{2,0,1:T(8,128)(2,1)S(1)} %all_to_all.10, bf16[1,512,7168]{2,1,0:T(8,128)(2,1)S(1)} %copy-done), kind=kOutput, calls=%fused_computation.18 | convolution fusion | flops 939851776 | bytes 9306112 | tf_op jit(solution)/shard_map/psd,fd->psf/dot_general | solution.py:47
  54.6 0.0 slice-done
  54.6 0.0 slice-done.1
  54.6 2.4 %fusion = bf16[16,8,7168]{2,1,0:T(8,128)(2,1)} fusion(bf16[128,512]{1,0:T(8,128)(2,1)S(1)} %fusion.13, bf16[1,512,7168]{2,1,0:T(8,128)(2,1)S(1)} %bitcast.42), kind=kOutput, calls=%fused_computation.2 | convolution fusion | flops 940441600 | bytes 9306112 | tf_op jit(solution)/shard_map/dot_general | solution.py:50
  57.0 0.0 copy-start.2
  57.0 5.2 %all-to-all-start.1 = ((bf16[16,8,7168]{2,1,0:T(8,128)(2,1)}), bf16[16,8,7168]{2,1,0:T(8,128)(2,1)S(1)}, u32[]{:S(2)}, u32[]{:S(2)}) async-start(bf16[16,8,7168]{2,1,0:T(8,128)(2,1)} %fusion), calls=%async_computation.1 | async-start | bytes 3670016 | tf_op jit(solution)/shard_map/all_to_all | solution.py:52
  62.2 0.0 copy-start.1
  62.2 0.0 copy-done.2
  62.2 0.1 fusion.21
  62.3 0.1 copy.26
  62.4 42.4 %all-to-all-done.1 = bf16[16,8,7168]{2,1,0:T(8,128)(2,1)S(1)} async-done(((bf16[16,8,7168]{2,1,0:T(8,128)(2,1)}), bf16[16,8,7168]{2,1,0:T(8,128)(2,1)S(1)}, u32[]{:S(2)}, u32[]{:S(2)}) %all-to-all-start.1) | async-done | bytes 1835040 | tf_op jit(solution)/shard_map/all_to_all | solution.py:52
  104.9 1.2 %convolution_bitcast_fusion = f32[32,7168]{1,0:T(8,128)S(1)} fusion(bf16[16,8,7168]{2,1,0:T(8,128)(2,1)S(1)} %all-to-all-done.1, bf16[16,8,16]{0,2,1:T(8,128)(2,1)S(1)} %get-tuple-element.5, bf16[16,8,16]{0,2,1:T(8,128)(2,1)S(1)} %get-tuple-element.6), kind=kOutput, calls=%fused_computation.3 | convolution fusion | flops 58736640 | bytes 2760704 | tf_op jit(solution)/shard_map/rps,psd->rd/dot_general | solution.py:57
  106.1 0.0 copy-done.1
  106.1 0.1 fusion.10
  106.2 1.5 %collective-permute-start = (bf16[16,7168]{1,0:T(8,128)(2,1)S(1)}, bf16[16,7168]{1,0:T(8,128)(2,1)S(1)}, u32[]{:S(2)}, u32[]{:S(2)}) collective-permute-start(bf16[16,7168]{1,0:T(8,128)(2,1)S(1)} %fusion.10), channel_id=1, source_target_pairs={{0,16},{16,0},{1,17},{17,1},{2,18},{18,2},{3,19},{19,3},{4,20},{20... | collective-permute-start | bytes 688136 | tf_op jit(solution)/shard_map/ppermute | solution.py:13
  107.7 1.1 %collective-permute-done = bf16[16,7168]{1,0:T(8,128)(2,1)S(1)} collective-permute-done((bf16[16,7168]{1,0:T(8,128)(2,1)S(1)}, bf16[16,7168]{1,0:T(8,128)(2,1)S(1)}, u32[]{:S(2)}, u32[]{:S(2)}) %collective-permute-start) | collective-permute-done | bytes 229408 | tf_op jit(solution)/shard_map/ppermute | solution.py:13
  108.8 0.7 copy.34
  (7 shorter events, 0.1 us)
Async XLA Ops:
  2.2 49.9 %copy-start = (bf16[1,512,7168]{2,1,0:T(8,128)(2,1)S(1)}, bf16[1,512,7168]{2,1,0:T(8,128)(2,1)}, u32[]{:S(2)}) copy-start(bf16[1,512,7168]{2,1,0:T(8,128)(2,1)} %param.8) | copy-start | bytes 22020100
  3.9 50.7 %slice-start = ((s8[7340032]{0:T(1024)(128)(4,1)}), s8[4194304]{0:T(1024)(128)(4,1)S(1)}, s32[]{:S(2)}) async-start(s8[7340032]{0:T(1024)(128)(4,1)} %bitcast.41), calls=%async_computation.2 | async-start | bytes 8388608
  52.1 2.6 %slice-start.1 = ((s8[7340032]{0:T(1024)(128)(4,1)}), s8[3145728]{0:T(1024)(128)(4,1)S(1)}, s32[]{:S(2)}) async-start(s8[7340032]{0:T(1024)(128)(4,1)} %bitcast.41), calls=%async_computation.3 | async-start | bytes 6291456
  57.0 5.2 %copy-start.2 = (f32[1,16,2]{1,2,0:T(2,128)S(1)}, f32[1,16,2]{1,2,0:T(2,128)}, u32[]{:S(2)}) copy-start(f32[1,16,2]{1,2,0:T(2,128)} %param.11) | copy-start | bytes 388
  57.0 47.8 %all-to-all-start.1 = ((bf16[16,8,7168]{2,1,0:T(8,128)(2,1)}), bf16[16,8,7168]{2,1,0:T(8,128)(2,1)S(1)}, u32[]{:S(2)}, u32[]{:S(2)}) async-start(bf16[16,8,7168]{2,1,0:T(8,128)(2,1)} %fusion), calls=%async_computation.1 | async-start | bytes 3670016 | tf_op jit(solution)/shard_map/all_to_all | solution.py:52
  62.2 43.9 %copy-start.1 = (bf16[1,16,7168]{2,1,0:T(8,128)(2,1)S(1)}, bf16[1,16,7168]{2,1,0:T(8,128)(2,1)}, u32[]{:S(2)}) copy-start(bf16[1,16,7168]{2,1,0:T(8,128)(2,1)} %param.6) | copy-start | bytes 688132
  106.2 2.6 %collective-permute-start = (bf16[16,7168]{1,0:T(8,128)(2,1)S(1)}, bf16[16,7168]{1,0:T(8,128)(2,1)S(1)}, u32[]{:S(2)}, u32[]{:S(2)}) collective-permute-start(bf16[16,7168]{1,0:T(8,128)(2,1)S(1)} %fusion.10), channel_id=1, source_target_pairs={{0,16},{16,0},{1,17},{17,1},{2,18},{18,2},{3,19},{19,3},{4,20},{20... | collective-permute-start | bytes 688136 | tf_op jit(solution)/shard_map/ppermute | solution.py:13

commit v19 on v17

--- a/solution.py
+++ b/solution.py
@@ -24,11 +24,13 @@
     weights = gate_weights[0]
     rows_here, width = tokens.shape
     top = routes.shape[1]
-    stacked = lax.optimization_barrier(jnp.concatenate([tokens, gain[None, :]], axis=0).astype(jnp.float32))
+    stacked, chosen = lax.optimization_barrier((
+        jnp.concatenate([tokens, gain[None, :]], axis=0).astype(jnp.float32),
+        (routes[:, :, None] == jnp.arange(EXPERTS)[None, None, :]).astype(jnp.int32),
+    ))
     wide = stacked[:rows_here]
     square = jnp.mean(wide ** 2, axis=-1, keepdims=True)
     normed = (wide * lax.rsqrt(square + 1e-06) * stacked[rows_here:]).astype(jnp.bfloat16)
-    chosen = lax.optimization_barrier((routes[:, :, None] == jnp.arange(EXPERTS)[None, None, :]).astype(jnp.int32))
     named = jnp.sum(chosen, axis=1)
     positions = jnp.arange(rows_here)
     earlier = (positions[None, :] < positions[:, None]).astype(jnp.int32)

time: 109 us -> 109 us (level)
  no operation moved by 1% of the time
where the time goes in v19:
time: 109 us
  blocking collectives  48.2 us (44%)
  waiting for transfers between devices  43.3 us (40%)
  starting transfers between devices  6.71 us (6%)
  matrix products  6.51 us (6%)
  other arithmetic  2.12 us (2%)
  local copies, waits for them, and re-layouts  2.05 us (2%)
    all_to_all x1, blocking collectives, shards(): lax.all_to_all(outgoing, 'expert', split_axis=1, concat_axis=1, tiled=True)  48.2 us
    all_to_all x1, waiting for transfers between devices, shards(): lax.all_to_all(partial, 'expert', split_axis=0, concat_axis=0, tiled=True)  42.2 us
    all_to_all x1, starting transfers between devices, shards(): lax.all_to_all(partial, 'expert', split_axis=0, concat_axis=0, tiled=True)  5.18 us
    dot_general x1, matrix products, shards(): jnp.einsum('psd,fd->psf', incoming, up_block, preferred_element_type=jnp....  2.54 us
    dot_general x1, matrix products, shards(): jnp.dot(active, down_block, preferred_element_type=jnp.float32)  2.38 us
  transfers between devices with their start and end apart: 2, of which 2 were waited for; matrix products, arithmetic and copies ran while one was open for 0% of the time, Pallas kernels for 0%

profile of v19, /device:TPU:13, one launch (start us, length us, event | category | flops | bytes accessed | tf_op | source)
XLA Modules:
  0.0 109.0 jit_solution(2199640007725550292)
XLA Ops:
  0.0 0.7 fusion.20
  0.7 1.0 maximum_convert_fusion
  1.7 0.2 multiply_reduce_fusion
  1.9 0.1 convolution_add_fusion
  2.0 0.1 multiply_reduce_fusion.1
  2.1 0.1 compare_reduce_fusion
  2.2 0.0 copy-start
  2.2 0.7 convolution_convert_fusion.1
  2.8 1.0 copy.30
  3.9 0.0 slice-start
  3.9 48.2 %all_to_all.10 = bf16[8,16,7168]{2,0,1:T(8,128)(2,1)S(1)} all-to-all(bf16[8,16,7168]{2,0,1:T(8,128)(2,1)S(1)} %copy.30), channel_id=1, replica_groups=mesh['segment'=2,'expert'=16] {'expert'}, dimensions={1} | all-to-all | bytes 3670016 | tf_op jit(solution)/shard_map/all_to_all | solution.py:48
  52.0 0.0 copy-done
  52.0 0.0 slice-start.1
  52.1 2.5 %fusion.14 = bf16[128,512]{1,0:T(8,128)(2,1)S(1)} fusion(bf16[8,16,7168]{2,0,1:T(8,128)(2,1)S(1)} %all_to_all.10, bf16[1,512,7168]{2,1,0:T(8,128)(2,1)S(1)} %copy-done), kind=kOutput, calls=%fused_computation.19 | convolution fusion | flops 939851776 | bytes 9306112 | tf_op jit(solution)/shard_map/psd,fd->psf/dot_general | solution.py:49
  54.6 0.0 slice-done
  54.6 0.0 slice-done.1
  54.6 2.4 %fusion = bf16[16,8,7168]{2,1,0:T(8,128)(2,1)} fusion(bf16[128,512]{1,0:T(8,128)(2,1)S(1)} %fusion.14, bf16[1,512,7168]{2,1,0:T(8,128)(2,1)S(1)} %bitcast.53), kind=kOutput, calls=%fused_computation.2 | convolution fusion | flops 940441600 | bytes 9306112 | tf_op jit(solution)/shard_map/dot_general | solution.py:52
  57.0 0.0 copy-start.2
  57.0 5.2 %all-to-all-start.1 = ((bf16[16,8,7168]{2,1,0:T(8,128)(2,1)}), bf16[16,8,7168]{2,1,0:T(8,128)(2,1)S(1)}, u32[]{:S(2)}, u32[]{:S(2)}) async-start(bf16[16,8,7168]{2,1,0:T(8,128)(2,1)} %fusion), calls=%async_computation.1 | async-start | bytes 3670016 | tf_op jit(solution)/shard_map/all_to_all | solution.py:54
  62.2 0.0 copy-start.1
  62.2 0.0 copy-done.2
  62.2 0.1 fusion.19
  62.3 0.1 reshape.68
  62.4 0.1 copy.32
  62.5 0.1 copy.31
  62.6 42.2 %all-to-all-done.1 = bf16[16,8,7168]{2,1,0:T(8,128)(2,1)S(1)} async-done(((bf16[16,8,7168]{2,1,0:T(8,128)(2,1)}), bf16[16,8,7168]{2,1,0:T(8,128)(2,1)S(1)}, u32[]{:S(2)}, u32[]{:S(2)}) %all-to-all-start.1) | async-done | bytes 1835040 | tf_op jit(solution)/shard_map/all_to_all | solution.py:54
  104.8 0.4 convolution_bitcast_fusion
  105.2 0.0 copy-done.1
  105.2 0.4 fusion.3
  105.7 1.5 %collective-permute-start = (bf16[16,7168]{1,0:T(8,128)(2,1)S(1)}, bf16[16,7168]{1,0:T(8,128)(2,1)S(1)}, u32[]{:S(2)}, u32[]{:S(2)}) collective-permute-start(bf16[16,7168]{1,0:T(8,128)(2,1)S(1)} %fusion.3), channel_id=1, source_target_pairs={{0,16},{16,0},{1,17},{17,1},{2,18},{18,2},{3,19},{19,3},{4,20},{20... | collective-permute-start | bytes 688136 | tf_op jit(solution)/shard_map/ppermute | solution.py:13
  107.2 1.1 %collective-permute-done = bf16[16,7168]{1,0:T(8,128)(2,1)S(1)} collective-permute-done((bf16[16,7168]{1,0:T(8,128)(2,1)S(1)}, bf16[16,7168]{1,0:T(8,128)(2,1)S(1)}, u32[]{:S(2)}, u32[]{:S(2)}) %collective-permute-start) | collective-permute-done | bytes 229408 | tf_op jit(solution)/shard_map/ppermute | solution.py:13
  108.3 0.7 copy.34
  (7 shorter events, 0.1 us)
Async XLA Ops:
  2.2 49.9 %copy-start = (bf16[1,512,7168]{2,1,0:T(8,128)(2,1)S(1)}, bf16[1,512,7168]{2,1,0:T(8,128)(2,1)}, u32[]{:S(2)}) copy-start(bf16[1,512,7168]{2,1,0:T(8,128)(2,1)} %param.8) | copy-start | bytes 22020100
  3.9 50.7 %slice-start = ((s8[7340032]{0:T(1024)(128)(4,1)}), s8[4194304]{0:T(1024)(128)(4,1)S(1)}, s32[]{:S(2)}) async-start(s8[7340032]{0:T(1024)(128)(4,1)} %bitcast.52), calls=%async_computation.2 | async-start | bytes 8388608
  52.0 2.6 %slice-start.1 = ((s8[7340032]{0:T(1024)(128)(4,1)}), s8[3145728]{0:T(1024)(128)(4,1)S(1)}, s32[]{:S(2)}) async-start(s8[7340032]{0:T(1024)(128)(4,1)} %bitcast.52), calls=%async_computation.3 | async-start | bytes 6291456
  57.0 5.2 %copy-start.2 = (f32[1,16,2]{1,2,0:T(2,128)S(1)}, f32[1,16,2]{1,2,0:T(2,128)}, u32[]{:S(2)}) copy-start(f32[1,16,2]{1,2,0:T(2,128)} %param.11) | copy-start | bytes 388
  57.0 47.8 %all-to-all-start.1 = ((bf16[16,8,7168]{2,1,0:T(8,128)(2,1)}), bf16[16,8,7168]{2,1,0:T(8,128)(2,1)S(1)}, u32[]{:S(2)}, u32[]{:S(2)}) async-start(bf16[16,8,7168]{2,1,0:T(8,128)(2,1)} %fusion), calls=%async_computation.1 | async-start | bytes 3670016 | tf_op jit(solution)/shard_map/all_to_all | solution.py:54
  62.2 43.0 %copy-start.1 = (bf16[1,16,7168]{2,1,0:T(8,128)(2,1)S(1)}, bf16[1,16,7168]{2,1,0:T(8,128)(2,1)}, u32[]{:S(2)}) copy-start(bf16[1,16,7168]{2,1,0:T(8,128)(2,1)} %param.6) | copy-start | bytes 688132
  105.7 2.6 %collective-permute-start = (bf16[16,7168]{1,0:T(8,128)(2,1)S(1)}, bf16[16,7168]{1,0:T(8,128)(2,1)S(1)}, u32[]{:S(2)}, u32[]{:S(2)}) collective-permute-start(bf16[16,7168]{1,0:T(8,128)(2,1)S(1)} %fusion.3), channel_id=1, source_target_pairs={{0,16},{16,0},{1,17},{17,1},{2,18},{18,2},{3,19},{19,3},{4,20},{20... | collective-permute-start | bytes 688136 | tf_op jit(solution)/shard_map/ppermute | solution.py:13
